TPU v7x, 128 devices: a whole 4x4x4 slice. The times are simulated.
128 devices in a mesh: dp: 8 (over z, core), ctx: 16 (over y, x).
Axes of the slice: x: 4, y: 4, z: 4, core: 2. Of those that a mesh axis runs over, the one named last changes fastest.
Arguments:
- ids: int32 [8, 4096, 8], P('dp', 'ctx'), may hold values from 0 to 1023
- tables: bfloat16 [8, 1024, 1024], P(None, 'dp', 'ctx'), may hold values from -2.09375 to 2.09375
- w_qkv: bfloat16 [1024, 3072], P('dp'), may hold values from -5 to 5
- w_out: bfloat16 [1024, 1024], P('dp'), may hold values from -0.1875 to 0.1875
- attn_gain: float32 [1024], replicated, may hold values from 0.1 to 1.9
- conv_gain: float32 [1024], replicated, may hold values from 0.1 to 1.9
- conv_kernel: float32 [31, 1024], replicated, may hold values from -1 to 1
- back_list: int32 [16, 2], replicated, may hold values from 0 to 17, as said below
- ahead_list: int32 [16, 1], replicated, may hold values from 1 to 17, as said below
- cotangent: bfloat16 [8, 4096, 1024], P('dp', 'ctx'), may hold values from -8 to 8
Outputs:
- block_out: bfloat16 [8, 4096, 1024], P('dp', 'ctx')
- grad_embedded: bfloat16 [8, 4096, 1024], P('dp', 'ctx')
- grad_qkv: float32 [1024, 3072], P('dp')
- grad_out: float32 [1024, 1024], P('dp')
- grad_kernel: float32 [31, 1024], replicated
Inputs may be any that keep to these rules, and one draw needn't show every extreme that they name: `back_list`: row b lists distinct blocks among b - 2 .. b - 1 that exist, first, then the filler 16 + 1; block 2 and the last block list all 2, the first none. `ahead_list`: row b lists distinct blocks among b + 1 .. b + 1 that exist, first, then the filler 16 + 1; block 0 lists all 1, the last none.
All inputs are finite; a program needn't handle non-finite values.
Results may differ from a plain program's by a relative error of at most 0.015.
Values may be sent and summed in bfloat16 or wider, within the bound.
No kernel may reach another device: no remote copies, remote signals or barrier semaphores. Data moves between devices by JAX's collectives and lax.ppermute only.
A program may use at most 128 MiB of HBM per device.

v0:
```python
import jax
import jax.numpy as jnp
from jax import lax
from jax.sharding import PartitionSpec as P

HEADS = 16


EPSILON = 1e-06
NEGATIVE = -1e30


def from_behind(value, axis, steps):
    count = lax.axis_size(axis)
    first, last = (max(0, -steps), min(count, count - steps))
    return lax.ppermute(value, axis, [(source, source + steps) for source in range(first, last)])


def with_halo(block, sides, width):
    for axis, dim in sides:
        count = lax.axis_size(axis)
        forward = [(i, i + 1) for i in range(count - 1)]
        backward = [(target, source) for source, target in forward]
        low = lax.ppermute(
            lax.slice_in_dim(block, block.shape[dim] - width, None, axis=dim), axis, forward
        )
        high = lax.ppermute(lax.slice_in_dim(block, 0, width, axis=dim), axis, backward)
        block = jnp.concatenate([low, block, high], axis=dim)
    return block


def inverse_rms(features):
    return lax.rsqrt(jnp.mean(features * features, axis=-1, keepdims=True) + EPSILON)


def norm_back(features, inverse, gains, upstream):
    inner = jnp.mean(features * gains * upstream, axis=-1, keepdims=True)
    return inverse * gains * upstream - features * inverse * inverse * inverse * inner


def silu_slope(conv_sum):
    sigmoid = jax.nn.sigmoid(conv_sum)
    return sigmoid * (1.0 + conv_sum * (1.0 - sigmoid))


def block_scores(queries, key_block, listed_block, score_scale):
    return jnp.where(
        listed_block,
        jnp.einsum("rqhd,rkhd->rhqk", queries, key_block, preferred_element_type=jnp.float32)
        * score_scale,
        NEGATIVE,
    )


def probabilities(queries, key_part, listed, score_scale):
    pieces = [
        block_scores(queries, key_part[:, position], listed[position], score_scale)
        for position in range(key_part.shape[1])
    ]
    scores = jnp.concatenate(pieces, axis=3)
    highest = jnp.max(scores, axis=3, keepdims=True)
    weights = jnp.exp(scores - highest)
    return weights / jnp.sum(weights, axis=3, keepdims=True)


def on_device(
    ids, tables, w_qkv, w_out, attn_gain, conv_gain, conv_kernel, back_list, ahead_list, cotangent
):
    recordings = ids.shape[0]
    frames_dev = ids.shape[1]
    head_count = HEADS
    tap_count = conv_kernel.shape[0]
    rim_width = (tap_count - 1) // 2
    group_width = 4
    group_count = head_count // group_width
    ids_whole = lax.all_gather(ids, "ctx", axis=1, tiled=True)
    table_whole = lax.all_gather(tables, "dp", axis=1, tiled=True)
    columns = jnp.zeros(ids_whole.shape[:2] + (table_whole.shape[2],), jnp.float32)
    for codebook in range(table_whole.shape[0]):
        columns = columns + jnp.take(
            table_whole[codebook], ids_whole[:, :, codebook], axis=0
        ).astype(jnp.float32)
    embedded = lax.all_to_all(
        columns.astype(jnp.bfloat16), "ctx", split_axis=1, concat_axis=2, tiled=True
    )
    weight_qkv, weight_out = (
        lax.all_gather(w_qkv, "dp", axis=0, tiled=True),
        lax.all_gather(w_out, "dp", axis=0, tiled=True),
    )
    model_width = weight_out.shape[0]
    head_size = model_width // head_count
    score_scale = head_size ** (-0.5)
    features = embedded.astype(jnp.float32).reshape(-1, model_width)
    attn_inverse = inverse_rms(features)
    normed = (features * attn_inverse * attn_gain).astype(jnp.bfloat16)
    projected = jnp.dot(normed, weight_qkv, preferred_element_type=jnp.float32).astype(jnp.bfloat16)
    projected = projected.reshape(recordings, frames_dev, 3 * model_width)
    own_pairs = projected[:, :, model_width:]
    ctx_index = lax.axis_index("ctx")
    back_row = lax.dynamic_index_in_dim(back_list, ctx_index, 0, keepdims=False)
    ahead_row = lax.dynamic_index_in_dim(ahead_list, ctx_index, 0, keepdims=False)
    offsets = [-(step + 1) for step in range(back_list.shape[1])] + [1]
    listed_items = [jnp.array(True)]
    pair_blocks = [own_pairs]
    for offset in offsets:
        list_row = back_row if offset < 0 else ahead_row
        listed_items.append(jnp.any(list_row == ctx_index + offset))
        pair_blocks.append(from_behind(own_pairs, "ctx", -offset))
    listed = jnp.stack(listed_items)
    seen_count = len(pair_blocks)
    stacked = jnp.stack(pair_blocks, axis=1)
    key_all = stacked[..., :model_width].reshape(
        recordings, seen_count, frames_dev, head_count, head_size
    )
    value_all = stacked[..., model_width:].reshape(
        recordings, seen_count, frames_dev, head_count, head_size
    )
    query_all = projected[:, :, :model_width].reshape(recordings, frames_dev, head_count, head_size)

    def forward_group(group):
        first_head = group * group_width
        queries = lax.dynamic_slice_in_dim(query_all, first_head, group_width, 2)
        key_part = lax.dynamic_slice_in_dim(key_all, first_head, group_width, 3)
        value_part = lax.dynamic_slice_in_dim(value_all, first_head, group_width, 3)
        probs_low = probabilities(queries, key_part, listed, score_scale).astype(jnp.bfloat16)
        value_flat = value_part.reshape(recordings, -1, group_width, head_size)
        return jnp.einsum(
            "rhqk,rkhd->rqhd", probs_low, value_flat, preferred_element_type=jnp.float32
        ).astype(jnp.bfloat16)

    mixed = lax.map(forward_group, jnp.arange(group_count, dtype=jnp.int32))
    mixed = jnp.moveaxis(mixed, 0, 2).reshape(recordings * frames_dev, model_width)
    projection = jnp.dot(mixed, weight_out, preferred_element_type=jnp.float32)
    middle = (features + projection).astype(jnp.bfloat16)
    middle_wide = middle.astype(jnp.float32)
    conv_inverse = inverse_rms(middle_wide)
    conv_input = (
        (middle_wide * conv_inverse * conv_gain)
        .astype(jnp.bfloat16)
        .reshape(recordings, frames_dev, model_width)
    )
    padded = with_halo(conv_input, (("ctx", 1),), rim_width).astype(jnp.float32)

    def conv_step(tap_index, sums):
        taps = lax.dynamic_index_in_dim(conv_kernel, tap_index, 0, keepdims=False)
        return sums + taps * lax.dynamic_slice_in_dim(padded, tap_index, frames_dev, 1)

    conv_sum = lax.fori_loop(
        0, tap_count, conv_step, jnp.zeros((recordings, frames_dev, model_width), jnp.float32)
    )
    middle_frames = middle_wide.reshape(recordings, frames_dev, model_width)
    block_out = (middle_frames + jax.nn.silu(conv_sum)).astype(jnp.bfloat16)
    upstream = cotangent.astype(jnp.float32)
    grad_conv_low = (upstream * silu_slope(conv_sum)).astype(jnp.bfloat16)
    grad_conv = lax.optimization_barrier(grad_conv_low).astype(jnp.float32)
    grad_padded = with_halo(grad_conv_low, (("ctx", 1),), rim_width).astype(jnp.float32)

    def back_step(tap_index, carry):
        grad_input, kernel_rows = carry
        window = lax.dynamic_slice_in_dim(padded, tap_index, frames_dev, 1)
        row = jnp.sum(grad_conv * window, axis=(0, 1))
        kernel_rows = lax.dynamic_update_index_in_dim(kernel_rows, row, tap_index, 0)
        taps = lax.dynamic_index_in_dim(conv_kernel, tap_index, 0, keepdims=False)
        start_row = 2 * rim_width - tap_index
        grad_input = grad_input + taps * lax.dynamic_slice_in_dim(
            grad_padded, start_row, frames_dev, 1
        )
        return (grad_input, kernel_rows)

    grad_input, kernel_rows = lax.fori_loop(
        0,
        tap_count,
        back_step,
        (
            jnp.zeros((recordings, frames_dev, model_width), jnp.float32),
            jnp.zeros((tap_count, model_width), jnp.float32),
        ),
    )
    grad_kernel = lax.psum(kernel_rows, ("dp", "ctx"))
    grad_middle = (
        upstream.reshape(-1, model_width)
        + norm_back(middle_wide, conv_inverse, conv_gain, grad_input.reshape(-1, model_width))
    ).astype(jnp.bfloat16)
    contract_rows = (((0,), (0,)), ((), ()))
    contract_columns = (((1,), (1,)), ((), ()))
    grad_mixed = lax.dot_general(
        grad_middle, weight_out, contract_columns, preferred_element_type=jnp.float32
    ).astype(jnp.bfloat16)
    grad_wout = lax.dot_general(
        mixed, grad_middle, contract_rows, preferred_element_type=jnp.float32
    )
    grad_heads = grad_mixed.reshape(recordings, frames_dev, head_count, head_size)

    def backward_group(group):
        first_head = group * group_width
        queries = lax.dynamic_slice_in_dim(query_all, first_head, group_width, 2)
        key_part = lax.dynamic_slice_in_dim(key_all, first_head, group_width, 3)
        value_part = lax.dynamic_slice_in_dim(value_all, first_head, group_width, 3)
        grad_part = lax.dynamic_slice_in_dim(grad_heads, first_head, group_width, 2)
        probs = probabilities(queries, key_part, listed, score_scale)
        probs_low = probs.astype(jnp.bfloat16)
        key_flat = key_part.reshape(recordings, -1, group_width, head_size)
        value_flat = value_part.reshape(recordings, -1, group_width, head_size)
        grad_probs = jnp.einsum(
            "rqhd,rkhd->rhqk", grad_part, value_flat, preferred_element_type=jnp.float32
        )
        row_sum = jnp.sum(probs * grad_probs, axis=3, keepdims=True)
        grad_scores = (probs * (grad_probs - row_sum) * score_scale).astype(jnp.bfloat16)
        grad_query = jnp.einsum(
            "rhqk,rkhd->rqhd", grad_scores, key_flat, preferred_element_type=jnp.float32
        )
        grad_key = jnp.einsum(
            "rhqk,rqhd->rkhd", grad_scores, queries, preferred_element_type=jnp.float32
        )
        grad_value = jnp.einsum(
            "rhqk,rqhd->rkhd", probs_low, grad_part, preferred_element_type=jnp.float32
        )
        return (grad_query, grad_key, grad_value)

    grad_query, grad_key, grad_value = lax.map(
        backward_group, jnp.arange(group_count, dtype=jnp.int32)
    )
    grad_query = jnp.moveaxis(grad_query, 0, 2).reshape(recordings * frames_dev, model_width)
    grad_key = jnp.moveaxis(grad_key, 0, 2).reshape(recordings, seen_count, frames_dev, model_width)
    grad_value = jnp.moveaxis(grad_value, 0, 2).reshape(
        recordings, seen_count, frames_dev, model_width
    )
    pair_total = jnp.concatenate([grad_key[:, 0], grad_value[:, 0]], axis=2)
    for position, offset in enumerate(offsets):
        outgoing = jnp.concatenate(
            [grad_key[:, position + 1], grad_value[:, position + 1]], axis=2
        ).astype(jnp.bfloat16)
        arrived = from_behind(outgoing, "ctx", offset)
        pair_total = pair_total + arrived.astype(jnp.float32)
    grad_projected = jnp.concatenate(
        [
            grad_query.astype(jnp.bfloat16),
            pair_total.reshape(recordings * frames_dev, 2 * model_width).astype(jnp.bfloat16),
        ],
        axis=1,
    )
    grad_wqkv = lax.dot_general(
        normed, grad_projected, contract_rows, preferred_element_type=jnp.float32
    )
    grad_normed = lax.dot_general(
        grad_projected, weight_qkv, contract_columns, preferred_element_type=jnp.float32
    )
    grad_embedded = (
        grad_middle.astype(jnp.float32) + norm_back(features, attn_inverse, attn_gain, grad_normed)
    ).astype(jnp.bfloat16)
    share_qkv, share_out = (
        lax.psum_scatter(grad_wqkv, ("dp", "ctx"), scatter_dimension=0, tiled=True),
        lax.psum_scatter(grad_wout, ("dp", "ctx"), scatter_dimension=0, tiled=True),
    )
    grad_qkv, grad_out = (
        lax.all_gather(share_qkv.astype(jnp.bfloat16), "ctx", axis=0, tiled=True).astype(
            share_qkv.dtype
        ),
        lax.all_gather(share_out.astype(jnp.bfloat16), "ctx", axis=0, tiled=True).astype(
            share_out.dtype
        ),
    )
    return (
        block_out,
        grad_embedded.reshape(recordings, frames_dev, model_width),
        grad_qkv,
        grad_out,
        grad_kernel,
    )


def solution(mesh):
    in_specs = (
        P("dp", "ctx", None),
        P(None, "dp", "ctx"),
        P("dp", None),
        P("dp", None),
        P(),
        P(),
        P(),
        P(),
        P(),
        P("dp", "ctx", None),
    )
    out_specs = (P("dp", "ctx", None), P("dp", "ctx", None), P("dp", None), P("dp", None), P())
    return jax.shard_map(
        on_device, mesh=mesh, in_specs=in_specs, out_specs=out_specs, check_vma=False
    )
```

profile of v0, /device:TPU:0, one launch (start us, length us, event | category | flops | bytes accessed | tf_op | source)
XLA Modules:
  0.0 1616.6 jit_solution(10427319216327694318)
XLA Ops:
  9.8 24.0 %all_gather.19 = s32[1,4096,8]{1,2,0:T(8,128)S(1)} all-gather(s32[1,256,8]{1,2,0:T(8,128)} %param.20), channel_id=1, replica_groups=mesh['dp'=8,'ctx'=16] {'ctx'}, dimensions={1}, use_global_device_ids=true | all-gather | bytes 139264 | tf_op jit(solution)/shard_map/all_gather | solution.py:76
  34.5 3.7 all-gather.4.cloned.1.call-done
  39.8 12.1 gather_fusion.2
  52.0 14.9 gather_fusion.3
  66.9 14.9 gather_fusion.4
  81.8 14.9 gather_fusion.5
  96.7 14.9 gather_fusion.6
  111.6 15.0 gather_fusion.7
  126.6 14.9 gather_fusion
  141.5 14.9 gather_fusion.1
  156.4 8.9 add_convert_fusion
  165.3 16.7 %copy.311 = bf16[1,4096,64]{2,0,1:T(2,128)(2,1)S(1)} copy(bf16[1,4096,64]{2,1,0:T(8,128)(2,1)S(1)} %add_convert_fusion) | data formatting | bytes 1048576 | tf_op jit(solution)/shard_map/convert_element_type | solution.py:84
  182.6 22.4 %reduce.51 = bf16[4096,64]{1,0:T(8,128)(2,1)S(1)} reduce(bf16[4096,1,64]{2,1,0:T(2,128)(2,1)S(1)} %bitcast.411, bf16[]{:T(256)} %broadcast.243), dimensions={1}, to_apply=%bitcast.323.reduce_sub_computation | reduce | bytes 1048578
  205.8 18.8 %all_to_all.4 = bf16[16,2,8192]{2,1,0:T(2,128)(2,1)S(1)} all-to-all(bf16[16,2,8192]{2,1,0:T(2,128)(2,1)S(1)} %reshape.824), channel_id=1, replica_groups=mesh['dp'=8,'ctx'=16] {'ctx'}, dimensions={0} | all-to-all | bytes 1048576 | tf_op jit(solution)/shard_map/all_to_all | solution.py:83
  230.4 4.6 fusion.102
  236.2 3.5 collective-permute-start
  239.6 3.3 collective-permute-start.1
  248.4 13.8 collective-permute-done
  262.2 20.3 %collective-permute-done.1 = bf16[1,256,2048]{2,1,0:T(8,128)(2,1)} collective-permute-done((bf16[1,256,2048]{2,1,0:T(8,128)(2,1)S(1)}, bf16[1,256,2048]{2,1,0:T(8,128)(2,1)}, u32[]{:S(2)}, u32[]{:S(2)}) %collective-permute-start.1) | collective-permute-done | bytes 1048608 | tf_op jit(solution)/shard_map/ppermute | solution.py:16
  282.5 4.9 collective-permute-done.2
  295.0 3.1 copy.276
  298.0 3.9 copy.275
  302.0 65.9 %while.56 = (s32[]{:T(128)}, bf16[4,1,256,4,64]{2,4,3,1,0:T(8,128)(2,1)}, s32[4]{0:T(128)S(1)}, bf16[1,4,256,16,64]{2,1,4,3,0:T(4,128)(2,1)}, bf16[1,256,16,64]{...) while((s32[]{:T(128)}, ...), condition=%wide.region_10.12_spmd, body=%wide.region_4.11_spmd.sunk | while | flops 282916864 | bytes 20639508 | solution.py:131
  371.0 3.2 collective-permute-start.3
  375.8 4.2 collective-permute-done.4
  380.2 40.1 %while.58 = (s32[]{:T(128)}, f32[1,256,1024]{2,1,0:T(8,128)S(1)}, f32[31,1024]{1,0:T(8,128)}, f32[1,286,1024]{2,1,0:T(8,128)S(1)}, s32[]{:T(128)}, /*index=5*/s32[]{:T(128)}) while((s32[]{:T(128)}, f32[1,256,1024]{2,1,0:T(8,128)S(1)}, f32[31,1024]{1,0:T(8,128)}, f32[1,286,1024]{2,1,0:T(8,128)S(1)}, s32[]{:T(128)}, ...), condition=%wide.region_13.15_spmd.clone, body=%wide.region_12.14_spmd.clone.sunk | while | flops 786435 | bytes 3158103 | solution.py:148
  421.8 3.5 collective-permute-start.5
  427.8 3.3 collective-permute-done.6
  433.3 130.4 %while.59 = (s32[]{:T(128)}, f32[1,256,1024]{2,1,0:T(8,128)S(1)}, f32[31,1024]{1,0:T(8,128)}, f32[31,1024]{1,0:T(8,128)}, f32[1,286,1024]{2,1,0:T(8,128)}, /*ind...) while((s32[]{:T(128)}, f32[1,256,1024]{2,1,0:T(8,128)S(1)}, ...), condition=%wide.region_16.18_spmd.clone, body=%wide.region_14.17_spmd.clone.sunk | while | flops 1309703 | bytes 5267637 | solution.py:170
  571.3 8.7 reduce-scatter.3.cloned.1.call-start
  580.0 157.8 %while.57 = (s32[]{:T(128)}, bf16[4,1,256,4,64]{2,4,3,1,0:T(8,128)(2,1)}, f32[4,1,1024,4,64]{2,4,3,1,0:T(8,128)}, f32[4,1,1024,4,64]{2,4,3,1,0:T(8,128)}, s32[4]...) while((s32[]{:T(128)}, ...), condition=%wide.region_25.27_spmd, body=%wide.region_18.26_spmd.sunk | while | flops 716965888 | bytes 64713528 | solution.py:220
  588.4 3.9 fusion.200
  596.6 3.9 fusion.192
  600.5 7.3 fusion.199
  612.4 7.0 fusion.198
  627.8 3.9 fusion.200
  636.1 3.9 fusion.192
  639.9 7.4 fusion.199
  651.8 7.0 fusion.198
  667.3 3.9 fusion.200
  675.5 3.9 fusion.192
  679.4 7.3 fusion.199
  691.3 7.0 fusion.198
  706.7 3.9 fusion.200
  714.9 3.9 fusion.192
  718.8 7.3 fusion.199
  730.7 7.0 fusion.198
  737.7 5.6 reshape.707
  743.3 5.6 reshape.708
  748.9 2.9 convert.25
  767.2 8.1 pad_maximum_fusion.1
  783.1 7.3 pad_maximum_fusion.2
  790.4 5.5 collective-permute-start.9
  795.9 4.9 slice_bitcast_fusion
  802.2 28.8 %collective-permute-done.8 = bf16[1,256,2048]{1,0,2:T(2,128)(2,1)S(1)} collective-permute-done((bf16[1,256,2048]{1,0,2:T(2,128)(2,1)}, bf16[1,256,2048]{1,0,2:T(2,128)(2,1)S(1)}, u32[]{:S(2)}, u32[]{:S(2)}) %collective-permute-start.8) | collective-permute-done | bytes 1048608 | tf_op jit(solution)/shard_map/ppermute | solution.py:16
  831.1 8.6 collective-permute-done.9
  839.7 19.2 %fusion.105 = bf16[1,256,2048]{1,0,2:T(2,128)(2,1)S(1)} fusion(bf16[1,256,2048]{1,0,2:T(2,128)(2,1)S(1)} %collective-permute-done.9, bf16[1,256,2048]{1,0,2:T(2,128)(2,1)S(1)} %collective-permute-done.8, f32[1,256,2048]{1,2,0:T(8,128)S(1)} %convert_element_type.227, f32[1,256,1024]{1,0,2:T(1,128)S(1)} %get-tuple-element.771, ...), kind=kLoop, calls=%fused_computation.122 | loop fusion | flops 3670016 | bytes 7340032 | tf_op jit(solution)/shard_map/convert_element_type | solution.py:238
  859.1 6.6 fusion.121
  866.7 4.8 multiply_reduce_fusion.2
  872.8 367.2 %reduce-scatter.5.cloned.1.call-done = f32[8,1024]{1,0:T(8,128)} async-done(((f32[1024,1024]{1,0:T(8,128)}), f32[8,1024]{1,0:T(8,128)}) %reduce-scatter.5.cloned.1.call-update) | async-done | bytes 32784 | tf_op jit(solution)/shard_map/reduce_scatter | solution.py:253
  1240.7 20.7 %all_gather.23 = bf16[128,1024]{1,0:T(8,128)(2,1)S(1)} all-gather(bf16[8,1024]{1,0:T(8,128)(2,1)S(1)} %convert_element_type.235), channel_id=1, replica_groups=mesh['dp'=8,'ctx'=16] {'ctx'}, dimensions={0}, use_global_device_ids=true | all-gather | bytes 278528 | tf_op jit(solution)/shard_map/all_gather | solution.py:259
  1262.3 201.9 %reduce-scatter.3.cloned.1.call-done = f32[8,3072]{1,0:T(8,128)} async-done(((f32[1024,3072]{1,0:T(8,128)}), f32[8,3072]{1,0:T(8,128)}) %reduce-scatter.3.cloned.1.call-update) | async-done | bytes 98320 | tf_op jit(solution)/shard_map/reduce_scatter | solution.py:252
  1465.1 22.2 %all_gather.22 = bf16[128,3072]{1,0:T(8,128)(2,1)S(1)} all-gather(bf16[8,3072]{1,0:T(8,128)(2,1)S(1)} %convert_element_type.233), channel_id=1, replica_groups=mesh['dp'=8,'ctx'=16] {'ctx'}, dimensions={0}, use_global_device_ids=true | all-gather | bytes 835584 | tf_op jit(solution)/shard_map/all_gather | solution.py:256
  1488.6 119.2 %all-reduce.2.cloned.1.call-done = f32[31,1024]{1,0:T(8,128)} async-done(((f32[31,1024]{1,0:T(8,128)}), f32[31,1024]{1,0:T(8,128)}) %all-reduce.2.cloned.1.call-update) | async-done | bytes 126992 | tf_op jit(solution)/shard_map/psum | solution.py:179
  (398 shorter events, 375.4 us)
Async XLA Ops:
  7.2 237.2 %copy-start = (s32[16,1]{0,1:T(1,128)S(1)}, s32[16,1]{0,1:T(1,128)}, u32[]{:S(2)}) copy-start(s32[16,1]{0,1:T(1,128)} %param.28) | copy-start | bytes 196
  7.2 31.0 %all-gather.4.cloned.1.call-start = ((), (), s32[]{:S(2)}) async-start(), calls=%async_computation.3 | async-start | bytes 2359296 | tf_op jit(solution)/shard_map/all_gather | solution.py:77
  9.0 220.7 %all-gather.6.cloned.1.call-start = ((), (), s32[]{:S(2)}) async-start(), calls=%async_computation.4 | async-start | bytes 7077888 | tf_op jit(solution)/shard_map/all_gather | solution.py:87
  9.8 358.2 %all-gather.8.cloned.1.call-start = ((), (), s32[]{:S(2)}) async-start(), calls=%async_computation.5 | async-start | bytes 2359296 | tf_op jit(solution)/shard_map/all_gather | solution.py:88
  141.5 14.9 copy-start.10
  228.1 2.3 copy-start.17
  229.5 5.6 copy-start.4
  229.7 0.7 copy-start.20
  229.7 15.9 copy-start.22
  235.0 1.1 copy-start.14
  236.2 26.1 %collective-permute-start = (bf16[1,256,2048]{2,1,0:T(8,128)(2,1)S(1)}, bf16[1,256,2048]{2,1,0:T(8,128)(2,1)}, u32[]{:S(2)}, u32[]{:S(2)}) collective-permute-start(bf16[1,256,2048]{2,1,0:T(8,128)(2,1)S(1)} %get-tuple-element.746), channel_id=1, source_target_pairs={{0,1},{1,2},{2,3},{3,4},{4,5},{5,6},{6,7},{7,8},{8,9},{9,10},{10,1... | collective-permute-start | bytes 3145736 | tf_op jit(solution)/shard_map/ppermute | solution.py:16
  239.6 42.9 %collective-permute-start.1 = (bf16[1,256,2048]{2,1,0:T(8,128)(2,1)S(1)}, bf16[1,256,2048]{2,1,0:T(8,128)(2,1)}, u32[]{:S(2)}, u32[]{:S(2)}) collective-permute-start(bf16[1,256,2048]{2,1,0:T(8,128)(2,1)S(1)} %get-tuple-element.746), channel_id=1, source_target_pairs={{0,2},{1,3},{2,4},{3,5},{4,6},{5,7},{6,8},{7,9},{8,10},{9,11},{10,... | collective-permute-start | bytes 3145736 | tf_op jit(solution)/shard_map/ppermute | solution.py:16
  242.9 44.5 %collective-permute-start.2 = (bf16[1,256,2048]{2,1,0:T(8,128)(2,1)S(1)}, bf16[1,256,2048]{2,1,0:T(8,128)(2,1)}, u32[]{:S(2)}, u32[]{:S(2)}) collective-permute-start(bf16[1,256,2048]{2,1,0:T(8,128)(2,1)S(1)} %get-tuple-element.746), channel_id=1, source_target_pairs={{1,0},{2,1},{3,2},{4,3},{5,4},{6,5},{7,6},{8,7},{9,8},{10,9},{11,1... | collective-permute-start | bytes 3145736 | tf_op jit(solution)/shard_map/ppermute | solution.py:16
  244.3 995.7 %reduce-scatter.5.cloned.1.call-start = ((), (), s32[]{:S(2)}) async-start(), calls=%async_computation.7 | async-start | bytes 4227072 | tf_op jit(solution)/shard_map/reduce_scatter | solution.py:253
  309.8 1.0 copy-start.3
  326.3 1.0 copy-start.3
  342.7 1.0 copy-start.3
  359.2 1.0 copy-start.3
  367.9 2.9 copy-start.19
  370.7 49.6 %copy-start.6 = (bf16[256,1024]{1,0:T(8,128)(2,1)}, bf16[256,1024]{1,0:T(8,128)(2,1)S(1)}, u32[]{:S(2)}) copy-start(bf16[256,1024]{1,0:T(8,128)(2,1)S(1)} %get-tuple-element.768) | copy-start | bytes 1572868
  371.0 4.8 collective-permute-start.3
  374.2 5.8 collective-permute-start.4
  380.2 40.2 %copy-start.13 = (bf16[1,256,1024]{2,1,0:T(8,128)(2,1)S(1)}, bf16[1,256,1024]{2,1,0:T(8,128)(2,1)}, u32[]{:S(2)}) copy-start(bf16[1,256,1024]{2,1,0:T(8,128)(2,1)} %param.29) | copy-start | bytes 1572868
  421.8 3.5 copy-start.7
  421.8 6.0 collective-permute-start.5
  425.3 5.8 collective-permute-start.6
  563.7 3.0 copy-start.11
  566.7 2.8 copy-start.8
  566.7 2.8 copy-start.12
  571.3 892.9 %reduce-scatter.3.cloned.1.call-start = ((), (), s32[]{:S(2)}) async-start(), calls=%async_computation.6 | async-start | bytes 12681216 | tf_op jit(solution)/shard_map/reduce_scatter | solution.py:252
  587.8 4.6 copy-start.2
  627.2 4.6 copy-start.2
  666.7 4.6 copy-start.2
  706.1 4.6 copy-start.2
  763.2 37.7 %collective-permute-start.7 = (bf16[1,256,2048]{1,2,0:T(8,128)(2,1)}, bf16[1,256,2048]{1,2,0:T(8,128)(2,1)}, u32[]{:S(2)}, u32[]{:S(2)}) collective-permute-start(bf16[1,256,2048]{1,2,0:T(8,128)(2,1)} %pad_maximum_fusion.4), channel_id=1, source_target_pairs={{1,0},{2,1},{3,2},{4,3},{5,4},{6,5},{7,6},{8,7},{9,8},{10,9},{11,1... | collective-permute-start | bytes 3145736 | tf_op jit(solution)/shard_map/ppermute | solution.py:16
  775.3 55.8 %collective-permute-start.8 = (bf16[1,256,2048]{1,0,2:T(2,128)(2,1)}, bf16[1,256,2048]{1,0,2:T(2,128)(2,1)S(1)}, u32[]{:S(2)}, u32[]{:S(2)}) collective-permute-start(bf16[1,256,2048]{1,0,2:T(2,128)(2,1)} %pad_maximum_fusion.1), channel_id=1, source_target_pairs={{2,0},{3,1},{4,2},{5,3},{6,4},{7,5},{8,6},{9,7},{10,8},{11,9},{12,... | collective-permute-start | bytes 3145736 | tf_op jit(solution)/shard_map/ppermute | solution.py:16
  790.4 49.2 %collective-permute-start.9 = (bf16[1,256,2048]{1,0,2:T(2,128)(2,1)S(1)}, bf16[1,256,2048]{1,0,2:T(2,128)(2,1)S(1)}, u32[]{:S(2)}, u32[]{:S(2)}) collective-permute-start(bf16[1,256,2048]{1,0,2:T(2,128)(2,1)S(1)} %pad_maximum_fusion.2), channel_id=1, source_target_pairs={{0,1},{1,2},{2,3},{3,4},{4,5},{5,6},{6,7},{7,8},{8,9},{9,10},{10,1... | collective-permute-start | bytes 3145736 | tf_op jit(solution)/shard_map/ppermute | solution.py:16
  839.7 19.4 %copy-start.5 = (f32[256,1024]{1,0:T(8,128)S(1)}, f32[256,1024]{1,0:T(8,128)}, u32[]{:S(2)}) copy-start(f32[256,1024]{1,0:T(8,128)} %copy-done.4) | copy-start | bytes 3145732
  839.7 19.4 %copy-start.15 = (bf16[4,1,256,4,64]{2,4,3,1,0:T(8,128)(2,1)S(1)}, bf16[4,1,256,4,64]{2,4,3,1,0:T(8,128)(2,1)}, u32[]{:S(2)}) copy-start(bf16[4,1,256,4,64]{2,4,3,1,0:T(8,128)(2,1)} %get-tuple-element.376) | copy-start | bytes 1572868
  839.7 19.4 %copy-start.18 = (f32[1024]{0:T(1024)S(1)}, f32[1024]{0:T(1024)}, u32[]{:S(2)}) copy-start(f32[1024]{0:T(1024)} %param.24) | copy-start | bytes 12292
  839.7 19.4 %copy-start.21 = (f32[256]{0:T(256)S(1)}, f32[256]{0:T(256)}, u32[]{:S(2)}) copy-start(f32[256]{0:T(256)} %copy-done.20) | copy-start | bytes 3076
  865.7 1.0 copy-start.16
  865.7 742.1 %all-reduce.2.cloned.1.call-start = ((), (), s32[]{:S(2)}) async-start(), calls=%async_computation.8 | async-start | bytes 262144 | tf_op jit(solution)/shard_map/psum | solution.py:179
  866.7 4.9 copy-start.9
  866.7 742.6 %copy-start.1 = (s32[16,1]{0,1:T(1,128)S(1)}, s32[16,1]{0,1:T(1,128)}, u32[]{:S(2)}) copy-start(s32[16,1]{0,1:T(1,128)} %param.28) | copy-start | bytes 196
Sparse Core Ops, SparseCore 0:
  10.3 27.8 all-gather.3
  39.9 41.4 all-gather.5
  244.4 25.3 all-gather.7
  571.4 668.5 reduce-scatter.4
  1245.6 218.5 reduce-scatter.2
  1470.0 137.6 all-reduce.1
where the time goes:
time: 1640 us; the launch traced here: 1620 us
  waiting for transfers between devices  777 us (47%)
  local copies, waits for them, and re-layouts  350 us (21%)
  matrix products  175 us (11%)
  other arithmetic  172 us (10%)
  blocking collectives  85.7 us (5%)
  starting transfers between devices  34.2 us (2%)
    reduce_scatter x1, waiting for transfers between devices, on_device(): lax.psum_scatter(grad_wout, ('dp', 'ctx'), scatter_dimension=0, tiled=True)  367 us
    reduce_scatter x1, waiting for transfers between devices, on_device(): lax.psum_scatter(grad_wqkv, ('dp', 'ctx'), scatter_dimension=0, tiled=True)  202 us
    psum x1, waiting for transfers between devices, on_device(): grad_kernel = lax.psum(kernel_rows, ('dp', 'ctx'))  119 us
    gather x8, local copies, waits for them, and re-layouts, on_device(): jnp.take(table_whole[codebook], ids_whole[:, :, codebook], axis=0)  117 us
    ppermute x6, waiting for transfers between devices, from_behind(): lax.ppermute(value, axis, [(source, source + steps) for source in range(f...  76.4 us
    add x31, other arithmetic, back_step(): grad_input + taps * lax.dynamic_slice_in_dim(grad_padded, start_row, fram...  63.2 us
    dot_general x32, matrix products, block_scores(): jnp.einsum('rqhd,rkhd->rhqk', queries, key_block, preferred_element_type=...  52.3 us
    dynamic_update_slice x31, local copies, waits for them, and re-layouts, back_step(): lax.dynamic_update_index_in_dim(kernel_rows, row, tap_index, 0)  43.4 us
  transfers between devices with their start and end apart: 16, of which 12 were waited for; matrix products, arithmetic and copies ran while one was open for 31% of the time, Pallas kernels for 0%

commit v1 on v0

--- a/solution.py
+++ b/solution.py
@@ -141,13 +141,9 @@
     )
     padded = with_halo(conv_input, (("ctx", 1),), rim_width).astype(jnp.float32)
 
-    def conv_step(tap_index, sums):
-        taps = lax.dynamic_index_in_dim(conv_kernel, tap_index, 0, keepdims=False)
-        return sums + taps * lax.dynamic_slice_in_dim(padded, tap_index, frames_dev, 1)
-
-    conv_sum = lax.fori_loop(
-        0, tap_count, conv_step, jnp.zeros((recordings, frames_dev, model_width), jnp.float32)
-    )
+    conv_sum = jnp.zeros((recordings, frames_dev, model_width), jnp.float32)
+    for tap_index in range(tap_count):
+        conv_sum = conv_sum + conv_kernel[tap_index] * padded[:, tap_index : tap_index + frames_dev]
     middle_frames = middle_wide.reshape(recordings, frames_dev, model_width)
     block_out = (middle_frames + jax.nn.silu(conv_sum)).astype(jnp.bfloat16)
     upstream = cotangent.astype(jnp.float32)
@@ -155,28 +151,17 @@
     grad_conv = lax.optimization_barrier(grad_conv_low).astype(jnp.float32)
     grad_padded = with_halo(grad_conv_low, (("ctx", 1),), rim_width).astype(jnp.float32)
 
-    def back_step(tap_index, carry):
-        grad_input, kernel_rows = carry
-        window = lax.dynamic_slice_in_dim(padded, tap_index, frames_dev, 1)
-        row = jnp.sum(grad_conv * window, axis=(0, 1))
-        kernel_rows = lax.dynamic_update_index_in_dim(kernel_rows, row, tap_index, 0)
-        taps = lax.dynamic_index_in_dim(conv_kernel, tap_index, 0, keepdims=False)
+    grad_input = jnp.zeros((recordings, frames_dev, model_width), jnp.float32)
+    kernel_list = []
+    for tap_index in range(tap_count):
+        window = padded[:, tap_index : tap_index + frames_dev]
+        kernel_list.append(jnp.sum(grad_conv * window, axis=(0, 1)))
         start_row = 2 * rim_width - tap_index
-        grad_input = grad_input + taps * lax.dynamic_slice_in_dim(
-            grad_padded, start_row, frames_dev, 1
-        )
-        return (grad_input, kernel_rows)
-
-    grad_input, kernel_rows = lax.fori_loop(
-        0,
-        tap_count,
-        back_step,
-        (
-            jnp.zeros((recordings, frames_dev, model_width), jnp.float32),
-            jnp.zeros((tap_count, model_width), jnp.float32),
-        ),
-    )
-    grad_kernel = lax.psum(kernel_rows, ("dp", "ctx"))
+        grad_input = grad_input + conv_kernel[tap_index] * grad_padded[
+            :, start_row : start_row + frames_dev
+        ]
+    kernel_rows = jnp.stack(kernel_list)
+    kernel_dp = lax.psum(kernel_rows, "dp")
     grad_middle = (
         upstream.reshape(-1, model_width)
         + norm_back(middle_wide, conv_inverse, conv_gain, grad_input.reshape(-1, model_width))
@@ -186,8 +171,10 @@
     grad_mixed = lax.dot_general(
         grad_middle, weight_out, contract_columns, preferred_element_type=jnp.float32
     ).astype(jnp.bfloat16)
+    mixed_columns = lax.all_to_all(mixed, "dp", split_axis=1, concat_axis=0, tiled=True)
+    middle_rows = lax.all_gather(grad_middle, "dp", axis=0, tiled=True)
     grad_wout = lax.dot_general(
-        mixed, grad_middle, contract_rows, preferred_element_type=jnp.float32
+        mixed_columns, middle_rows, contract_rows, preferred_element_type=jnp.float32
     )
     grad_heads = grad_mixed.reshape(recordings, frames_dev, head_count, head_size)
 
@@ -239,8 +226,10 @@
         ],
         axis=1,
     )
+    normed_columns = lax.all_to_all(normed, "dp", split_axis=1, concat_axis=0, tiled=True)
+    projected_rows = lax.all_gather(grad_projected, "dp", axis=0, tiled=True)
     grad_wqkv = lax.dot_general(
-        normed, grad_projected, contract_rows, preferred_element_type=jnp.float32
+        normed_columns, projected_rows, contract_rows, preferred_element_type=jnp.float32
     )
     grad_normed = lax.dot_general(
         grad_projected, weight_qkv, contract_columns, preferred_element_type=jnp.float32
@@ -248,18 +237,17 @@
     grad_embedded = (
         grad_middle.astype(jnp.float32) + norm_back(features, attn_inverse, attn_gain, grad_normed)
     ).astype(jnp.bfloat16)
-    share_qkv, share_out = (
-        lax.psum_scatter(grad_wqkv, ("dp", "ctx"), scatter_dimension=0, tiled=True),
-        lax.psum_scatter(grad_wout, ("dp", "ctx"), scatter_dimension=0, tiled=True),
-    )
-    grad_qkv, grad_out = (
-        lax.all_gather(share_qkv.astype(jnp.bfloat16), "ctx", axis=0, tiled=True).astype(
-            share_qkv.dtype
-        ),
-        lax.all_gather(share_out.astype(jnp.bfloat16), "ctx", axis=0, tiled=True).astype(
-            share_out.dtype
-        ),
-    )
+    row_width = grad_wqkv.shape[1] + grad_wout.shape[1]
+    kernel_padded = jnp.pad(kernel_dp, ((0, (-tap_count * model_width) % row_width // model_width), (0, 0)))
+    kernel_packed = kernel_padded.reshape(-1, row_width)
+    packed = jnp.concatenate(
+        [jnp.concatenate([grad_wqkv, grad_wout], axis=1), kernel_packed], axis=0
+    )
+    summed = lax.psum(packed, "ctx")
+    shard_rows = grad_wqkv.shape[0]
+    grad_qkv = summed[:shard_rows, : grad_wqkv.shape[1]]
+    grad_out = summed[:shard_rows, grad_wqkv.shape[1] :]
+    grad_kernel = summed[shard_rows:].reshape(-1, model_width)[:tap_count]
     return (
         block_out,
         grad_embedded.reshape(recordings, frames_dev, model_width),

time: 1640 us -> 906 us (0.55)
  waiting for transfers between devices: 777 us -> 262 us
  local copies, waits for them, and re-layouts: 350 us -> 252 us
  other arithmetic: 172 us -> 101 us
  blocking collectives: 85.7 us -> 56.3 us
    reduce_scatter x2 -> x0, waiting for transfers between devices: 569 us -> none  [the longest x1 367 us: on_device(): lax.psum_scatter(grad_wout, ('dp', 'ctx'), scatter_dimension=0, tiled=True)]
    all_gather x0 -> x2, waiting for transfers between devices: none -> 83.6 us  [the longest x1 83.5 us: on_device(): projected_rows = lax.all_gather(grad_projected, 'dp', axis=0, tiled=True)]
    add x62 -> x0, other arithmetic: 78.9 us -> none  [the longest x31 63.2 us: back_step(): grad_input + taps * lax.dynamic_slice_in_dim(grad_padded, start_row, fram...]
    dynamic_slice x62 -> x0, local copies, waits for them, and re-layouts: 47.5 us -> none  [the longest x31 23.9 us: conv_step(): taps = lax.dynamic_index_in_dim(conv_kernel, tap_index, 0, keepdims=False)]
    dynamic_update_slice x31 -> x0, local copies, waits for them, and re-layouts: 43.4 us -> none  [back_step(): lax.dynamic_update_index_in_dim(kernel_rows, row, tap_index, 0)]
    all_gather x2 -> x0, blocking collectives: 42.9 us -> none  [the longest x1 22.2 us: on_device(): lax.all_gather(share_qkv.astype(jnp.bfloat16), 'ctx', axis=0, tiled=True)]
    psum x1 -> x2, waiting for transfers between devices: 119 us -> 88.8 us  [the longest x1 88.8 us: on_device(): summed = lax.psum(packed, 'ctx')]
  transfers between devices with their start and end apart: 16 -> 18, of which waited for: 12 -> 9; matrix products, arithmetic and copies ran while one was open for 31% -> 54% of each run, Pallas kernels for 0% -> 0%
where the time goes in v1:
time: 906 us; the launch traced here: 895 us
  waiting for transfers between devices  262 us (29%)
  local copies, waits for them, and re-layouts  252 us (28%)
  matrix products  170 us (19%)
  other arithmetic  101 us (11%)
  blocking collectives  56.3 us (6%)
  starting transfers between devices  31.5 us (3%)
  between operations  16.1 us (2%)
    gather x8, local copies, waits for them, and re-layouts, on_device(): jnp.take(table_whole[codebook], ids_whole[:, :, codebook], axis=0)  117 us
    psum x1, waiting for transfers between devices, on_device(): summed = lax.psum(packed, 'ctx')  88.8 us
    all_gather x1, waiting for transfers between devices, on_device(): projected_rows = lax.all_gather(grad_projected, 'dp', axis=0, tiled=True)  83.5 us
    ppermute x6, waiting for transfers between devices, from_behind(): lax.ppermute(value, axis, [(source, source + steps) for source in range(f...  72.6 us
    dot_general x32, matrix products, block_scores(): jnp.einsum('rqhd,rkhd->rhqk', queries, key_block, preferred_element_type=...  52.1 us
    dot_general x4, matrix products, backward_group(): jnp.einsum('rhqk,rqhd->rkhd', grad_scores, queries, preferred_element_typ...  29.9 us
    dot_general x4, matrix products, backward_group(): jnp.einsum('rhqk,rkhd->rqhd', grad_scores, key_flat, preferred_element_ty...  28 us
    all_gather x1, blocking collectives, on_device(): ids_whole = lax.all_gather(ids, 'ctx', axis=1, tiled=True)  24 us
  transfers between devices with their start and end apart: 18, of which 9 were waited for; matrix products, arithmetic and copies ran while one was open for 54% of the time, Pallas kernels for 0%

profile of v1, /device:TPU:0, one launch (start us, length us, event | category | flops | bytes accessed | tf_op | source)
XLA Modules:
  0.0 895.1 jit_solution(8023950666195141221)
XLA Ops:
  9.8 24.0 %all_gather.19 = s32[1,4096,8]{1,2,0:T(8,128)S(1)} all-gather(s32[1,256,8]{1,2,0:T(8,128)} %param.16), channel_id=1, replica_groups=mesh['dp'=8,'ctx'=16] {'ctx'}, dimensions={1}, use_global_device_ids=true | all-gather | bytes 139264 | tf_op jit(solution)/shard_map/all_gather | solution.py:76
  34.5 3.7 all-gather.6.cloned.1.call-done
  39.8 12.1 %gather_fusion = bf16[4096,64]{1,0:T(8,128)(2,1)S(1)} fusion(bf16[1024,64]{1,0:T(8,128)(2,1)S(1)} %get-tuple-element.450, s32[4096]{0:T(1024)S(1)} %broadcast_clamp_fusion.7), kind=kCustom, calls=%fused_computation.clone | custom fusion | bytes 1064960 | tf_op jit(solution)/shard_map/jit(_take)/gather | solution.py:80
  52.0 15.0 %gather_fusion.7 = bf16[4096,64]{1,0:T(8,128)(2,1)} fusion(bf16[1024,64]{1,0:T(8,128)(2,1)S(1)} %get-tuple-element.451, s32[4096]{0:T(1024)S(1)} %broadcast_clamp_fusion), kind=kCustom, calls=%fused_computation.7.clone | custom fusion | bytes 1064960 | tf_op jit(solution)/shard_map/jit(_take)/gather | solution.py:80
  67.0 14.9 %gather_fusion.6 = bf16[4096,64]{1,0:T(8,128)(2,1)} fusion(bf16[1024,64]{1,0:T(8,128)(2,1)S(1)} %get-tuple-element.452, s32[4096]{0:T(1024)S(1)} %broadcast_clamp_fusion.1), kind=kCustom, calls=%fused_computation.6.clone | custom fusion | bytes 1064960 | tf_op jit(solution)/shard_map/jit(_take)/gather | solution.py:80
  81.9 14.9 %gather_fusion.5 = bf16[4096,64]{1,0:T(8,128)(2,1)} fusion(bf16[1024,64]{1,0:T(8,128)(2,1)S(1)} %get-tuple-element.453, s32[4096]{0:T(1024)S(1)} %broadcast_clamp_fusion.2), kind=kCustom, calls=%fused_computation.5.clone | custom fusion | bytes 1064960 | tf_op jit(solution)/shard_map/jit(_take)/gather | solution.py:80
  96.8 14.9 %gather_fusion.4 = bf16[4096,64]{1,0:T(8,128)(2,1)} fusion(bf16[1024,64]{1,0:T(8,128)(2,1)S(1)} %get-tuple-element.454, s32[4096]{0:T(1024)S(1)} %broadcast_clamp_fusion.3), kind=kCustom, calls=%fused_computation.4.clone | custom fusion | bytes 1064960 | tf_op jit(solution)/shard_map/jit(_take)/gather | solution.py:80
  111.7 14.9 %gather_fusion.3 = bf16[4096,64]{1,0:T(8,128)(2,1)} fusion(bf16[1024,64]{1,0:T(8,128)(2,1)S(1)} %get-tuple-element.455, s32[4096]{0:T(1024)S(1)} %broadcast_clamp_fusion.4), kind=kCustom, calls=%fused_computation.3.clone | custom fusion | bytes 1064960 | tf_op jit(solution)/shard_map/jit(_take)/gather | solution.py:80
  126.6 14.9 %gather_fusion.2 = bf16[4096,64]{1,0:T(8,128)(2,1)} fusion(bf16[1024,64]{1,0:T(8,128)(2,1)S(1)} %get-tuple-element.456, s32[4096]{0:T(1024)S(1)} %broadcast_clamp_fusion.5), kind=kCustom, calls=%fused_computation.2.clone | custom fusion | bytes 1064960 | tf_op jit(solution)/shard_map/jit(_take)/gather | solution.py:80
  141.5 14.9 %gather_fusion.1 = bf16[4096,64]{1,0:T(8,128)(2,1)} fusion(bf16[1024,64]{1,0:T(8,128)(2,1)S(1)} %get-tuple-element.457, s32[4096]{0:T(1024)S(1)} %broadcast_clamp_fusion.6), kind=kCustom, calls=%fused_computation.1.clone | custom fusion | bytes 1064960 | tf_op jit(solution)/shard_map/jit(_take)/gather | solution.py:80
  156.4 8.9 add_convert_fusion
  165.3 16.7 %copy.339 = bf16[1,4096,64]{2,0,1:T(2,128)(2,1)S(1)} copy(bf16[1,4096,64]{2,1,0:T(8,128)(2,1)S(1)} %add_convert_fusion) | data formatting | bytes 1048576 | tf_op jit(solution)/shard_map/convert_element_type | solution.py:84
  182.6 22.4 %reduce.51 = bf16[4096,64]{1,0:T(8,128)(2,1)S(1)} reduce(bf16[4096,1,64]{2,1,0:T(2,128)(2,1)S(1)} %bitcast.477, bf16[]{:T(256)} %broadcast.264), dimensions={1}, to_apply=%bitcast.392.reduce_sub_computation | reduce | bytes 1048578
  205.8 18.8 %all_to_all.44 = bf16[16,2,8192]{2,1,0:T(2,128)(2,1)S(1)} all-to-all(bf16[16,2,8192]{2,1,0:T(2,128)(2,1)S(1)} %reshape.933), channel_id=1, replica_groups=mesh['dp'=8,'ctx'=16] {'ctx'}, dimensions={0} | all-to-all | bytes 1048576 | tf_op jit(solution)/shard_map/all_to_all | solution.py:83
  230.3 4.6 fusion.102
  236.4 3.7 collective-permute-start.1
  240.1 3.5 collective-permute-start
  249.1 13.9 %collective-permute-done.1 = bf16[1,256,2048]{2,1,0:T(8,128)(2,1)} collective-permute-done((bf16[1,256,2048]{2,1,0:T(8,128)(2,1)}, bf16[1,256,2048]{2,1,0:T(8,128)(2,1)}, u32[]{:S(2)}, u32[]{:S(2)}) %collective-permute-start.1) | collective-permute-done | bytes 1048608 | tf_op jit(solution)/shard_map/ppermute | solution.py:16
  263.0 21.3 %collective-permute-done = bf16[1,256,2048]{2,1,0:T(8,128)(2,1)} collective-permute-done((bf16[1,256,2048]{2,1,0:T(8,128)(2,1)}, bf16[1,256,2048]{2,1,0:T(8,128)(2,1)}, u32[]{:S(2)}, u32[]{:S(2)}) %collective-permute-start) | collective-permute-done | bytes 1048608 | tf_op jit(solution)/shard_map/ppermute | solution.py:16
  288.9 4.0 copy.299
  292.8 3.9 copy.297
  296.7 4.8 copy.300
  301.5 46.4 %while.24 = (s32[]{:T(128)}, bf16[4,1,256,4,64]{2,4,3,1,0:T(8,128)(2,1)}, s32[4]{0:T(128)S(1)}, bf16[1,4,256,16,64]{2,1,4,3,0:T(4,128)(2,1)}, bf16[1,256,16,64]{...) while((s32[]{:T(128)}, ...), condition=%wide.region_10.12_spmd, body=%wide.region_4.11_spmd.sunk | while | flops 282916864 | bytes 16444675 | solution.py:131
  350.7 4.4 collective-permute-start.3
  357.0 4.0 collective-permute-done.4
  361.1 5.3 fusion.115
  369.0 3.3 collective-permute-start.5
  378.3 5.6 fusion.120
  388.2 143.2 %while.25 = (s32[]{:T(128)}, bf16[4,1,256,4,64]{2,4,3,1,0:T(8,128)(2,1)}, f32[4,1,1024,4,64]{2,4,3,1,0:T(8,128)}, f32[4,1,1024,4,64]{2,4,3,1,0:T(8,128)}, s32[4]...) while((s32[]{:T(128)}, ...), condition=%wide.region_20.22_spmd, body=%wide.region_13.21_spmd.sunk | while | flops 716965888 | bytes 66809192 | solution.py:207
  402.7 3.6 fusion.259
  406.4 7.0 fusion.265
  413.4 7.3 fusion.266
  420.7 3.1 fusion.267
  438.3 3.6 fusion.259
  442.0 7.0 fusion.265
  449.0 8.0 fusion.266
  457.0 3.2 fusion.267
  474.7 3.6 fusion.259
  478.3 7.0 fusion.265
  485.4 7.3 fusion.266
  492.7 3.2 fusion.267
  510.3 3.6 fusion.259
  514.0 7.0 fusion.265
  521.0 7.3 fusion.266
  528.3 3.1 fusion.267
  531.4 5.6 reshape.813
  542.1 5.8 reshape.812
  550.8 3.8 fusion.198
  554.6 3.6 copy.307
  564.9 3.6 copy.311
  568.5 3.6 copy.312
  574.6 7.6 pad_maximum_fusion.2
  583.5 7.3 pad_maximum_fusion.3
  590.8 5.5 collective-permute-start.9
  596.3 4.9 slice_bitcast_fusion
  601.4 35.3 %collective-permute-done.8 = bf16[1,256,2048]{1,0,2:T(2,128)(2,1)S(1)} collective-permute-done((bf16[1,256,2048]{1,0,2:T(2,128)(2,1)S(1)}, bf16[1,256,2048]{1,0,2:T(2,128)(2,1)S(1)}, u32[]{:S(2)}, u32[]{:S(2)}) %collective-permute-start.8) | collective-permute-done | bytes 1048608 | tf_op jit(solution)/shard_map/ppermute | solution.py:16
  638.7 19.2 %fusion.105 = bf16[1,256,2048]{1,0,2:T(2,128)(2,1)S(1)} fusion(bf16[1,256,2048]{1,0,2:T(2,128)(2,1)S(1)} %collective-permute-done.9, bf16[1,256,2048]{1,0,2:T(2,128)(2,1)S(1)} %collective-permute-done.8, f32[1,256,2048]{1,2,0:T(8,128)S(1)} %convert_element_type.227, f32[1,256,1024]{1,0,2:T(1,128)S(1)} %get-tuple-element.513, ...), kind=kLoop, calls=%fused_computation.149 | loop fusion | flops 3670016 | bytes 7340032 | tf_op jit(solution)/shard_map/convert_element_type | solution.py:225
  659.7 13.5 %all_to_all.45 = bf16[256,8,128]{0,2,1:T(8,128)(2,1)S(1)} all-to-all(bf16[256,8,128]{0,2,1:T(8,128)(2,1)S(1)} %multiply_convert_fusion.1), channel_id=1, replica_groups=mesh['dp'=8,'ctx'=16] {'dp'}, dimensions={1} | all-to-all | bytes 1048576 | tf_op jit(solution)/shard_map/all_to_all | solution.py:229
  673.2 3.5 all-to-all-start.2
  678.3 8.6 all-to-all-done.2
  690.2 83.5 %all-gather.12.cloned.1.call-done = bf16[2048,3072]{0,1:T(8,128)(2,1)} async-done(((bf16[256,3072]{0,1:T(8,128)(2,1)}), bf16[2048,3072]{0,1:T(8,128)(2,1)}) %all-gather.12.cloned.1.call-update) | async-done | bytes 12582928 | tf_op jit(solution)/shard_map/all_gather | solution.py:230
  773.7 8.9 fusion.203
  786.7 4.8 multiply_reduce_fusion.1
  792.8 88.8 %all-reduce.6.cloned.1.call-done = f32[136,4096]{1,0:T(8,128)} async-done(((f32[136,4096]{1,0:T(8,128)}), f32[136,4096]{1,0:T(8,128)}) %all-reduce.6.cloned.1.call-update) | async-done | bytes 2228240 | tf_op jit(solution)/shard_map/psum | solution.py:246
  (255 shorter events, 177.3 us)
Async XLA Ops:
  7.2 237.8 %copy-start = (s32[16,1]{0,1:T(1,128)S(1)}, s32[16,1]{0,1:T(1,128)}, u32[]{:S(2)}) copy-start(s32[16,1]{0,1:T(1,128)} %param.24) | copy-start | bytes 196
  7.2 31.0 %all-gather.6.cloned.1.call-start = ((), (), s32[]{:S(2)}) async-start(), calls=%async_computation.3 | async-start | bytes 2359296 | tf_op jit(solution)/shard_map/all_gather | solution.py:77
  9.0 220.7 %all-gather.8.cloned.1.call-start = ((), (), s32[]{:S(2)}) async-start(), calls=%async_computation.4 | async-start | bytes 7077888 | tf_op jit(solution)/shard_map/all_gather | solution.py:87
  9.8 338.1 %all-gather.10.cloned.1.call-start = ((), (), s32[]{:S(2)}) async-start(), calls=%async_computation.5 | async-start | bytes 2359296 | tf_op jit(solution)/shard_map/all_gather | solution.py:88
  141.5 14.9 %copy-start.12 = (bf16[4096,64]{1,0:T(8,128)(2,1)S(1)}, bf16[4096,64]{1,0:T(8,128)(2,1)}, u32[]{:S(2)}) copy-start(bf16[4096,64]{1,0:T(8,128)(2,1)} %gather_fusion.7) | copy-start | bytes 1572868
  228.1 2.2 copy-start.19
  229.2 5.7 copy-start.8
  229.6 118.3 %copy-start.6 = (f32[256,1024]{1,0:T(8,128)}, f32[256,1024]{1,0:T(8,128)S(1)}, u32[]{:S(2)}) copy-start(f32[256,1024]{1,0:T(8,128)S(1)} %copy.302) | copy-start | bytes 3145732
  229.6 0.6 copy-start.21
  229.6 16.6 %copy-start.23 = (s32[16,2]{0,1:T(2,128)S(1)}, s32[16,2]{0,1:T(2,128)}, u32[]{:S(2)}) copy-start(s32[16,2]{0,1:T(2,128)} %param.23) | copy-start | bytes 388
  229.7 17.3 %copy-start.17 = (f32[31,1024]{1,0:T(8,128)S(1)}, f32[31,1024]{1,0:T(8,128)}, u32[]{:S(2)}) copy-start(f32[31,1024]{1,0:T(8,128)} %param.22) | copy-start | bytes 380932
  234.9 1.5 copy-start.14
  236.4 26.6 %collective-permute-start.1 = (bf16[1,256,2048]{2,1,0:T(8,128)(2,1)}, bf16[1,256,2048]{2,1,0:T(8,128)(2,1)}, u32[]{:S(2)}, u32[]{:S(2)}) collective-permute-start(bf16[1,256,2048]{2,1,0:T(8,128)(2,1)} %get-tuple-element.459), channel_id=1, source_target_pairs={{0,2},{1,3},{2,4},{3,5},{4,6},{5,7},{6,8},{7,9},{8,10},{9,11},{10,... | collective-permute-start | bytes 3145736 | tf_op jit(solution)/shard_map/ppermute | solution.py:16
  240.1 44.2 %collective-permute-start = (bf16[1,256,2048]{2,1,0:T(8,128)(2,1)}, bf16[1,256,2048]{2,1,0:T(8,128)(2,1)}, u32[]{:S(2)}, u32[]{:S(2)}) collective-permute-start(bf16[1,256,2048]{2,1,0:T(8,128)(2,1)} %get-tuple-element.459), channel_id=1, source_target_pairs={{0,1},{1,2},{2,3},{3,4},{4,5},{5,6},{6,7},{7,8},{8,9},{9,10},{10,1... | collective-permute-start | bytes 3145736 | tf_op jit(solution)/shard_map/ppermute | solution.py:16
  243.6 40.7 %collective-permute-start.2 = (bf16[1,256,2048]{2,1,0:T(8,128)(2,1)}, bf16[1,256,2048]{2,1,0:T(8,128)(2,1)}, u32[]{:S(2)}, u32[]{:S(2)}) collective-permute-start(bf16[1,256,2048]{2,1,0:T(8,128)(2,1)} %get-tuple-element.459), channel_id=1, source_target_pairs={{1,0},{2,1},{3,2},{4,3},{5,4},{6,5},{7,6},{8,7},{9,8},{10,9},{11,1... | collective-permute-start | bytes 3145736 | tf_op jit(solution)/shard_map/ppermute | solution.py:16
  244.9 432.4 %all-reduce.4.cloned.1.call-start = ((), (), s32[]{:S(2)}) async-start(), calls=%async_computation.8 | async-start | bytes 262144 | tf_op jit(solution)/shard_map/psum | solution.py:164
  347.9 2.7 copy-start.18
  347.9 13.3 %copy-start.13 = (bf16[1,256,1024]{2,1,0:T(8,128)(2,1)S(1)}, bf16[1,256,1024]{2,1,0:T(8,128)(2,1)}, u32[]{:S(2)}) copy-start(bf16[1,256,1024]{2,1,0:T(8,128)(2,1)} %param.25) | copy-start | bytes 1572868
  350.5 33.4 %copy-start.4 = (bf16[256,1024]{1,0:T(8,128)(2,1)}, bf16[256,1024]{1,0:T(8,128)(2,1)S(1)}, u32[]{:S(2)}) copy-start(bf16[256,1024]{1,0:T(8,128)(2,1)S(1)} %get-tuple-element.510) | copy-start | bytes 1572868
  350.7 6.2 collective-permute-start.3
  355.2 5.8 collective-permute-start.4
  369.0 9.1 %collective-permute-start.5 = (bf16[1,15,1024]{2,1,0:T(8,128)(2,1)S(1)}, bf16[1,15,1024]{2,1,0:T(8,128)(2,1)S(1)}, u32[]{:S(2)}, u32[]{:S(2)}) collective-permute-start(bf16[1,15,1024]{2,1,0:T(8,128)(2,1)S(1)} %get-tuple-element.460), channel_id=1, source_target_pairs={{0,1},{1,2},{2,3},{3,4},{4,5},{5,6},{6,7},{7,8},{8,9},{9,10},{10,1... | collective-permute-start | bytes 92168 | tf_op jit(solution)/shard_map/ppermute | solution.py:24
  372.3 5.8 collective-permute-start.6
  378.1 309.2 %all-gather.14.cloned.1.call-start = ((), (), s32[]{:S(2)}) async-start(), calls=%async_computation.7 | async-start | bytes 4718592 | tf_op jit(solution)/shard_map/all_gather | solution.py:175
  384.4 3.6 copy-start.10
  388.0 385.8 %all-gather.12.cloned.1.call-start = ((), (), s32[]{:S(2)}) async-start(), calls=%async_computation.6 | async-start | bytes 14155776 | tf_op jit(solution)/shard_map/all_gather | solution.py:230
  396.4 6.3 copy-start.3
  401.1 1.0 copy-start.2
  432.1 6.3 copy-start.3
  436.8 1.0 copy-start.2
  468.4 6.3 copy-start.3
  473.1 1.0 copy-start.2
  504.1 6.3 copy-start.3
  508.8 1.0 copy-start.2
  573.3 27.9 %collective-permute-start.7 = (bf16[1,256,2048]{1,2,0:T(8,128)(2,1)S(1)}, bf16[1,256,2048]{1,2,0:T(8,128)(2,1)S(1)}, u32[]{:S(2)}, u32[]{:S(2)}) collective-permute-start(bf16[1,256,2048]{1,2,0:T(8,128)(2,1)S(1)} %pad_maximum_fusion.5), channel_id=1, source_target_pairs={{1,0},{2,1},{3,2},{4,3},{5,4},{6,5},{7,6},{8,7},{9,8},{10,9},{11,1... | collective-permute-start | bytes 3145736 | tf_op jit(solution)/shard_map/ppermute | solution.py:16
  582.2 54.6 %collective-permute-start.8 = (bf16[1,256,2048]{1,0,2:T(2,128)(2,1)S(1)}, bf16[1,256,2048]{1,0,2:T(2,128)(2,1)S(1)}, u32[]{:S(2)}, u32[]{:S(2)}) collective-permute-start(bf16[1,256,2048]{1,0,2:T(2,128)(2,1)S(1)} %pad_maximum_fusion.2), channel_id=1, source_target_pairs={{2,0},{3,1},{4,2},{5,3},{6,4},{7,5},{8,6},{9,7},{10,8},{11,9},{12,... | collective-permute-start | bytes 3145736 | tf_op jit(solution)/shard_map/ppermute | solution.py:16
  590.8 48.0 %collective-permute-start.9 = (bf16[1,256,2048]{1,0,2:T(2,128)(2,1)S(1)}, bf16[1,256,2048]{1,0,2:T(2,128)(2,1)S(1)}, u32[]{:S(2)}, u32[]{:S(2)}) collective-permute-start(bf16[1,256,2048]{1,0,2:T(2,128)(2,1)S(1)} %pad_maximum_fusion.3), channel_id=1, source_target_pairs={{0,1},{1,2},{2,3},{3,4},{4,5},{5,6},{6,7},{7,8},{8,9},{9,10},{10,1... | collective-permute-start | bytes 3145736 | tf_op jit(solution)/shard_map/ppermute | solution.py:16
  638.7 19.4 %copy-start.15 = (bf16[4,1,256,4,64]{2,4,3,1,0:T(8,128)(2,1)S(1)}, bf16[4,1,256,4,64]{2,4,3,1,0:T(8,128)(2,1)}, u32[]{:S(2)}) copy-start(bf16[4,1,256,4,64]{2,4,3,1,0:T(8,128)(2,1)} %get-tuple-element.118) | copy-start | bytes 1572868
  657.9 1.5 copy-start.9
  657.9 1.5 copy-start.20
  657.9 1.5 copy-start.22
  673.2 13.8 %all-to-all-start.2 = ((bf16[256,8,128]{0,2,1:T(8,128)(2,1)}), bf16[256,8,128]{0,2,1:T(8,128)(2,1)S(1)}, u32[]{:S(2)}, u32[]{:S(2)}) async-start(bf16[256,8,128]{0,2,1:T(8,128)(2,1)} %bitcast.135), calls=%async_computation.2 | async-start | bytes 1048576 | tf_op jit(solution)/shard_map/all_to_all | solution.py:174
  676.7 204.9 %all-reduce.6.cloned.1.call-start = ((), (), s32[]{:S(2)}) async-start(), calls=%async_computation.9 | async-start | bytes 4456448 | tf_op jit(solution)/shard_map/psum | solution.py:246
  782.7 1.6 copy-start.5
  782.7 4.0 copy-start.7
  784.2 2.5 copy-start.16
  786.7 4.8 copy-start.11
  786.7 101.1 %copy-start.1 = (s32[16,1]{0,1:T(1,128)S(1)}, s32[16,1]{0,1:T(1,128)}, u32[]{:S(2)}) copy-start(s32[16,1]{0,1:T(1,128)} %param.24) | copy-start | bytes 196
Sparse Core Ops, SparseCore 0:
  10.3 27.8 all-gather.5
  39.9 41.4 all-gather.7
  245.0 24.2 all-gather.9
  378.2 62.8 all-reduce.3
  442.7 31.2 all-gather.13
  659.6 114.1 all-gather.11
  784.4 97.1 all-reduce.5

commit v2 on v1

--- a/solution.py
+++ b/solution.py
@@ -75,11 +75,15 @@
     group_count = head_count // group_width
     ids_whole = lax.all_gather(ids, "ctx", axis=1, tiled=True)
     table_whole = lax.all_gather(tables, "dp", axis=1, tiled=True)
-    columns = jnp.zeros(ids_whole.shape[:2] + (table_whole.shape[2],), jnp.float32)
+    vocab = table_whole.shape[1]
+    entries = lax.broadcasted_iota(jnp.int32, (1, vocab), 1)
+    columns = jnp.zeros((ids_whole.shape[1], table_whole.shape[2]), jnp.float32)
     for codebook in range(table_whole.shape[0]):
-        columns = columns + jnp.take(
-            table_whole[codebook], ids_whole[:, :, codebook], axis=0
-        ).astype(jnp.float32)
+        picks = (ids_whole[0, :, codebook][:, None] == entries).astype(jnp.bfloat16)
+        columns = columns + jnp.dot(
+            picks, table_whole[codebook], preferred_element_type=jnp.float32
+        )
+    columns = columns[None]
     embedded = lax.all_to_all(
         columns.astype(jnp.bfloat16), "ctx", split_axis=1, concat_axis=2, tiled=True
     )
@@ -171,7 +175,11 @@
     grad_mixed = lax.dot_general(
         grad_middle, weight_out, contract_columns, preferred_element_type=jnp.float32
     ).astype(jnp.bfloat16)
-    mixed_columns = lax.all_to_all(mixed, "dp", split_axis=1, concat_axis=0, tiled=True)
+    dp_index = lax.axis_index("dp")
+    shard_width = model_width // lax.axis_size("dp")
+    mixed_columns = lax.dynamic_slice_in_dim(
+        lax.all_gather(mixed, "dp", axis=0, tiled=True), dp_index * shard_width, shard_width, 1
+    )
     middle_rows = lax.all_gather(grad_middle, "dp", axis=0, tiled=True)
     grad_wout = lax.dot_general(
         mixed_columns, middle_rows, contract_rows, preferred_element_type=jnp.float32
@@ -226,10 +234,18 @@
         ],
         axis=1,
     )
-    normed_columns = lax.all_to_all(normed, "dp", split_axis=1, concat_axis=0, tiled=True)
-    projected_rows = lax.all_gather(grad_projected, "dp", axis=0, tiled=True)
-    grad_wqkv = lax.dot_general(
-        normed_columns, projected_rows, contract_rows, preferred_element_type=jnp.float32
+    normed_columns = lax.dynamic_slice_in_dim(
+        lax.all_gather(normed, "dp", axis=0, tiled=True), dp_index * shard_width, shard_width, 1
+    )
+    query_rows = lax.all_gather(grad_projected[:, :model_width], "dp", axis=0, tiled=True)
+    grad_wq = lax.dot_general(
+        normed_columns, query_rows, contract_rows, preferred_element_type=jnp.float32
+    )
+    early = lax.psum(jnp.concatenate([grad_wq, grad_wout], axis=1), "ctx")
+    early, pair_part = lax.optimization_barrier((early, grad_projected[:, model_width:]))
+    pair_rows = lax.all_gather(pair_part, "dp", axis=0, tiled=True)
+    grad_wkv = lax.dot_general(
+        normed_columns, pair_rows, contract_rows, preferred_element_type=jnp.float32
     )
     grad_normed = lax.dot_general(
         grad_projected, weight_qkv, contract_columns, preferred_element_type=jnp.float32
@@ -237,17 +253,19 @@
     grad_embedded = (
         grad_middle.astype(jnp.float32) + norm_back(features, attn_inverse, attn_gain, grad_normed)
     ).astype(jnp.bfloat16)
-    row_width = grad_wqkv.shape[1] + grad_wout.shape[1]
-    kernel_padded = jnp.pad(kernel_dp, ((0, (-tap_count * model_width) % row_width // model_width), (0, 0)))
-    kernel_packed = kernel_padded.reshape(-1, row_width)
-    packed = jnp.concatenate(
-        [jnp.concatenate([grad_wqkv, grad_wout], axis=1), kernel_packed], axis=0
-    )
-    summed = lax.psum(packed, "ctx")
-    shard_rows = grad_wqkv.shape[0]
-    grad_qkv = summed[:shard_rows, : grad_wqkv.shape[1]]
-    grad_out = summed[:shard_rows, grad_wqkv.shape[1] :]
-    grad_kernel = summed[shard_rows:].reshape(-1, model_width)[:tap_count]
+    row_width = grad_wkv.shape[1]
+    kernel_padded = jnp.pad(
+        kernel_dp, ((0, (-tap_count * model_width) % row_width // model_width), (0, 0))
+    )
+    late = lax.psum(
+        jnp.concatenate([grad_wkv, kernel_padded.reshape(-1, row_width)], axis=0), "ctx"
+    )
+    shard_rows = grad_wkv.shape[0]
+    grad_qkv = jnp.concatenate(
+        [early[:, :model_width], late[:shard_rows]], axis=1
+    )
+    grad_out = early[:, model_width:]
+    grad_kernel = late[shard_rows:].reshape(-1, model_width)[:tap_count]
     return (
         block_out,
         grad_embedded.reshape(recordings, frames_dev, model_width),

time: 906 us -> 851 us (0.939)
  local copies, waits for them, and re-layouts: 252 us -> 109 us
  waiting for transfers between devices: 262 us -> 329 us
  matrix products: 170 us -> 208 us
  blocking collectives: 56.3 us -> 42.6 us
    gather x8 -> x0, local copies, waits for them, and re-layouts: 117 us -> none  [on_device(): jnp.take(table_whole[codebook], ids_whole[:, :, codebook], axis=0)]
    psum x1, waiting for transfers between devices: 0.02 us -> 60.1 us  [on_device(): kernel_dp = lax.psum(kernel_rows, 'dp')]
    dot_general x1 -> x10, matrix products: 8.93 us -> 41.6 us  [the longest x8 31.2 us: on_device(): jnp.dot(picks, table_whole[codebook], preferred_element_type=jnp.float32)]
    all_gather x1 -> x4, waiting for transfers between devices: 83.5 us -> 53.7 us  [the longest x1 53.7 us: on_device(): pair_rows = lax.all_gather(pair_part, 'dp', axis=0, tiled=True)]
    psum x1 -> x2, waiting for transfers between devices: 88.8 us -> 112 us  [the longest x1 80.7 us: on_device(): lax.psum(jnp.concatenate([grad_wkv, kernel_padded.reshape(-1, row_width)]...]
    ppermute x6, waiting for transfers between devices: 72.6 us -> 95.4 us  [from_behind(): lax.ppermute(value, axis, [(source, source + steps) for source in range(f...]
    convert_element_type x1, local copies, waits for them, and re-layouts: 16.7 us -> 2.78 us  [on_device(): columns.astype(jnp.bfloat16)]
    all_to_all x1 -> x0, blocking collectives: 13.5 us -> none  [on_device(): lax.all_to_all(normed, 'dp', split_axis=1, concat_axis=0, tiled=True)]
  transfers between devices with their start and end apart: 18 -> 21, of which waited for: 9 -> 12; matrix products, arithmetic and copies ran while one was open for 54% -> 47% of each run, Pallas kernels for 0% -> 0%
where the time goes in v2:
time: 851 us; the launch traced here: 840 us
  waiting for transfers between devices  329 us (39%)
  matrix products  208 us (24%)
  local copies, waits for them, and re-layouts  109 us (13%)
  other arithmetic  98.3 us (12%)
  blocking collectives  42.6 us (5%)
  starting transfers between devices  31.1 us (4%)
  between operations  15.9 us (2%)
    ppermute x6, waiting for transfers between devices, from_behind(): lax.ppermute(value, axis, [(source, source + steps) for source in range(f...  95.4 us
    psum x1, waiting for transfers between devices, on_device(): lax.psum(jnp.concatenate([grad_wkv, kernel_padded.reshape(-1, row_width)]...  80.7 us
    psum x1, waiting for transfers between devices, on_device(): kernel_dp = lax.psum(kernel_rows, 'dp')  60.1 us
    dot_general x32, matrix products, block_scores(): jnp.einsum('rqhd,rkhd->rhqk', queries, key_block, preferred_element_type=...  54.6 us
    all_gather x1, waiting for transfers between devices, on_device(): pair_rows = lax.all_gather(pair_part, 'dp', axis=0, tiled=True)  53.7 us
    dot_general x4, matrix products, backward_group(): jnp.einsum('rhqk,rqhd->rkhd', grad_scores, queries, preferred_element_typ...  32.1 us
    psum x1, waiting for transfers between devices, on_device(): early = lax.psum(jnp.concatenate([grad_wq, grad_wout], axis=1), 'ctx')  31.5 us
    dot_general x8, matrix products, on_device(): jnp.dot(picks, table_whole[codebook], preferred_element_type=jnp.float32)  31.2 us
  transfers between devices with their start and end apart: 21, of which 12 were waited for; matrix products, arithmetic and copies ran while one was open for 47% of the time, Pallas kernels for 0%

profile of v2, /device:TPU:0, one launch (start us, length us, event | category | flops | bytes accessed | tf_op | source)
XLA Modules:
  0.0 839.8 jit_solution(4028925955012139706)
XLA Ops:
  8.7 24.0 %all_gather.27 = s32[1,4096,8]{1,2,0:T(8,128)S(1)} all-gather(s32[1,256,8]{1,2,0:T(8,128)} %param.14), channel_id=1, replica_groups=mesh['dp'=8,'ctx'=16] {'ctx'}, dimensions={1}, use_global_device_ids=true | all-gather | bytes 139264 | tf_op jit(solution)/shard_map/all_gather | solution.py:76
  32.8 2.9 all-gather.9.cloned.1.call-done
  35.8 4.7 fusion.102
  40.5 3.7 fusion.124
  44.2 3.7 fusion.123
  47.9 3.7 fusion.122
  51.6 3.7 fusion.121
  55.4 3.7 fusion.120
  59.1 3.7 fusion.119
  62.8 4.2 fusion.126
  67.1 2.8 copy.259
  70.4 22.4 %reduce.35 = bf16[4096,64]{1,0:T(8,128)(2,1)S(1)} reduce(bf16[4096,1,64]{2,1,0:T(2,128)(2,1)S(1)} %bitcast.401, bf16[]{:T(256)} %broadcast.183), dimensions={1}, to_apply=%bitcast.270.reduce_sub_computation | reduce | bytes 1048578
  93.5 18.5 %all_to_all.4 = bf16[16,2,8192]{2,1,0:T(2,128)(2,1)S(1)} all-to-all(bf16[16,2,8192]{2,1,0:T(2,128)(2,1)S(1)} %reshape.766), channel_id=1, replica_groups=mesh['dp'=8,'ctx'=16] {'ctx'}, dimensions={0} | all-to-all | bytes 1048576 | tf_op jit(solution)/shard_map/all_to_all | solution.py:87
  119.6 4.6 fusion.127
  127.9 6.2 collective-permute-start.1
  140.8 14.1 %collective-permute-done.2 = bf16[1,256,2048]{2,1,0:T(8,128)(2,1)} collective-permute-done((bf16[1,256,2048]{2,1,0:T(8,128)(2,1)}, bf16[1,256,2048]{2,1,0:T(8,128)(2,1)}, u32[]{:S(2)}, u32[]{:S(2)}) %collective-permute-start.2) | collective-permute-done | bytes 1048608 | tf_op jit(solution)/shard_map/ppermute | solution.py:16
  157.0 20.0 %collective-permute-done = bf16[1,256,2048]{2,1,0:T(8,128)(2,1)} collective-permute-done((bf16[1,256,2048]{2,1,0:T(8,128)(2,1)}, bf16[1,256,2048]{2,1,0:T(8,128)(2,1)}, u32[]{:S(2)}, u32[]{:S(2)}) %collective-permute-start) | collective-permute-done | bytes 1048608 | tf_op jit(solution)/shard_map/ppermute | solution.py:16
  181.8 2.8 copy.263
  184.6 3.0 copy.266
  187.7 4.0 copy.265
  191.6 50.3 %while.24 = (s32[]{:T(128)}, bf16[4,1,256,4,64]{2,4,3,1,0:T(8,128)(2,1)}, s32[4]{0:T(128)S(1)}, bf16[1,4,256,16,64]{2,1,4,3,0:T(4,128)(2,1)}, bf16[1,256,16,64]{...) while((s32[]{:T(128)}, ...), condition=%wide.region_10.11_spmd, body=%wide.region_4.10_spmd.sunk | while | flops 282916864 | bytes 18541856 | solution.py:135
  246.3 5.0 collective-permute-start.3
  253.1 5.3 fusion.144
  259.7 4.9 collective-permute-start.5
  266.3 6.0 fusion.149
  277.1 144.4 %while.25 = (s32[]{:T(128)}, bf16[4,1,256,4,64]{2,4,3,1,0:T(8,128)(2,1)}, f32[4,1,1024,4,64]{2,4,3,1,0:T(8,128)}, f32[4,1,1024,4,64]{2,4,3,1,0:T(8,128)}, s32[4]...) while((s32[]{:T(128)}, ...), condition=%wide.region_20.21_spmd, body=%wide.region_13.0_spmd.sunk | while | flops 716965888 | bytes 68906344 | solution.py:215
  282.6 3.7 fusion.295
  294.9 6.8 fusion.301
  301.7 8.1 fusion.302
  309.8 3.5 fusion.303
  318.7 3.7 fusion.295
  331.1 6.9 fusion.301
  338.0 8.1 fusion.302
  346.0 3.4 fusion.303
  355.0 3.7 fusion.295
  367.2 6.8 fusion.301
  374.0 8.0 fusion.302
  382.0 3.5 fusion.303
  391.0 3.7 fusion.295
  403.2 6.8 fusion.301
  410.0 8.0 fusion.302
  418.0 3.4 fusion.303
  421.6 3.6 fusion.180
  425.2 5.7 reshape.760
  430.9 2.8 copy.298
  436.3 5.7 reshape.759
  442.1 2.9 convert.25
  445.0 3.8 fusion.234
  453.1 8.1 pad_maximum_fusion.2
  461.2 5.4 collective-permute-start.9
  472.5 3.1 fusion.214
  475.7 3.9 fusion.218
  480.7 8.4 pad_maximum_fusion.1
  497.1 2.7 stack.147
  499.8 4.9 slice_bitcast_fusion
  504.8 16.9 %collective-permute-done.7 = bf16[1,256,2048]{1,2,0:T(8,128)(2,1)S(1)} collective-permute-done((bf16[1,256,2048]{1,2,0:T(8,128)(2,1)}, bf16[1,256,2048]{1,2,0:T(8,128)(2,1)S(1)}, u32[]{:S(2)}, u32[]{:S(2)}) %collective-permute-start.7) | collective-permute-done | bytes 1048608 | tf_op jit(solution)/shard_map/ppermute | solution.py:16
  521.9 42.2 %collective-permute-done.8 = bf16[1,256,2048]{1,0,2:T(2,128)(2,1)} collective-permute-done((bf16[1,256,2048]{1,0,2:T(2,128)(2,1)}, bf16[1,256,2048]{1,0,2:T(2,128)(2,1)}, u32[]{:S(2)}, u32[]{:S(2)}) %collective-permute-start.8) | collective-permute-done | bytes 1048608 | tf_op jit(solution)/shard_map/ppermute | solution.py:16
  564.1 20.2 %fusion.130 = bf16[1,256,2048]{1,0,2:T(2,128)(2,1)S(1)} fusion(bf16[1,256,2048]{1,0,2:T(2,128)(2,1)} %collective-permute-done.9, bf16[1,256,2048]{1,0,2:T(2,128)(2,1)} %collective-permute-done.8, f32[1,256,2048]{1,2,0:T(8,128)S(1)} %convert_element_type.196, f32[1,256,1024]{1,0,2:T(1,128)S(1)} %get-tuple-element.488, f32[1,256,1024]{1,0,2:T(1,128)S(1)} %get-tuple-element.489), kind=kLoop, calls=%fused_computation.172 | loop fusion | flops 3670016 | bytes 7340032 | tf_op jit(solution)/shard_map/convert_element_type | solution.py:233
  585.5 31.5 %all-reduce.5.cloned.1.call-done = f32[128,2048]{1,0:T(8,128)} async-done(((f32[128,2048]{1,0:T(8,128)}), f32[128,2048]{1,0:T(8,128)}) %all-reduce.5.cloned.1.call-update) | async-done | bytes 1048592 | tf_op jit(solution)/shard_map/psum | solution.py:244
  618.5 60.1 %all-reduce.7.cloned.1.call-done = f32[31,1024]{1,0:T(8,128)} async-done(((f32[31,1024]{1,0:T(8,128)}), f32[31,1024]{1,0:T(8,128)}) %all-reduce.7.cloned.1.call-update) | async-done | bytes 126992 | tf_op jit(solution)/shard_map/psum | solution.py:168
  679.5 53.7 %all-gather.23.cloned.1.call-done = bf16[2048,2048]{0,1:T(8,128)(2,1)} async-done(((bf16[256,2048]{0,1:T(8,128)(2,1)}), bf16[2048,2048]{0,1:T(8,128)(2,1)}) %all-gather.23.cloned.1.call-update) | async-done | bytes 8388624 | tf_op jit(solution)/shard_map/all_gather | solution.py:246
  733.2 6.5 fusion.216
  740.9 4.9 multiply_reduce_fusion.1
  747.9 80.7 %all-reduce.9.cloned.1.call-done = f32[144,2048]{1,0:T(8,128)} async-done(((f32[144,2048]{1,0:T(8,128)}), f32[144,2048]{1,0:T(8,128)}) %all-reduce.9.cloned.1.call-update) | async-done | bytes 1179664 | tf_op jit(solution)/shard_map/psum | solution.py:260
  (273 shorter events, 174.6 us)
Async XLA Ops:
  7.2 129.5 %copy-start = (s32[16,1]{0,1:T(1,128)S(1)}, s32[16,1]{0,1:T(1,128)}, u32[]{:S(2)}) copy-start(s32[16,1]{0,1:T(1,128)} %param.22) | copy-start | bytes 196
  7.2 28.6 %all-gather.9.cloned.1.call-start = ((), (), s32[]{:S(2)}) async-start(), calls=%async_computation.1 | async-start | bytes 1179648 | tf_op jit(solution)/shard_map/all_gather | solution.py:77
  7.9 110.9 %all-gather.11.cloned.1.call-start = ((), (), s32[]{:S(2)}) async-start(), calls=%async_computation.2 | async-start | bytes 7077888 | tf_op jit(solution)/shard_map/all_gather | solution.py:91
  8.7 233.5 %all-gather.13.cloned.1.call-start = ((), (), s32[]{:S(2)}) async-start(), calls=%async_computation.3 | async-start | bytes 2359296 | tf_op jit(solution)/shard_map/all_gather | solution.py:92
  35.8 4.7 copy-start.30
  115.6 1.0 copy-start.13
  115.6 3.0 copy-start.25
  117.0 125.2 %copy-start.6 = (f32[256,1024]{1,0:T(8,128)}, f32[256,1024]{1,0:T(8,128)S(1)}, u32[]{:S(2)}) copy-start(f32[256,1024]{1,0:T(8,128)S(1)} %copy.267) | copy-start | bytes 3145732
  118.6 0.6 copy-start.27
  118.8 0.8 copy-start.19
  118.8 19.1 %copy-start.29 = (s32[16,2]{0,1:T(2,128)S(1)}, s32[16,2]{0,1:T(2,128)}, u32[]{:S(2)}) copy-start(s32[16,2]{0,1:T(2,128)} %param.21) | copy-start | bytes 388
  124.2 1.1 copy-start.20
  126.6 28.3 %collective-permute-start.2 = (bf16[1,256,2048]{2,1,0:T(8,128)(2,1)}, bf16[1,256,2048]{2,1,0:T(8,128)(2,1)}, u32[]{:S(2)}, u32[]{:S(2)}) collective-permute-start(bf16[1,256,2048]{2,1,0:T(8,128)(2,1)} %get-tuple-element.438), channel_id=1, source_target_pairs={{1,0},{2,1},{3,2},{4,3},{5,4},{6,5},{7,6},{8,7},{9,8},{10,9},{11,1... | collective-permute-start | bytes 3145736 | tf_op jit(solution)/shard_map/ppermute | solution.py:16
  127.9 29.1 %collective-permute-start.1 = (bf16[1,256,2048]{2,1,0:T(8,128)(2,1)}, bf16[1,256,2048]{2,1,0:T(8,128)(2,1)}, u32[]{:S(2)}, u32[]{:S(2)}) collective-permute-start(bf16[1,256,2048]{2,1,0:T(8,128)(2,1)} %get-tuple-element.438), channel_id=1, source_target_pairs={{0,2},{1,3},{2,4},{3,5},{4,6},{5,7},{6,8},{7,9},{8,10},{9,11},{10,... | collective-permute-start | bytes 3145736 | tf_op jit(solution)/shard_map/ppermute | solution.py:16
  134.0 43.0 %collective-permute-start = (bf16[1,256,2048]{2,1,0:T(8,128)(2,1)}, bf16[1,256,2048]{2,1,0:T(8,128)(2,1)}, u32[]{:S(2)}, u32[]{:S(2)}) collective-permute-start(bf16[1,256,2048]{2,1,0:T(8,128)(2,1)} %get-tuple-element.438), channel_id=1, source_target_pairs={{0,1},{1,2},{2,3},{3,4},{4,5},{5,6},{6,7},{7,8},{8,9},{9,10},{10,1... | collective-permute-start | bytes 3145736 | tf_op jit(solution)/shard_map/ppermute | solution.py:16
  136.6 335.9 %all-gather.19.cloned.1.call-start = ((), (), s32[]{:S(2)}) async-start(), calls=%async_computation.6 | async-start | bytes 4718592 | tf_op jit(solution)/shard_map/all_gather | solution.py:181
  191.6 50.4 %copy-start.23 = (f32[31,1024]{1,0:T(8,128)S(1)}, f32[31,1024]{1,0:T(8,128)}, u32[]{:S(2)}) copy-start(f32[31,1024]{1,0:T(8,128)} %param.20) | copy-start | bytes 380932
  198.6 4.0 copy-start.10
  211.2 4.0 copy-start.10
  223.8 4.0 copy-start.10
  236.3 4.0 copy-start.10
  242.0 2.8 copy-start.24
  242.0 11.1 %copy-start.17 = (bf16[1,256,1024]{2,1,0:T(8,128)(2,1)S(1)}, bf16[1,256,1024]{2,1,0:T(8,128)(2,1)}, u32[]{:S(2)}) copy-start(bf16[1,256,1024]{2,1,0:T(8,128)(2,1)} %param.23) | copy-start | bytes 1572868
  242.0 230.5 %all-gather.21.cloned.1.call-start = ((), (), s32[]{:S(2)}) async-start(), calls=%async_computation.7 | async-start | bytes 4718592 | tf_op jit(solution)/shard_map/all_gather | solution.py:183
  244.8 27.6 %copy-start.8 = (bf16[256,1024]{1,0:T(8,128)(2,1)}, bf16[256,1024]{1,0:T(8,128)(2,1)S(1)}, u32[]{:S(2)}) copy-start(bf16[256,1024]{1,0:T(8,128)(2,1)S(1)} %get-tuple-element.485) | copy-start | bytes 1572868
  245.0 6.4 collective-permute-start.4
  246.3 6.6 collective-permute-start.3
  253.1 5.3 copy-start.2
  258.4 14.0 %copy-start.11 = (bf16[1,256,1024]{2,1,0:T(8,128)(2,1)}, bf16[1,256,1024]{2,1,0:T(8,128)(2,1)S(1)}, u32[]{:S(2)}) copy-start(bf16[1,256,1024]{2,1,0:T(8,128)(2,1)S(1)} %get-tuple-element.411) | copy-start | bytes 1572868
  258.4 6.2 collective-permute-start.6
  259.7 6.4 collective-permute-start.5
  266.3 8.0 copy-start.18
  273.6 202.0 %all-gather.15.cloned.1.call-start = ((), (), s32[]{:S(2)}) async-start(), calls=%async_computation.4 | async-start | bytes 4718592 | tf_op jit(solution)/shard_map/all_gather | solution.py:238
  274.2 201.4 %all-gather.17.cloned.1.call-start = ((), (), s32[]{:S(2)}) async-start(), calls=%async_computation.5 | async-start | bytes 4718592 | tf_op jit(solution)/shard_map/all_gather | solution.py:240
  277.1 144.5 %copy-start.3 = (f32[1,286,1024]{2,1,0:T(8,128)S(1)}, f32[1,286,1024]{2,1,0:T(8,128)}, u32[]{:S(2)}) copy-start(f32[1,286,1024]{2,1,0:T(8,128)} %copy-done.2) | copy-start | bytes 3514372
  291.7 1.7 copy-start.4
  293.3 1.0 copy-start.5
  327.9 1.7 copy-start.4
  329.5 1.0 copy-start.5
  364.0 1.7 copy-start.4
  365.7 1.0 copy-start.5
  400.0 1.7 copy-start.4
  401.7 1.0 copy-start.5
  421.5 195.5 %all-reduce.5.cloned.1.call-start = ((), (), s32[]{:S(2)}) async-start(), calls=%async_computation.8 | async-start | bytes 2097152 | tf_op jit(solution)/shard_map/psum | solution.py:244
  461.2 60.6 %collective-permute-start.9 = (bf16[1,256,2048]{1,0,2:T(2,128)(2,1)}, bf16[1,256,2048]{1,0,2:T(2,128)(2,1)}, u32[]{:S(2)}, u32[]{:S(2)}) collective-permute-start(bf16[1,256,2048]{1,0,2:T(2,128)(2,1)} %pad_maximum_fusion.2), channel_id=1, source_target_pairs={{0,1},{1,2},{2,3},{3,4},{4,5},{5,6},{6,7},{7,8},{8,9},{9,10},{10,1... | collective-permute-start | bytes 3145736 | tf_op jit(solution)/shard_map/ppermute | solution.py:16
  480.7 14.6 %copy-start.12 = (bf16[1,256,1024]{2,1,0:T(8,128)(2,1)S(1)}, bf16[1,256,1024]{2,1,0:T(8,128)(2,1)}, u32[]{:S(2)}) copy-start(bf16[1,256,1024]{2,1,0:T(8,128)(2,1)} %copy-done.11) | copy-start | bytes 1572868
  480.7 197.9 %all-reduce.7.cloned.1.call-start = ((), (), s32[]{:S(2)}) async-start(), calls=%async_computation.10 | async-start | bytes 262144 | tf_op jit(solution)/shard_map/psum | solution.py:168
  489.1 75.1 %collective-permute-start.8 = (bf16[1,256,2048]{1,0,2:T(2,128)(2,1)}, bf16[1,256,2048]{1,0,2:T(2,128)(2,1)}, u32[]{:S(2)}, u32[]{:S(2)}) collective-permute-start(bf16[1,256,2048]{1,0,2:T(2,128)(2,1)} %pad_maximum_fusion.1), channel_id=1, source_target_pairs={{2,0},{3,1},{4,2},{5,3},{6,4},{7,5},{8,6},{9,7},{10,8},{11,9},{12,... | collective-permute-start | bytes 3145736 | tf_op jit(solution)/shard_map/ppermute | solution.py:16
  494.0 27.7 %collective-permute-start.7 = (bf16[1,256,2048]{1,2,0:T(8,128)(2,1)}, bf16[1,256,2048]{1,2,0:T(8,128)(2,1)S(1)}, u32[]{:S(2)}, u32[]{:S(2)}) collective-permute-start(bf16[1,256,2048]{1,2,0:T(8,128)(2,1)} %pad_maximum_fusion.5), channel_id=1, source_target_pairs={{1,0},{2,1},{3,2},{4,3},{5,4},{6,5},{7,6},{8,7},{9,8},{10,9},{11,1... | collective-permute-start | bytes 3145736 | tf_op jit(solution)/shard_map/ppermute | solution.py:16
  499.8 233.5 %all-gather.23.cloned.1.call-start = ((), (), s32[]{:S(2)}) async-start(), calls=%async_computation.9 | async-start | bytes 9437184 | tf_op jit(solution)/shard_map/all_gather | solution.py:246
  584.3 33.0 %copy-start.9 = (bf16[256,1024]{1,0:T(8,128)(2,1)S(1)}, bf16[256,1024]{1,0:T(8,128)(2,1)}, u32[]{:S(2)}) copy-start(bf16[256,1024]{1,0:T(8,128)(2,1)} %copy-done.8) | copy-start | bytes 1572868
  584.3 33.0 %copy-start.15 = (f32[1,256,1024]{2,1,0:T(8,128)S(1)}, f32[1,256,1024]{2,1,0:T(8,128)}, u32[]{:S(2)}) copy-start(f32[1,256,1024]{2,1,0:T(8,128)} %get-tuple-element.412) | copy-start | bytes 3145732
  617.0 211.7 %all-reduce.9.cloned.1.call-start = ((), (), s32[]{:S(2)}) async-start(), calls=%async_computation.11 | async-start | bytes 2359296 | tf_op jit(solution)/shard_map/psum | solution.py:260
  679.5 61.4 %copy-start.7 = (f32[256,1024]{1,0:T(8,128)S(1)}, f32[256,1024]{1,0:T(8,128)}, u32[]{:S(2)}) copy-start(f32[256,1024]{1,0:T(8,128)} %copy-done.6) | copy-start | bytes 3145732
  679.5 61.4 %copy-start.16 = (bf16[1,256,2048]{1,2,0:T(8,128)(2,1)S(1)}, bf16[1,256,2048]{1,2,0:T(8,128)(2,1)}, u32[]{:S(2)}) copy-start(bf16[1,256,2048]{1,2,0:T(8,128)(2,1)} %copy.299) | copy-start | bytes 3145732
  679.5 61.4 %copy-start.22 = (bf16[4,1,256,4,64]{2,4,3,1,0:T(8,128)(2,1)S(1)}, bf16[4,1,256,4,64]{2,4,3,1,0:T(8,128)(2,1)}, u32[]{:S(2)}) copy-start(bf16[4,1,256,4,64]{2,4,3,1,0:T(8,128)(2,1)} %get-tuple-element.119) | copy-start | bytes 1572868
  679.5 61.4 %copy-start.26 = (f32[1024]{0:T(1024)S(1)}, f32[1024]{0:T(1024)}, u32[]{:S(2)}) copy-start(f32[1024]{0:T(1024)} %param.18) | copy-start | bytes 12292
  740.9 4.9 copy-start.14
  740.9 4.9 copy-start.28
  740.9 6.1 copy-start.21
  745.8 87.0 %copy-start.1 = (s32[16,1]{0,1:T(1,128)S(1)}, s32[16,1]{0,1:T(1,128)}, u32[]{:S(2)}) copy-start(s32[16,1]{0,1:T(1,128)} %param.22) | copy-start | bytes 196
Sparse Core Ops, SparseCore 0:
  9.7 26.0 all-gather.8
  37.5 42.0 all-gather.10
  136.7 23.8 all-gather.12
  242.1 36.2 all-gather.18
  279.9 33.1 all-gather.20
  314.7 32.1 all-gather.14
  421.6 40.7 all-gather.16
  480.8 136.1 all-reduce.4
  619.9 58.6 all-reduce.6
  680.2 53.0 all-gather.22
  741.0 87.6 all-reduce.8

commit v3 on v2

--- a/solution.py
+++ b/solution.py
@@ -76,17 +76,18 @@
     ids_whole = lax.all_gather(ids, "ctx", axis=1, tiled=True)
     table_whole = lax.all_gather(tables, "dp", axis=1, tiled=True)
     vocab = table_whole.shape[1]
-    entries = lax.broadcasted_iota(jnp.int32, (1, vocab), 1)
-    columns = jnp.zeros((ids_whole.shape[1], table_whole.shape[2]), jnp.float32)
+    entries = lax.broadcasted_iota(jnp.int32, (vocab, 1), 0)
+    transposed = jnp.zeros((table_whole.shape[2], ids_whole.shape[1]), jnp.float32)
     for codebook in range(table_whole.shape[0]):
-        picks = (ids_whole[0, :, codebook][:, None] == entries).astype(jnp.bfloat16)
-        columns = columns + jnp.dot(
-            picks, table_whole[codebook], preferred_element_type=jnp.float32
-        )
-    columns = columns[None]
-    embedded = lax.all_to_all(
-        columns.astype(jnp.bfloat16), "ctx", split_axis=1, concat_axis=2, tiled=True
-    )
+        picks = (entries == ids_whole[0, :, codebook][None, :]).astype(jnp.bfloat16)
+        transposed = transposed + lax.dot_general(
+            table_whole[codebook], picks, (((0,), (0,)), ((), ())),
+            preferred_element_type=jnp.float32,
+        )
+    ctx_count = lax.axis_size("ctx")
+    transposed = transposed.astype(jnp.bfloat16).reshape(transposed.shape[0], ctx_count, frames_dev)
+    gathered = lax.all_to_all(transposed, "ctx", split_axis=1, concat_axis=0, tiled=True)
+    embedded = gathered.reshape(-1, frames_dev).T[None]
     weight_qkv, weight_out = (
         lax.all_gather(w_qkv, "dp", axis=0, tiled=True),
         lax.all_gather(w_out, "dp", axis=0, tiled=True),
@@ -165,7 +166,7 @@
             :, start_row : start_row + frames_dev
         ]
     kernel_rows = jnp.stack(kernel_list)
-    kernel_dp = lax.psum(kernel_rows, "dp")
+    kernel_dp = jnp.sum(lax.all_gather(kernel_rows, "dp"), axis=0)
     grad_middle = (
         upstream.reshape(-1, model_width)
         + norm_back(middle_wide, conv_inverse, conv_gain, grad_input.reshape(-1, model_width))
@@ -215,6 +216,7 @@
     grad_query, grad_key, grad_value = lax.map(
         backward_group, jnp.arange(group_count, dtype=jnp.int32)
     )
+    kernel_dp, grad_query = lax.optimization_barrier((kernel_dp, grad_query))
     grad_query = jnp.moveaxis(grad_query, 0, 2).reshape(recordings * frames_dev, model_width)
     grad_key = jnp.moveaxis(grad_key, 0, 2).reshape(recordings, seen_count, frames_dev, model_width)
     grad_value = jnp.moveaxis(grad_value, 0, 2).reshape(
@@ -241,8 +243,7 @@
     grad_wq = lax.dot_general(
         normed_columns, query_rows, contract_rows, preferred_element_type=jnp.float32
     )
-    early = lax.psum(jnp.concatenate([grad_wq, grad_wout], axis=1), "ctx")
-    early, pair_part = lax.optimization_barrier((early, grad_projected[:, model_width:]))
+    pair_part = grad_projected[:, model_width:]
     pair_rows = lax.all_gather(pair_part, "dp", axis=0, tiled=True)
     grad_wkv = lax.dot_general(
         normed_columns, pair_rows, contract_rows, preferred_element_type=jnp.float32
@@ -253,19 +254,19 @@
     grad_embedded = (
         grad_middle.astype(jnp.float32) + norm_back(features, attn_inverse, attn_gain, grad_normed)
     ).astype(jnp.bfloat16)
-    row_width = grad_wkv.shape[1]
+    weight_rows = jnp.concatenate([grad_wq, grad_wkv, grad_wout], axis=1)
+    row_width = weight_rows.shape[1]
     kernel_padded = jnp.pad(
         kernel_dp, ((0, (-tap_count * model_width) % row_width // model_width), (0, 0))
     )
-    late = lax.psum(
-        jnp.concatenate([grad_wkv, kernel_padded.reshape(-1, row_width)], axis=0), "ctx"
-    )
-    shard_rows = grad_wkv.shape[0]
-    grad_qkv = jnp.concatenate(
-        [early[:, :model_width], late[:shard_rows]], axis=1
-    )
-    grad_out = early[:, model_width:]
-    grad_kernel = late[shard_rows:].reshape(-1, model_width)[:tap_count]
+    summed = lax.psum(
+        jnp.concatenate([weight_rows, kernel_padded.reshape(-1, row_width)], axis=0), "ctx"
+    )
+    shard_rows = weight_rows.shape[0]
+    qkv_width = grad_wq.shape[1] + grad_wkv.shape[1]
+    grad_qkv = summed[:shard_rows, :qkv_width]
+    grad_out = summed[:shard_rows, qkv_width:]
+    grad_kernel = summed[shard_rows:].reshape(-1, model_width)[:tap_count]
     return (
         block_out,
         grad_embedded.reshape(recordings, frames_dev, model_width),

time: 851 us -> 810 us (0.952)
  waiting for transfers between devices: 329 us -> 287 us
  other arithmetic: 98.3 us -> 70.8 us
  blocking collectives: 42.6 us -> 58.9 us
  local copies, waits for them, and re-layouts: 109 us -> 122 us
    psum x3 -> x1, waiting for transfers between devices: 172 us -> 82.7 us  [on_device(): lax.psum(jnp.concatenate([weight_rows, kernel_padded.reshape(-1, row_widt...]
    all_gather x1, waiting for transfers between devices: 53.7 us -> 117 us  [on_device(): pair_rows = lax.all_gather(pair_part, 'dp', axis=0, tiled=True)]
    unnamed x1 -> x0, other arithmetic: 22.4 us -> none
    ppermute x6, waiting for transfers between devices: 95.4 us -> 77.7 us  [from_behind(): lax.ppermute(value, axis, [(source, source + steps) for source in range(f...]
    all_gather x0 -> x1, blocking collectives: none -> 16.2 us  [on_device(): kernel_dp = jnp.sum(lax.all_gather(kernel_rows, 'dp'), axis=0)]
    another operation x12, local copies, waits for them, and re-layouts: 10.8 us -> 26.6 us
  transfers between devices with their start and end apart: 21 -> 19, of which waited for: 12 -> 9; matrix products, arithmetic and copies ran while one was open for 47% -> 47% of each run, Pallas kernels for 0% -> 0%
where the time goes in v3:
time: 810 us; the launch traced here: 798 us
  waiting for transfers between devices  287 us (35%)
  matrix products  212 us (26%)
  local copies, waits for them, and re-layouts  122 us (15%)
  other arithmetic  70.8 us (9%)
  blocking collectives  58.9 us (7%)
  starting transfers between devices  26.3 us (3%)
  between operations  15.6 us (2%)
    all_gather x1, waiting for transfers between devices, on_device(): pair_rows = lax.all_gather(pair_part, 'dp', axis=0, tiled=True)  117 us
    psum x1, waiting for transfers between devices, on_device(): lax.psum(jnp.concatenate([weight_rows, kernel_padded.reshape(-1, row_widt...  82.7 us
    ppermute x6, waiting for transfers between devices, from_behind(): lax.ppermute(value, axis, [(source, source + steps) for source in range(f...  77.7 us
    dot_general x32, matrix products, block_scores(): jnp.einsum('rqhd,rkhd->rhqk', queries, key_block, preferred_element_type=...  51.9 us
    dot_general x4, matrix products, backward_group(): jnp.einsum('rhqk,rqhd->rkhd', grad_scores, queries, preferred_element_typ...  29.7 us
    dot_general x4, matrix products, backward_group(): jnp.einsum('rhqk,rkhd->rqhd', grad_scores, key_flat, preferred_element_ty...  28.5 us
    another operation x12, local copies, waits for them, and re-layouts  26.6 us
    dot_general x8, matrix products, on_device(): lax.dot_general(table_whole[codebook], picks, (((0,), (0,)), ((), ())), p...  26.1 us
  transfers between devices with their start and end apart: 19, of which 9 were waited for; matrix products, arithmetic and copies ran while one was open for 47% of the time, Pallas kernels for 0%

profile of v3, /device:TPU:0, one launch (start us, length us, event | category | flops | bytes accessed | tf_op | source)
XLA Modules:
  0.0 798.3 jit_solution(3212954255579846021)
XLA Ops:
  8.7 24.0 %all_gather.33 = s32[1,4096,8]{1,2,0:T(8,128)S(1)} all-gather(s32[1,256,8]{1,2,0:T(8,128)} %param.14), channel_id=1, replica_groups=mesh['dp'=8,'ctx'=16] {'ctx'}, dimensions={1}, use_global_device_ids=true | all-gather | bytes 139264 | tf_op jit(solution)/shard_map/all_gather | solution.py:76
  32.8 2.9 all-gather.12.cloned.1.call-done
  35.8 4.0 fusion.102
  39.8 3.1 fusion.127
  42.9 3.1 fusion.126
  46.0 3.1 fusion.125
  49.1 3.5 fusion.124
  52.6 3.1 fusion.123
  55.7 3.1 fusion.122
  58.8 3.1 fusion.128
  61.9 18.7 %all_to_all.4 = bf16[64,16,256]{2,0,1:T(8,128)(2,1)S(1)} all-to-all(bf16[64,16,256]{2,0,1:T(8,128)(2,1)S(1)} %bitcast.428), channel_id=1, replica_groups=mesh['dp'=8,'ctx'=16] {'ctx'}, dimensions={1} | all-to-all | bytes 1048576 | tf_op jit(solution)/shard_map/all_to_all | solution.py:89
  82.2 4.6 fusion.129
  88.0 3.5 collective-permute-start
  91.5 3.2 collective-permute-start.1
  100.3 13.8 %collective-permute-done = bf16[1,256,2048]{2,1,0:T(8,128)(2,1)} collective-permute-done((bf16[1,256,2048]{2,1,0:T(8,128)(2,1)S(1)}, bf16[1,256,2048]{2,1,0:T(8,128)(2,1)}, u32[]{:S(2)}, u32[]{:S(2)}) %collective-permute-start) | collective-permute-done | bytes 1048608 | tf_op jit(solution)/shard_map/ppermute | solution.py:16
  114.1 20.3 %collective-permute-done.1 = bf16[1,256,2048]{2,1,0:T(8,128)(2,1)} collective-permute-done((bf16[1,256,2048]{2,1,0:T(8,128)(2,1)S(1)}, bf16[1,256,2048]{2,1,0:T(8,128)(2,1)}, u32[]{:S(2)}, u32[]{:S(2)}) %collective-permute-start.1) | collective-permute-done | bytes 1048608 | tf_op jit(solution)/shard_map/ppermute | solution.py:16
  134.4 5.3 collective-permute-done.2
  147.2 3.1 copy.163
  150.3 3.9 copy.162
  154.2 65.7 %while.24 = (s32[]{:T(128)}, bf16[4,1,256,4,64]{2,4,3,1,0:T(8,128)(2,1)}, s32[4]{0:T(128)S(1)}, bf16[1,4,256,16,64]{2,1,4,3,0:T(4,128)(2,1)}, bf16[1,256,16,64]{...) while((s32[]{:T(128)}, ...), condition=%wide.region_9.10_spmd, body=%wide.region_3.9_spmd.sunk | while | flops 282916864 | bytes 20639508 | solution.py:136
  167.8 2.9 fusion.288
  184.2 2.9 fusion.288
  200.7 2.9 fusion.288
  217.1 2.9 fusion.288
  220.0 2.9 fusion.149
  223.1 4.3 collective-permute-start.3
  229.1 4.1 collective-permute-done.4
  233.4 5.2 fusion.146
  247.0 16.2 %all-gather.2 = f32[8,31,1024]{2,1,0:T(8,128)S(1)} all-gather(f32[1,31,1024]{2,1,0:T(8,128)S(1)} %bitcast.430), channel_id=2, replica_groups=mesh['dp'=8,'ctx'=16] {'dp'}, dimensions={0}, use_global_device_ids=true | all-gather | bytes 1142784 | tf_op jit(solution)/shard_map/all_gather | solution.py:169
  264.1 5.6 fusion.151
  273.7 158.0 %while.25 = (s32[]{:T(128)}, bf16[4,1,256,4,64]{2,4,3,1,0:T(8,128)(2,1)}, f32[4,1,1024,4,64]{2,4,3,1,0:T(8,128)}, f32[4,1,1024,4,64]{2,4,3,1,0:T(8,128)}, s32[4]...) while((s32[]{:T(128)}, ...), condition=%wide.region_51.52_spmd, body=%wide.region_44.51_spmd.sunk | while | flops 716965888 | bytes 64713528 | solution.py:216
  282.3 3.9 fusion.305
  290.6 3.9 fusion.297
  294.4 7.4 fusion.304
  306.3 7.1 fusion.303
  321.7 3.9 fusion.305
  330.0 3.9 fusion.297
  333.8 7.5 fusion.304
  345.8 7.1 fusion.303
  361.2 3.9 fusion.305
  369.4 3.9 fusion.297
  373.3 7.4 fusion.304
  385.2 7.1 fusion.303
  400.6 3.9 fusion.305
  408.8 3.9 fusion.297
  412.6 7.4 fusion.304
  424.5 7.1 fusion.303
  433.1 5.8 reshape.758
  438.8 5.7 reshape.759
  444.5 2.9 convert.26
  453.8 2.9 copy.199
  462.7 8.1 %pad_maximum_fusion.2 = bf16[1,256,2048]{1,0,2:T(2,128)(2,1)} fusion(bf16[1,256,1024]{1,0,2:T(2,128)(2,1)S(1)} %concatenate.135, bf16[1,256,1024]{1,0,2:T(2,128)(2,1)S(1)} %copy.173), kind=kLoop, calls=%fused_computation.173 | loop fusion | flops 524288 | bytes 2097152 | tf_op jit(solution)/shard_map/concatenate | solution.py:227
  478.7 7.3 pad_maximum_fusion.3
  486.0 5.5 collective-permute-start.9
  491.5 5.2 slice_bitcast_fusion
  498.1 26.9 %collective-permute-done.8 = bf16[1,256,2048]{1,0,2:T(2,128)(2,1)S(1)} collective-permute-done((bf16[1,256,2048]{1,0,2:T(2,128)(2,1)}, bf16[1,256,2048]{1,0,2:T(2,128)(2,1)S(1)}, u32[]{:S(2)}, u32[]{:S(2)}) %collective-permute-start.8) | collective-permute-done | bytes 1048608 | tf_op jit(solution)/shard_map/ppermute | solution.py:16
  525.0 11.5 %collective-permute-done.9 = bf16[1,256,2048]{1,0,2:T(2,128)(2,1)S(1)} collective-permute-done((bf16[1,256,2048]{1,0,2:T(2,128)(2,1)S(1)}, bf16[1,256,2048]{1,0,2:T(2,128)(2,1)S(1)}, u32[]{:S(2)}, u32[]{:S(2)}) %collective-permute-start.9) | collective-permute-done | bytes 1048608 | tf_op jit(solution)/shard_map/ppermute | solution.py:16
  536.5 19.8 %fusion.132 = bf16[1,256,2048]{1,0,2:T(2,128)(2,1)} fusion(bf16[1,256,2048]{1,0,2:T(2,128)(2,1)S(1)} %collective-permute-done.9, bf16[1,256,2048]{1,0,2:T(2,128)(2,1)S(1)} %collective-permute-done.8, f32[1,256,2048]{1,2,0:T(8,128)S(1)} %convert_element_type.189, f32[1,256,1024]{1,0,2:T(1,128)S(1)} %get-tuple-element.423, ...), kind=kLoop, calls=%fused_computation.175 | loop fusion | flops 3670016 | bytes 7340032 | tf_op jit(solution)/shard_map/convert_element_type | solution.py:235
  556.7 3.9 fusion.222
  560.7 3.1 fusion.219
  563.8 116.9 %all-gather.26.cloned.1.call-done = bf16[1,2048,2048]{1,0,2:T(2,128)(2,1)} async-done(((bf16[1,256,2048]{1,0,2:T(2,128)(2,1)}), bf16[1,2048,2048]{1,0,2:T(2,128)(2,1)}) %all-gather.26.cloned.1.call-update) | async-done | bytes 8388624 | tf_op jit(solution)/shard_map/all_gather | solution.py:247
  680.7 11.2 %fusion.110 = f32[128,2048]{1,0:T(8,128)S(1)} fusion(bf16[1,2048,2048]{1,0,2:T(2,128)(2,1)} %all-gather.26.cloned.1.call-done, bf16[2048,1024]{1,0:T(8,128)(2,1)} %all-gather.18.cloned.1.call-done, s32[]{:T(128)S(6)} %select_n.70), kind=kOutput, calls=%fused_computation.146 | convolution fusion | flops 1073741824 | bytes 18350084 | tf_op jit(solution)/shard_map/dot_general | solution.py:248
  696.4 4.8 fusion.216
  702.4 82.7 %all-reduce.3.cloned.1.call-done = f32[136,4096]{1,0:T(8,128)} async-done(((f32[136,4096]{1,0:T(8,128)}), f32[136,4096]{1,0:T(8,128)}) %all-reduce.3.cloned.1.call-update) | async-done | bytes 2228240 | tf_op jit(solution)/shard_map/psum | solution.py:262
  (236 shorter events, 184.4 us)
Async XLA Ops:
  7.2 89.0 %copy-start = (s32[16,1]{0,1:T(1,128)S(1)}, s32[16,1]{0,1:T(1,128)}, u32[]{:S(2)}) copy-start(s32[16,1]{0,1:T(1,128)} %param.22) | copy-start | bytes 196
  7.2 28.6 %all-gather.12.cloned.1.call-start = ((), (), s32[]{:S(2)}) async-start(), calls=%async_computation.1 | async-start | bytes 1179648 | tf_op jit(solution)/shard_map/all_gather | solution.py:77
  7.9 73.6 %all-gather.14.cloned.1.call-start = ((), (), s32[]{:S(2)}) async-start(), calls=%async_computation.2 | async-start | bytes 7077888 | tf_op jit(solution)/shard_map/all_gather | solution.py:92
  8.7 211.3 %all-gather.16.cloned.1.call-start = ((), (), s32[]{:S(2)}) async-start(), calls=%async_computation.3 | async-start | bytes 2359296 | tf_op jit(solution)/shard_map/all_gather | solution.py:93
  35.8 4.0 copy-start.22
  61.9 19.4 %copy-start.17 = (f32[1024]{0:T(1024)S(1)}, f32[1024]{0:T(1024)}, u32[]{:S(2)}) copy-start(f32[1024]{0:T(1024)} %param.18) | copy-start | bytes 12292
  81.1 5.8 copy-start.4
  81.3 0.7 copy-start.19
  81.4 0.8 copy-start.11
  81.4 16.0 %copy-start.21 = (s32[16,2]{0,1:T(2,128)S(1)}, s32[16,2]{0,1:T(2,128)}, u32[]{:S(2)}) copy-start(s32[16,2]{0,1:T(2,128)} %param.21) | copy-start | bytes 388
  81.5 16.7 %copy-start.15 = (f32[31,1024]{1,0:T(8,128)S(1)}, f32[31,1024]{1,0:T(8,128)}, u32[]{:S(2)}) copy-start(f32[31,1024]{1,0:T(8,128)} %param.20) | copy-start | bytes 380932
  86.9 1.1 copy-start.12
  88.0 26.1 %collective-permute-start = (bf16[1,256,2048]{2,1,0:T(8,128)(2,1)S(1)}, bf16[1,256,2048]{2,1,0:T(8,128)(2,1)}, u32[]{:S(2)}, u32[]{:S(2)}) collective-permute-start(bf16[1,256,2048]{2,1,0:T(8,128)(2,1)S(1)} %get-tuple-element.375), channel_id=1, source_target_pairs={{0,1},{1,2},{2,3},{3,4},{4,5},{5,6},{6,7},{7,8},{8,9},{9,10},{10,1... | collective-permute-start | bytes 3145736 | tf_op jit(solution)/shard_map/ppermute | solution.py:16
  91.5 42.8 %collective-permute-start.1 = (bf16[1,256,2048]{2,1,0:T(8,128)(2,1)S(1)}, bf16[1,256,2048]{2,1,0:T(8,128)(2,1)}, u32[]{:S(2)}, u32[]{:S(2)}) collective-permute-start(bf16[1,256,2048]{2,1,0:T(8,128)(2,1)S(1)} %get-tuple-element.375), channel_id=1, source_target_pairs={{0,2},{1,3},{2,4},{3,5},{4,6},{5,7},{6,8},{7,9},{8,10},{9,11},{10,... | collective-permute-start | bytes 3145736 | tf_op jit(solution)/shard_map/ppermute | solution.py:16
  94.8 44.9 %collective-permute-start.2 = (bf16[1,256,2048]{2,1,0:T(8,128)(2,1)S(1)}, bf16[1,256,2048]{2,1,0:T(8,128)(2,1)}, u32[]{:S(2)}, u32[]{:S(2)}) collective-permute-start(bf16[1,256,2048]{2,1,0:T(8,128)(2,1)S(1)} %get-tuple-element.375), channel_id=1, source_target_pairs={{1,0},{2,1},{3,2},{4,3},{5,4},{6,5},{7,6},{8,7},{9,8},{10,9},{11,1... | collective-permute-start | bytes 3145736 | tf_op jit(solution)/shard_map/ppermute | solution.py:16
  96.1 460.6 %all-gather.18.cloned.1.call-start = ((), (), s32[]{:S(2)}) async-start(), calls=%async_computation.4 | async-start | bytes 4718592 | tf_op jit(solution)/shard_map/all_gather | solution.py:240
  162.0 1.0 copy-start.3
  178.4 1.0 copy-start.3
  194.8 1.0 copy-start.3
  211.3 1.0 copy-start.3
  220.0 2.9 copy-start.16
  220.0 13.4 %copy-start.10 = (bf16[1,256,1024]{2,1,0:T(8,128)(2,1)S(1)}, bf16[1,256,1024]{2,1,0:T(8,128)(2,1)}, u32[]{:S(2)}) copy-start(bf16[1,256,1024]{2,1,0:T(8,128)(2,1)} %param.23) | copy-start | bytes 1572868
  222.9 46.8 %copy-start.7 = (bf16[256,1024]{1,0:T(8,128)(2,1)}, bf16[256,1024]{1,0:T(8,128)(2,1)S(1)}, u32[]{:S(2)}) copy-start(bf16[256,1024]{1,0:T(8,128)(2,1)S(1)} %get-tuple-element.420) | copy-start | bytes 1572868
  223.1 5.9 collective-permute-start.3
  227.4 5.8 collective-permute-start.4
  228.8 327.9 %all-gather.20.cloned.1.call-start = ((), (), s32[]{:S(2)}) async-start(), calls=%async_computation.5 | async-start | bytes 4718592 | tf_op jit(solution)/shard_map/all_gather | solution.py:242
  242.9 21.0 %collective-permute-start.5 = (bf16[1,15,1024]{2,1,0:T(8,128)(2,1)S(1)}, bf16[1,15,1024]{2,1,0:T(8,128)(2,1)S(1)}, u32[]{:S(2)}, u32[]{:S(2)}) collective-permute-start(bf16[1,15,1024]{2,1,0:T(8,128)(2,1)S(1)} %get-tuple-element.376), channel_id=1, source_target_pairs={{0,1},{1,2},{2,3},{3,4},{4,5},{5,6},{6,7},{7,8},{8,9},{9,10},{10,1... | collective-permute-start | bytes 92168 | tf_op jit(solution)/shard_map/ppermute | solution.py:24
  245.5 18.4 %collective-permute-start.6 = (bf16[1,15,1024]{2,1,0:T(8,128)(2,1)S(1)}, bf16[1,15,1024]{2,1,0:T(8,128)(2,1)S(1)}, u32[]{:S(2)}, u32[]{:S(2)}) collective-permute-start(bf16[1,15,1024]{2,1,0:T(8,128)(2,1)S(1)} %get-tuple-element.377), channel_id=1, source_target_pairs={{1,0},{2,1},{3,2},{4,3},{5,4},{6,5},{7,6},{8,7},{9,8},{10,9},{11,1... | collective-permute-start | bytes 92168 | tf_op jit(solution)/shard_map/ppermute | solution.py:27
  270.1 3.5 copy-start.8
  281.7 4.6 copy-start.2
  321.1 4.6 copy-start.2
  360.6 4.6 copy-start.2
  399.9 4.6 copy-start.2
  431.7 129.0 %all-gather.22.cloned.1.call-start = ((), (), s32[]{:S(2)}) async-start(), calls=%async_computation.6 | async-start | bytes 4718592 | tf_op jit(solution)/shard_map/all_gather | solution.py:182
  432.3 128.4 %all-gather.24.cloned.1.call-start = ((), (), s32[]{:S(2)}) async-start(), calls=%async_computation.7 | async-start | bytes 4718592 | tf_op jit(solution)/shard_map/all_gather | solution.py:184
  433.0 247.7 %all-gather.26.cloned.1.call-start = ((), (), s32[]{:S(2)}) async-start(), calls=%async_computation.9 | async-start | bytes 18874368 | tf_op jit(solution)/shard_map/all_gather | solution.py:247
  458.7 38.0 %collective-permute-start.7 = (bf16[1,256,2048]{1,2,0:T(8,128)(2,1)}, bf16[1,256,2048]{1,2,0:T(8,128)(2,1)}, u32[]{:S(2)}, u32[]{:S(2)}) collective-permute-start(bf16[1,256,2048]{1,2,0:T(8,128)(2,1)} %pad_maximum_fusion.4), channel_id=1, source_target_pairs={{1,0},{2,1},{3,2},{4,3},{5,4},{6,5},{7,6},{8,7},{9,8},{10,9},{11,1... | collective-permute-start | bytes 3145736 | tf_op jit(solution)/shard_map/ppermute | solution.py:16
  470.8 54.2 %collective-permute-start.8 = (bf16[1,256,2048]{1,0,2:T(2,128)(2,1)}, bf16[1,256,2048]{1,0,2:T(2,128)(2,1)S(1)}, u32[]{:S(2)}, u32[]{:S(2)}) collective-permute-start(bf16[1,256,2048]{1,0,2:T(2,128)(2,1)} %pad_maximum_fusion.2), channel_id=1, source_target_pairs={{2,0},{3,1},{4,2},{5,3},{6,4},{7,5},{8,6},{9,7},{10,8},{11,9},{12,... | collective-permute-start | bytes 3145736 | tf_op jit(solution)/shard_map/ppermute | solution.py:16
  486.0 50.5 %collective-permute-start.9 = (bf16[1,256,2048]{1,0,2:T(2,128)(2,1)S(1)}, bf16[1,256,2048]{1,0,2:T(2,128)(2,1)S(1)}, u32[]{:S(2)}, u32[]{:S(2)}) collective-permute-start(bf16[1,256,2048]{1,0,2:T(2,128)(2,1)S(1)} %pad_maximum_fusion.3), channel_id=1, source_target_pairs={{0,1},{1,2},{2,3},{3,4},{4,5},{5,6},{6,7},{7,8},{8,9},{9,10},{10,1... | collective-permute-start | bytes 3145736 | tf_op jit(solution)/shard_map/ppermute | solution.py:16
  536.5 20.1 %copy-start.13 = (f32[31,1024]{1,0:T(8,128)S(1)}, f32[31,1024]{1,0:T(8,128)}, u32[]{:S(2)}) copy-start(f32[31,1024]{1,0:T(8,128)} %reduce_sum.385) | copy-start | bytes 380932
  556.3 228.8 %all-reduce.3.cloned.1.call-start = ((), (), s32[]{:S(2)}) async-start(), calls=%async_computation.8 | async-start | bytes 4456448 | tf_op jit(solution)/shard_map/psum | solution.py:262
  691.9 4.2 copy-start.6
  693.4 2.9 copy-start.5
  693.4 2.9 copy-start.18
  693.4 2.9 copy-start.14
  696.3 4.9 copy-start.9
  696.3 4.9 copy-start.20
  696.4 95.0 %copy-start.1 = (s32[16,1]{0,1:T(1,128)S(1)}, s32[16,1]{0,1:T(1,128)}, u32[]{:S(2)}) copy-start(s32[16,1]{0,1:T(1,128)} %param.22) | copy-start | bytes 196
Sparse Core Ops, SparseCore 0:
  9.7 26.0 all-gather.11
  37.5 41.9 all-gather.13
  96.2 25.8 all-gather.15
  228.9 36.5 all-gather.17
  431.8 36.8 all-gather.19
  470.8 37.0 all-gather.21
  509.6 33.1 all-gather.23
  556.4 124.2 all-gather.25
  693.6 91.5 all-reduce.2

commit v4 on v3

--- a/solution.py
+++ b/solution.py
@@ -71,8 +71,6 @@
     head_count = HEADS
     tap_count = conv_kernel.shape[0]
     rim_width = (tap_count - 1) // 2
-    group_width = 4
-    group_count = head_count // group_width
     ids_whole = lax.all_gather(ids, "ctx", axis=1, tiled=True)
     table_whole = lax.all_gather(tables, "dp", axis=1, tiled=True)
     vocab = table_whole.shape[1]
@@ -122,19 +120,23 @@
     )
     query_all = projected[:, :, :model_width].reshape(recordings, frames_dev, head_count, head_size)
 
-    def forward_group(group):
-        first_head = group * group_width
-        queries = lax.dynamic_slice_in_dim(query_all, first_head, group_width, 2)
-        key_part = lax.dynamic_slice_in_dim(key_all, first_head, group_width, 3)
-        value_part = lax.dynamic_slice_in_dim(value_all, first_head, group_width, 3)
-        probs_low = probabilities(queries, key_part, listed, score_scale).astype(jnp.bfloat16)
-        value_flat = value_part.reshape(recordings, -1, group_width, head_size)
-        return jnp.einsum(
-            "rhqk,rkhd->rqhd", probs_low, value_flat, preferred_element_type=jnp.float32
-        ).astype(jnp.bfloat16)
-
-    mixed = lax.map(forward_group, jnp.arange(group_count, dtype=jnp.int32))
-    mixed = jnp.moveaxis(mixed, 0, 2).reshape(recordings * frames_dev, model_width)
+    key_flat = key_all.reshape(recordings, -1, head_count, head_size)
+    value_flat = value_all.reshape(recordings, -1, head_count, head_size)
+    visible = jnp.repeat(listed, frames_dev)
+    scores = jnp.where(
+        visible,
+        jnp.einsum("rqhd,rkhd->rhqk", query_all, key_flat, preferred_element_type=jnp.float32)
+        * score_scale,
+        NEGATIVE,
+    )
+    highest = jnp.max(scores, axis=3, keepdims=True)
+    weights = jnp.exp(scores - highest)
+    probs = weights / jnp.sum(weights, axis=3, keepdims=True)
+    probs_low = probs.astype(jnp.bfloat16)
+    mixed = jnp.einsum(
+        "rhqk,rkhd->rqhd", probs_low, value_flat, preferred_element_type=jnp.float32
+    ).astype(jnp.bfloat16)
+    mixed = mixed.reshape(recordings * frames_dev, model_width)
     projection = jnp.dot(mixed, weight_out, preferred_element_type=jnp.float32)
     middle = (features + projection).astype(jnp.bfloat16)
     middle_wide = middle.astype(jnp.float32)
@@ -187,41 +189,24 @@
     )
     grad_heads = grad_mixed.reshape(recordings, frames_dev, head_count, head_size)
 
-    def backward_group(group):
-        first_head = group * group_width
-        queries = lax.dynamic_slice_in_dim(query_all, first_head, group_width, 2)
-        key_part = lax.dynamic_slice_in_dim(key_all, first_head, group_width, 3)
-        value_part = lax.dynamic_slice_in_dim(value_all, first_head, group_width, 3)
-        grad_part = lax.dynamic_slice_in_dim(grad_heads, first_head, group_width, 2)
-        probs = probabilities(queries, key_part, listed, score_scale)
-        probs_low = probs.astype(jnp.bfloat16)
-        key_flat = key_part.reshape(recordings, -1, group_width, head_size)
-        value_flat = value_part.reshape(recordings, -1, group_width, head_size)
-        grad_probs = jnp.einsum(
-            "rqhd,rkhd->rhqk", grad_part, value_flat, preferred_element_type=jnp.float32
-        )
-        row_sum = jnp.sum(probs * grad_probs, axis=3, keepdims=True)
-        grad_scores = (probs * (grad_probs - row_sum) * score_scale).astype(jnp.bfloat16)
-        grad_query = jnp.einsum(
-            "rhqk,rkhd->rqhd", grad_scores, key_flat, preferred_element_type=jnp.float32
-        )
-        grad_key = jnp.einsum(
-            "rhqk,rqhd->rkhd", grad_scores, queries, preferred_element_type=jnp.float32
-        )
-        grad_value = jnp.einsum(
-            "rhqk,rqhd->rkhd", probs_low, grad_part, preferred_element_type=jnp.float32
-        )
-        return (grad_query, grad_key, grad_value)
-
-    grad_query, grad_key, grad_value = lax.map(
-        backward_group, jnp.arange(group_count, dtype=jnp.int32)
+    grad_probs = jnp.einsum(
+        "rqhd,rkhd->rhqk", grad_heads, value_flat, preferred_element_type=jnp.float32
+    )
+    row_sum = jnp.sum(probs * grad_probs, axis=3, keepdims=True)
+    grad_scores = (probs * (grad_probs - row_sum) * score_scale).astype(jnp.bfloat16)
+    grad_query = jnp.einsum(
+        "rhqk,rkhd->rqhd", grad_scores, key_flat, preferred_element_type=jnp.float32
+    )
+    grad_key = jnp.einsum(
+        "rhqk,rqhd->rkhd", grad_scores, query_all, preferred_element_type=jnp.float32
+    )
+    grad_value = jnp.einsum(
+        "rhqk,rqhd->rkhd", probs_low, grad_heads, preferred_element_type=jnp.float32
     )
     kernel_dp, grad_query = lax.optimization_barrier((kernel_dp, grad_query))
-    grad_query = jnp.moveaxis(grad_query, 0, 2).reshape(recordings * frames_dev, model_width)
-    grad_key = jnp.moveaxis(grad_key, 0, 2).reshape(recordings, seen_count, frames_dev, model_width)
-    grad_value = jnp.moveaxis(grad_value, 0, 2).reshape(
-        recordings, seen_count, frames_dev, model_width
-    )
+    grad_query = grad_query.reshape(recordings * frames_dev, model_width)
+    grad_key = grad_key.reshape(recordings, seen_count, frames_dev, model_width)
+    grad_value = grad_value.reshape(recordings, seen_count, frames_dev, model_width)
     pair_total = jnp.concatenate([grad_key[:, 0], grad_value[:, 0]], axis=2)
     for position, offset in enumerate(offsets):
         outgoing = jnp.concatenate(

time: 810 us -> 578 us (0.71)
  waiting for transfers between devices: 287 us -> 218 us
  local copies, waits for them, and re-layouts: 122 us -> 57.3 us
  matrix products: 212 us -> 157 us
  other arithmetic: 70.8 us -> 35.8 us
    dot_general x52 -> x5, matrix products: 153 us -> 90.4 us  [the longest x1 31.7 us: on_device(): jnp.einsum('rhqk,rqhd->rkhd', grad_scores, query_all, preferred_element_t...]
    all_gather x1, waiting for transfers between devices: 117 us -> 63.9 us  [on_device(): pair_rows = lax.all_gather(pair_part, 'dp', axis=0, tiled=True)]
    dynamic_slice x24 -> x0, local copies, waits for them, and re-layouts: 30.1 us -> none  [the longest x8 9.25 us: backward_group(): key_part = lax.dynamic_slice_in_dim(key_all, first_head, group_width, 3)]
    another operation x12 -> x2, local copies, waits for them, and re-layouts: 26.6 us -> 5.92 us
    convert_element_type x1, other arithmetic: 19.8 us -> 1.61 us  [on_device(): pair_total.reshape(recordings * frames_dev, 2 * model_width)]
    ppermute x6, waiting for transfers between devices: 77.7 us -> 61.4 us  [from_behind(): lax.ppermute(value, axis, [(source, source + steps) for source in range(f...]
    concatenate x3, other arithmetic: 16.5 us -> 0.23 us  [on_device(): jnp.concatenate([grad_key[:, position + 1], grad_value[:, position + 1]],...]
    sub x0 -> x1, matrix products: none -> 10.9 us  [on_device(): weights = jnp.exp(scores - highest)]
  transfers between devices with their start and end apart: 19 -> 19, of which waited for: 9 -> 11; matrix products, arithmetic and copies ran while one was open for 47% -> 42% of each run, Pallas kernels for 0% -> 0%
where the time goes in v4:
time: 578 us; the launch traced here: 567 us
  waiting for transfers between devices  218 us (38%)
  matrix products  157 us (27%)
  blocking collectives  57.8 us (10%)
  local copies, waits for them, and re-layouts  57.3 us (10%)
  other arithmetic  35.8 us (6%)
  starting transfers between devices  25.8 us (4%)
  between operations  15.5 us (3%)
    psum x1, waiting for transfers between devices, on_device(): lax.psum(jnp.concatenate([weight_rows, kernel_padded.reshape(-1, row_widt...  83.1 us
    all_gather x1, waiting for transfers between devices, on_device(): pair_rows = lax.all_gather(pair_part, 'dp', axis=0, tiled=True)  63.9 us
    ppermute x6, waiting for transfers between devices, from_behind(): lax.ppermute(value, axis, [(source, source + steps) for source in range(f...  61.4 us
    dot_general x1, matrix products, on_device(): jnp.einsum('rhqk,rqhd->rkhd', grad_scores, query_all, preferred_element_t...  31.7 us
    dot_general x1, matrix products, on_device(): jnp.einsum('rhqk,rkhd->rqhd', grad_scores, key_flat, preferred_element_ty...  30 us
    dot_general x8, matrix products, on_device(): lax.dot_general(table_whole[codebook], picks, (((0,), (0,)), ((), ())), p...  25.8 us
    all_gather x1, blocking collectives, on_device(): ids_whole = lax.all_gather(ids, 'ctx', axis=1, tiled=True)  24 us
    all_to_all x1, blocking collectives, on_device(): lax.all_to_all(transposed, 'ctx', split_axis=1, concat_axis=0, tiled=True)  19 us
  transfers between devices with their start and end apart: 19, of which 11 were waited for; matrix products, arithmetic and copies ran while one was open for 42% of the time, Pallas kernels for 0%

profile of v4, /device:TPU:0, one launch (start us, length us, event | category | flops | bytes accessed | tf_op | source)
XLA Modules:
  0.0 567.2 jit_solution(4686721731895928746)
XLA Ops:
  9.4 24.0 %all_gather.33 = s32[1,4096,8]{1,2,0:T(8,128)S(1)} all-gather(s32[1,256,8]{1,2,0:T(8,128)} %param.10), channel_id=1, replica_groups=mesh['dp'=8,'ctx'=16] {'ctx'}, dimensions={1}, use_global_device_ids=true | all-gather | bytes 139264 | tf_op jit(solution)/shard_map/all_gather | solution.py:74
  33.6 2.2 all-gather.12.cloned.1.call-done
  35.8 4.0 fusion.3
  39.8 3.1 fusion.39
  42.9 3.1 fusion.38
  46.0 3.1 fusion.37
  49.0 3.3 fusion.36
  52.3 3.1 fusion.35
  55.4 3.1 fusion.34
  58.5 3.1 fusion.40
  61.7 19.0 %all_to_all.4 = bf16[64,16,256]{2,0,1:T(8,128)(2,1)S(1)} all-to-all(bf16[64,16,256]{2,0,1:T(8,128)(2,1)S(1)} %bitcast.231), channel_id=1, replica_groups=mesh['dp'=8,'ctx'=16] {'ctx'}, dimensions={1} | all-to-all | bytes 1048576 | tf_op jit(solution)/shard_map/all_to_all | solution.py:87
  82.1 4.8 fusion.45
  87.0 1.5 slice_bitcast_fusion.24
  88.5 3.5 collective-permute-start
  91.9 3.3 collective-permute-start.1
  98.5 1.4 pad_add_fusion
  102.2 12.6 %collective-permute-done = bf16[1,256,2048]{2,1,0:T(8,128)(2,1)} collective-permute-done((bf16[1,256,2048]{2,1,0:T(8,128)(2,1)}, bf16[1,256,2048]{2,1,0:T(8,128)(2,1)}, u32[]{:S(2)}, u32[]{:S(2)}) %collective-permute-start) | collective-permute-done | bytes 1048608 | tf_op jit(solution)/shard_map/ppermute | solution.py:16
  114.8 20.3 %collective-permute-done.1 = bf16[1,256,2048]{2,1,0:T(8,128)(2,1)} collective-permute-done((bf16[1,256,2048]{2,1,0:T(8,128)(2,1)}, bf16[1,256,2048]{2,1,0:T(8,128)(2,1)}, u32[]{:S(2)}, u32[]{:S(2)}) %collective-permute-start.1) | collective-permute-done | bytes 1048608 | tf_op jit(solution)/shard_map/ppermute | solution.py:16
  135.1 5.1 collective-permute-done.2
  140.2 2.1 pad_maximum_fusion
  142.3 2.5 fusion.165
  144.8 3.0 copy.44
  147.8 2.7 reshape.465
  150.5 4.3 copy.42
  154.8 3.2 reshape.462
  158.0 10.9 %fusion.171 = (f32[16,256]{1,0:T(8,128)S(1)}, f32[16,256,1024]{2,1,0:T(8,128)}) fusion(pred[1024]{0:T(1024)(128)(4,1)S(1)} %reshape.463, bf16[256,16,64]{0,2,1:T(8,128)(2,1)} %bitcast.233, bf16[1024,16,64]{0,2,1:T(8,128)(2,1)} %reshape.465), kind=kOutput, calls=%fused_computation.282 | convolution fusion | flops 553649152 | bytes 19416064 | tf_op jit(solution)/shard_map/sub | solution.py:133
  169.0 9.4 %fusion.65 = bf16[16,64,256]{2,1,0:T(8,128)(2,1)} fusion(bf16[1024,16,64]{0,2,1:T(8,128)(2,1)S(1)} %reshape.462, f32[16,256,1024]{2,1,0:T(8,128)} %get-tuple-element.100, f32[16,256]{1,0:T(8,128)S(1)} %get-tuple-element.99), kind=kOutput, calls=%fused_computation.108 | convolution fusion | flops 545521664 | bytes 19415040 | tf_op jit(solution)/shard_map/rhqk,rkhd->rqhd/dot_general | solution.py:136
  178.4 2.6 fusion.79
  181.6 4.2 collective-permute-start.3
  185.8 1.5 collective-permute-start.4
  187.4 4.2 collective-permute-done.4
  191.8 5.4 fusion.76
  197.2 2.6 collective-permute-start.5
  201.0 2.4 fusion.111
  203.5 3.2 fusion.112
  206.6 3.1 stack.160
  209.7 14.7 %all-gather.2 = f32[8,31,1024]{2,1,0:T(8,128)} all-gather(f32[1,31,1024]{2,1,0:T(8,128)S(1)} %bitcast.232), channel_id=2, replica_groups=mesh['dp'=8,'ctx'=16] {'dp'}, dimensions={0}, use_global_device_ids=true | all-gather | bytes 1142784 | tf_op jit(solution)/shard_map/all_gather | solution.py:171
  225.9 5.6 fusion.81
  232.1 3.3 convolution_convert_fusion.1
  235.4 2.0 copy.45
  237.4 9.9 %fusion.172 = f32[16,256,1024]{2,1,0:T(8,128)} fusion(bf16[256,16,64]{0,2,1:T(8,128)(2,1)} %bitcast.227, bf16[1024,16,64]{0,2,1:T(8,128)(2,1)} %copy-done.2), kind=kOutput, calls=%fused_computation.283 | convolution fusion | flops 536870912 | bytes 19398656 | tf_op jit(solution)/shard_map/rqhd,rkhd->rhqk/dot_general | solution.py:192
  247.3 30.0 %fusion.61 = bf16[1,256,16,64]{1,3,2,0:T(8,128)(2,1)} fusion(bf16[1024,16,64]{0,2,1:T(8,128)(2,1)} %reshape.465, f32[16,256,1024]{2,1,0:T(8,128)} %fusion.172, f32[16,256,1024]{2,1,0:T(8,128)} %get-tuple-element.100, f32[16,256]{1,0:T(8,128)S(1)} %copy-done.24), kind=kOutput, calls=%fused_computation.102 | convolution fusion | flops 566236160 | bytes 36192256 | tf_op jit(solution)/shard_map/rhqk,rkhd->rqhd/dot_general | solution.py:197
  278.9 31.7 %fusion.49 = f32[1,1024,16,64]{1,3,2,0:T(8,128)} fusion(bf16[256,16,64]{0,2,1:T(8,128)(2,1)} %bitcast.234, f32[16,256,1024]{2,1,0:T(8,128)} %fusion.172, f32[16,256,1024]{2,1,0:T(8,128)} %get-tuple-element.100, f32[16,256]{1,0:T(8,128)S(1)} %copy-done.24), kind=kOutput, calls=%fused_computation.88 | convolution fusion | flops 566236160 | bytes 38289408 | tf_op jit(solution)/shard_map/rhqk,rqhd->rkhd/dot_general | solution.py:200
  310.6 5.6 reshape.472
  316.3 5.3 copy.46
  321.6 3.9 convert.26
  325.5 9.4 %fusion.46 = f32[1,1024,16,64]{1,3,2,0:T(8,128)} fusion(bf16[256,16,64]{0,2,1:T(8,128)(2,1)S(1)} %bitcast.228, f32[16,256,1024]{2,1,0:T(8,128)} %get-tuple-element.100, f32[16,256]{1,0:T(8,128)S(1)} %copy-done.24), kind=kOutput, calls=%fused_computation.87 | convolution fusion | flops 545259520 | bytes 21512192 | tf_op jit(solution)/shard_map/rhqk,rqhd->rkhd/dot_general | solution.py:203
  334.9 5.7 %reshape.473 = f32[1,4,256,1024]{2,1,3,0:T(4,128)} reshape(f32[1,1024,16,64]{1,3,2,0:T(8,128)} %fusion.46) | data formatting | bytes 8388608 | tf_op jit(solution)/shard_map/reshape | solution.py:209
  340.6 5.3 copy.47
  345.9 2.7 convert.27
  352.1 4.8 collective-permute-start.9
  356.9 1.7 slice_bitcast_fusion
  358.6 18.5 %collective-permute-done.7 = bf16[1,256,2048]{2,1,0:T(8,128)(2,1)S(1)} collective-permute-done((bf16[1,256,2048]{2,1,0:T(8,128)(2,1)S(1)}, bf16[1,256,2048]{2,1,0:T(8,128)(2,1)S(1)}, u32[]{:S(2)}, u32[]{:S(2)}) %collective-permute-start.7) | collective-permute-done | bytes 1048608 | tf_op jit(solution)/shard_map/ppermute | solution.py:16
  377.1 4.9 collective-permute-done.8
  382.1 1.6 fusion.54
  384.1 4.7 fusion.152
  389.0 3.9 fusion.149
  392.8 63.9 %all-gather.26.cloned.1.call-done = bf16[1,2048,2048]{2,1,0:T(8,128)(2,1)} async-done(((bf16[1,256,2048]{2,1,0:T(8,128)(2,1)}), bf16[1,2048,2048]{2,1,0:T(8,128)(2,1)}) %all-gather.26.cloned.1.call-update) | async-done | bytes 8388624 | tf_op jit(solution)/shard_map/all_gather | solution.py:232
  456.7 4.9 fusion.14
  461.7 1.5 pad_maximum_fusion.1
  464.7 5.1 fusion.146
  471.0 83.1 %all-reduce.3.cloned.1.call-done = f32[136,4096]{1,0:T(8,128)} async-done(((f32[136,4096]{1,0:T(8,128)}), f32[136,4096]{1,0:T(8,128)}) %all-reduce.3.cloned.1.call-update) | async-done | bytes 2228240 | tf_op jit(solution)/shard_map/psum | solution.py:247
  555.7 2.7 slice.678
  558.4 1.9 slice.679
  (118 shorter events, 22.4 us)
Async XLA Ops:
  7.2 89.3 %copy-start = (s32[16,1]{0,1:T(1,128)S(1)}, s32[16,1]{0,1:T(1,128)}, u32[]{:S(2)}) copy-start(s32[16,1]{0,1:T(1,128)} %param.18) | copy-start | bytes 196
  7.2 28.6 %all-gather.12.cloned.1.call-start = ((), (), s32[]{:S(2)}) async-start(), calls=%async_computation.1 | async-start | bytes 1179648 | tf_op jit(solution)/shard_map/all_gather | solution.py:75
  7.9 74.2 %all-gather.14.cloned.1.call-start = ((), (), s32[]{:S(2)}) async-start(), calls=%async_computation.2 | async-start | bytes 7077888 | tf_op jit(solution)/shard_map/all_gather | solution.py:90
  8.7 169.7 %all-gather.16.cloned.1.call-start = ((), (), s32[]{:S(2)}) async-start(), calls=%async_computation.3 | async-start | bytes 2359296 | tf_op jit(solution)/shard_map/all_gather | solution.py:91
  9.4 374.7 %all-gather.18.cloned.1.call-start = ((), (), s32[]{:S(2)}) async-start(), calls=%async_computation.4 | async-start | bytes 4718592 | tf_op jit(solution)/shard_map/all_gather | solution.py:225
  35.8 4.0 copy-start.22
  61.6 20.3 %copy-start.15 = (f32[1024]{0:T(1024)S(1)}, f32[1024]{0:T(1024)}, u32[]{:S(2)}) copy-start(f32[1024]{0:T(1024)} %param.14) | copy-start | bytes 12292
  81.3 0.6 copy-start.19
  82.1 4.9 copy-start.9
  82.1 15.7 %copy-start.21 = (s32[16,2]{0,1:T(2,128)S(1)}, s32[16,2]{0,1:T(2,128)}, u32[]{:S(2)}) copy-start(s32[16,2]{0,1:T(2,128)} %param.17) | copy-start | bytes 388
  82.1 17.9 %copy-start.13 = (f32[31,1024]{1,0:T(8,128)S(1)}, f32[31,1024]{1,0:T(8,128)}, u32[]{:S(2)}) copy-start(f32[31,1024]{1,0:T(8,128)} %param.16) | copy-start | bytes 380932
  87.0 1.5 copy-start.12
  88.5 26.4 %collective-permute-start = (bf16[1,256,2048]{2,1,0:T(8,128)(2,1)}, bf16[1,256,2048]{2,1,0:T(8,128)(2,1)}, u32[]{:S(2)}, u32[]{:S(2)}) collective-permute-start(bf16[1,256,2048]{2,1,0:T(8,128)(2,1)} %get-tuple-element.55), channel_id=1, source_target_pairs={{0,1},{1,2},{2,3},{3,4},{4,5},{5,6},{6,7},{7,8},{8,9},{9,10},{10,1... | collective-permute-start | bytes 3145736 | tf_op jit(solution)/shard_map/ppermute | solution.py:16
  91.9 43.2 %collective-permute-start.1 = (bf16[1,256,2048]{2,1,0:T(8,128)(2,1)}, bf16[1,256,2048]{2,1,0:T(8,128)(2,1)}, u32[]{:S(2)}, u32[]{:S(2)}) collective-permute-start(bf16[1,256,2048]{2,1,0:T(8,128)(2,1)} %get-tuple-element.55), channel_id=1, source_target_pairs={{0,2},{1,3},{2,4},{3,5},{4,6},{5,7},{6,8},{7,9},{8,10},{9,11},{10,... | collective-permute-start | bytes 3145736 | tf_op jit(solution)/shard_map/ppermute | solution.py:16
  95.2 45.0 %collective-permute-start.2 = (bf16[1,256,2048]{2,1,0:T(8,128)(2,1)}, bf16[1,256,2048]{2,1,0:T(8,128)(2,1)}, u32[]{:S(2)}, u32[]{:S(2)}) collective-permute-start(bf16[1,256,2048]{2,1,0:T(8,128)(2,1)} %get-tuple-element.55), channel_id=1, source_target_pairs={{1,0},{2,1},{3,2},{4,3},{5,4},{6,5},{7,6},{8,7},{9,8},{10,9},{11,1... | collective-permute-start | bytes 3145736 | tf_op jit(solution)/shard_map/ppermute | solution.py:16
  100.0 284.1 %all-gather.20.cloned.1.call-start = ((), (), s32[]{:S(2)}) async-start(), calls=%async_computation.5 | async-start | bytes 4718592 | tf_op jit(solution)/shard_map/all_gather | solution.py:227
  158.0 11.0 %copy-start.2 = (bf16[1024,16,64]{0,2,1:T(8,128)(2,1)}, bf16[1024,16,64]{0,2,1:T(8,128)(2,1)S(1)}, u32[]{:S(2)}) copy-start(bf16[1024,16,64]{0,2,1:T(8,128)(2,1)S(1)} %reshape.462) | copy-start | bytes 6291460
  169.0 9.4 %copy-start.23 = (f32[16,256]{1,0:T(8,128)}, f32[16,256]{1,0:T(8,128)S(1)}, u32[]{:S(2)}) copy-start(f32[16,256]{1,0:T(8,128)S(1)} %get-tuple-element.99) | copy-start | bytes 49156
  178.3 2.6 copy-start.14
  181.0 0.6 copy-start.17
  181.6 5.8 %collective-permute-start.3 = (bf16[1,15,1024]{2,1,0:T(8,128)(2,1)S(1)}, bf16[1,15,1024]{2,1,0:T(8,128)(2,1)S(1)}, u32[]{:S(2)}, u32[]{:S(2)}) collective-permute-start(bf16[1,15,1024]{2,1,0:T(8,128)(2,1)S(1)} %get-tuple-element.58), channel_id=1, source_target_pairs={{0,1},{1,2},{2,3},{3,4},{4,5},{5,6},{6,7},{7,8},{8,9},{9,10},{10,1... | collective-permute-start | bytes 92168 | tf_op jit(solution)/shard_map/ppermute | solution.py:24
  185.8 5.8 %collective-permute-start.4 = (bf16[1,15,1024]{2,1,0:T(8,128)(2,1)S(1)}, bf16[1,15,1024]{2,1,0:T(8,128)(2,1)S(1)}, u32[]{:S(2)}, u32[]{:S(2)}) collective-permute-start(bf16[1,15,1024]{2,1,0:T(8,128)(2,1)S(1)} %get-tuple-element.59), channel_id=1, source_target_pairs={{1,0},{2,1},{3,2},{4,3},{5,4},{6,5},{7,6},{8,7},{9,8},{10,9},{11,1... | collective-permute-start | bytes 92168 | tf_op jit(solution)/shard_map/ppermute | solution.py:27
  197.2 28.6 %collective-permute-start.5 = (bf16[1,15,1024]{2,1,0:T(8,128)(2,1)S(1)}, bf16[1,15,1024]{2,1,0:T(8,128)(2,1)S(1)}, u32[]{:S(2)}, u32[]{:S(2)}) collective-permute-start(bf16[1,15,1024]{2,1,0:T(8,128)(2,1)S(1)} %get-tuple-element.56), channel_id=1, source_target_pairs={{0,1},{1,2},{2,3},{3,4},{4,5},{5,6},{6,7},{7,8},{8,9},{9,10},{10,1... | collective-permute-start | bytes 92168 | tf_op jit(solution)/shard_map/ppermute | solution.py:24
  199.7 26.0 %collective-permute-start.6 = (bf16[1,15,1024]{2,1,0:T(8,128)(2,1)S(1)}, bf16[1,15,1024]{2,1,0:T(8,128)(2,1)S(1)}, u32[]{:S(2)}, u32[]{:S(2)}) collective-permute-start(bf16[1,15,1024]{2,1,0:T(8,128)(2,1)S(1)} %get-tuple-element.57), channel_id=1, source_target_pairs={{1,0},{2,1},{3,2},{4,3},{5,4},{6,5},{7,6},{8,7},{9,8},{10,9},{11,1... | collective-permute-start | bytes 92168 | tf_op jit(solution)/shard_map/ppermute | solution.py:27
  225.9 5.7 %copy-start.6 = (bf16[1,256,1024]{2,1,0:T(8,128)(2,1)S(1)}, bf16[1,256,1024]{2,1,0:T(8,128)(2,1)}, u32[]{:S(2)}) copy-start(bf16[1,256,1024]{2,1,0:T(8,128)(2,1)} %param.19) | copy-start | bytes 1572868
  225.9 5.7 %copy-start.18 = (f32[256]{0:T(256)S(1)}, f32[256]{0:T(256)}, u32[]{:S(2)}) copy-start(f32[256]{0:T(256)} %copy-done.17) | copy-start | bytes 3076
  232.1 15.2 %copy-start.4 = (bf16[256,1024]{1,0:T(8,128)(2,1)}, bf16[256,1024]{1,0:T(8,128)(2,1)S(1)}, u32[]{:S(2)}) copy-start(bf16[256,1024]{1,0:T(8,128)(2,1)S(1)} %fusion.75) | copy-start | bytes 1572868
  237.4 9.9 %copy-start.24 = (f32[16,256]{1,0:T(8,128)S(1)}, f32[16,256]{1,0:T(8,128)}, u32[]{:S(2)}) copy-start(f32[16,256]{1,0:T(8,128)} %copy-done.23) | copy-start | bytes 49156
  277.3 111.6 %all-gather.22.cloned.1.call-start = ((), (), s32[]{:S(2)}) async-start(), calls=%async_computation.6 | async-start | bytes 4718592 | tf_op jit(solution)/shard_map/all_gather | solution.py:184
  277.9 111.1 %all-gather.24.cloned.1.call-start = ((), (), s32[]{:S(2)}) async-start(), calls=%async_computation.7 | async-start | bytes 4718592 | tf_op jit(solution)/shard_map/all_gather | solution.py:186
  278.7 178.1 %all-gather.26.cloned.1.call-start = ((), (), s32[]{:S(2)}) async-start(), calls=%async_computation.9 | async-start | bytes 9437184 | tf_op jit(solution)/shard_map/all_gather | solution.py:232
  321.6 3.9 copy-start.7
  345.9 3.0 copy-start.3
  349.3 27.8 %collective-permute-start.7 = (bf16[1,256,2048]{2,1,0:T(8,128)(2,1)S(1)}, bf16[1,256,2048]{2,1,0:T(8,128)(2,1)S(1)}, u32[]{:S(2)}, u32[]{:S(2)}) collective-permute-start(bf16[1,256,2048]{2,1,0:T(8,128)(2,1)S(1)} %pad_maximum_fusion.2), channel_id=1, source_target_pairs={{1,0},{2,1},{3,2},{4,3},{5,4},{6,5},{7,6},{8,7},{9,8},{10,9},{11,1... | collective-permute-start | bytes 3145736 | tf_op jit(solution)/shard_map/ppermute | solution.py:16
  350.7 31.3 %collective-permute-start.8 = (bf16[1,256,2048]{2,1,0:T(8,128)(2,1)S(1)}, bf16[1,256,2048]{2,1,0:T(8,128)(2,1)S(1)}, u32[]{:S(2)}, u32[]{:S(2)}) collective-permute-start(bf16[1,256,2048]{2,1,0:T(8,128)(2,1)S(1)} %pad_maximum_fusion.3), channel_id=1, source_target_pairs={{2,0},{3,1},{4,2},{5,3},{6,4},{7,5},{8,6},{9,7},{10,8},{11,9},{12,... | collective-permute-start | bytes 3145736 | tf_op jit(solution)/shard_map/ppermute | solution.py:16
  352.1 30.0 %collective-permute-start.9 = (bf16[1,256,2048]{2,1,0:T(8,128)(2,1)S(1)}, bf16[1,256,2048]{2,1,0:T(8,128)(2,1)S(1)}, u32[]{:S(2)}, u32[]{:S(2)}) collective-permute-start(bf16[1,256,2048]{2,1,0:T(8,128)(2,1)S(1)} %pad_maximum_fusion.4), channel_id=1, source_target_pairs={{0,1},{1,2},{2,3},{3,4},{4,5},{5,6},{6,7},{7,8},{8,9},{9,10},{10,1... | collective-permute-start | bytes 3145736 | tf_op jit(solution)/shard_map/ppermute | solution.py:16
  383.7 170.4 %all-reduce.3.cloned.1.call-start = ((), (), s32[]{:S(2)}) async-start(), calls=%async_computation.8 | async-start | bytes 4456448 | tf_op jit(solution)/shard_map/psum | solution.py:247
  456.7 4.9 copy-start.10
  456.7 4.9 copy-start.11
  461.7 2.7 copy-start.8
  461.7 2.9 copy-start.16
  464.6 5.1 copy-start.5
  464.6 5.1 copy-start.20
  464.7 95.6 %copy-start.1 = (s32[16,1]{0,1:T(1,128)S(1)}, s32[16,1]{0,1:T(1,128)}, u32[]{:S(2)}) copy-start(s32[16,1]{0,1:T(1,128)} %param.18) | copy-start | bytes 196
Sparse Core Ops, SparseCore 0:
  9.7 26.0 all-gather.11
  37.5 41.9 all-gather.13
  81.2 25.2 all-gather.15
  108.1 32.8 all-gather.17
  277.5 37.3 all-gather.19
  316.9 37.0 all-gather.21
  355.8 33.1 all-gather.23
  391.3 65.4 all-gather.25
  463.4 90.6 all-reduce.2

commit v5 on v4

--- a/solution.py
+++ b/solution.py
@@ -137,6 +137,9 @@
         "rhqk,rkhd->rqhd", probs_low, value_flat, preferred_element_type=jnp.float32
     ).astype(jnp.bfloat16)
     mixed = mixed.reshape(recordings * frames_dev, model_width)
+    normed_all, mixed = lax.optimization_barrier(
+        (lax.all_gather(normed, "dp", axis=0, tiled=True), mixed)
+    )
     projection = jnp.dot(mixed, weight_out, preferred_element_type=jnp.float32)
     middle = (features + projection).astype(jnp.bfloat16)
     middle_wide = middle.astype(jnp.float32)
@@ -173,6 +176,9 @@
         upstream.reshape(-1, model_width)
         + norm_back(middle_wide, conv_inverse, conv_gain, grad_input.reshape(-1, model_width))
     ).astype(jnp.bfloat16)
+    mixed_all, grad_middle = lax.optimization_barrier(
+        (lax.all_gather(mixed, "dp", axis=0, tiled=True), grad_middle)
+    )
     contract_rows = (((0,), (0,)), ((), ()))
     contract_columns = (((1,), (1,)), ((), ()))
     grad_mixed = lax.dot_general(
@@ -180,13 +186,8 @@
     ).astype(jnp.bfloat16)
     dp_index = lax.axis_index("dp")
     shard_width = model_width // lax.axis_size("dp")
-    mixed_columns = lax.dynamic_slice_in_dim(
-        lax.all_gather(mixed, "dp", axis=0, tiled=True), dp_index * shard_width, shard_width, 1
-    )
+    mixed_columns = lax.dynamic_slice_in_dim(mixed_all, dp_index * shard_width, shard_width, 1)
     middle_rows = lax.all_gather(grad_middle, "dp", axis=0, tiled=True)
-    grad_wout = lax.dot_general(
-        mixed_columns, middle_rows, contract_rows, preferred_element_type=jnp.float32
-    )
     grad_heads = grad_mixed.reshape(recordings, frames_dev, head_count, head_size)
 
     grad_probs = jnp.einsum(
@@ -197,21 +198,42 @@
     grad_query = jnp.einsum(
         "rhqk,rkhd->rqhd", grad_scores, key_flat, preferred_element_type=jnp.float32
     )
-    grad_key = jnp.einsum(
-        "rhqk,rqhd->rkhd", grad_scores, query_all, preferred_element_type=jnp.float32
-    )
-    grad_value = jnp.einsum(
-        "rhqk,rqhd->rkhd", probs_low, grad_heads, preferred_element_type=jnp.float32
-    )
-    kernel_dp, grad_query = lax.optimization_barrier((kernel_dp, grad_query))
+    grad_key_own = jnp.einsum(
+        "rhqk,rqhd->rkhd", grad_scores[..., :frames_dev], query_all,
+        preferred_element_type=jnp.float32,
+    )
+    grad_value_own = jnp.einsum(
+        "rhqk,rqhd->rkhd", probs_low[..., :frames_dev], grad_heads,
+        preferred_element_type=jnp.float32,
+    )
+    grad_key_far = jnp.einsum(
+        "rhqk,rqhd->rkhd", grad_scores[..., frames_dev:], query_all,
+        preferred_element_type=jnp.float32,
+    ).astype(jnp.bfloat16)
+    grad_value_far = jnp.einsum(
+        "rhqk,rqhd->rkhd", probs_low[..., frames_dev:], grad_heads,
+        preferred_element_type=jnp.float32,
+    ).astype(jnp.bfloat16)
+    kernel_dp, middle_rows, grad_query = lax.optimization_barrier(
+        (kernel_dp, middle_rows, grad_query)
+    )
+    grad_wout = lax.dot_general(
+        mixed_columns, middle_rows, contract_rows, preferred_element_type=jnp.float32
+    )
     grad_query = grad_query.reshape(recordings * frames_dev, model_width)
-    grad_key = grad_key.reshape(recordings, seen_count, frames_dev, model_width)
-    grad_value = grad_value.reshape(recordings, seen_count, frames_dev, model_width)
-    pair_total = jnp.concatenate([grad_key[:, 0], grad_value[:, 0]], axis=2)
+    grad_key_far = grad_key_far.reshape(recordings, seen_count - 1, frames_dev, model_width)
+    grad_value_far = grad_value_far.reshape(recordings, seen_count - 1, frames_dev, model_width)
+    pair_total = jnp.concatenate(
+        [
+            grad_key_own.reshape(recordings, frames_dev, model_width),
+            grad_value_own.reshape(recordings, frames_dev, model_width),
+        ],
+        axis=2,
+    )
     for position, offset in enumerate(offsets):
         outgoing = jnp.concatenate(
-            [grad_key[:, position + 1], grad_value[:, position + 1]], axis=2
-        ).astype(jnp.bfloat16)
+            [grad_key_far[:, position], grad_value_far[:, position]], axis=2
+        )
         arrived = from_behind(outgoing, "ctx", offset)
         pair_total = pair_total + arrived.astype(jnp.float32)
     grad_projected = jnp.concatenate(
@@ -221,9 +243,7 @@
         ],
         axis=1,
     )
-    normed_columns = lax.dynamic_slice_in_dim(
-        lax.all_gather(normed, "dp", axis=0, tiled=True), dp_index * shard_width, shard_width, 1
-    )
+    normed_columns = lax.dynamic_slice_in_dim(normed_all, dp_index * shard_width, shard_width, 1)
     query_rows = lax.all_gather(grad_projected[:, :model_width], "dp", axis=0, tiled=True)
     grad_wq = lax.dot_general(
         normed_columns, query_rows, contract_rows, preferred_element_type=jnp.float32

time: 578 us -> 559 us (0.967)
  matrix products: 157 us -> 119 us
  local copies, waits for them, and re-layouts: 57.3 us -> 75.8 us
  waiting for transfers between devices: 218 us -> 206 us
  other arithmetic: 35.8 us -> 47.6 us
    dot_general x3 -> x4, matrix products: 51 us -> 17.1 us  [the longest x1 5.62 us: on_device(): jnp.einsum('rhqk,rqhd->rkhd', grad_scores[..., frames_dev:], query_all, p...]
    slice x0 -> x5, local copies, waits for them, and re-layouts: none -> 24.4 us  [the longest x4 17.4 us: on_device(): grad_key_far[:, position]]
    dot_general x1, matrix products: 30 us -> 7.47 us  [on_device(): jnp.einsum('rhqk,rkhd->rqhd', grad_scores, key_flat, preferred_element_ty...]
    sub x0 -> x1, matrix products: none -> 22.4 us  [on_device(): grad_probs - row_sum]
    ppermute x6, waiting for transfers between devices: 61.4 us -> 50 us  [from_behind(): lax.ppermute(value, axis, [(source, source + steps) for source in range(f...]
    unnamed x50 -> x37, local copies, waits for them, and re-layouts: 1.29 us -> 11.2 us
    convert_element_type x0 -> x1, other arithmetic: none -> 9.52 us  [on_device(): probs_low = probs.astype(jnp.bfloat16)]
    reshape x4, local copies, waits for them, and re-layouts: 21.9 us -> 14.7 us  [the longest x1 5.29 us: on_device(): grad_value_far.reshape(recordings, seen_count - 1, frames_dev, model_width)]
  transfers between devices with their start and end apart: 19 -> 19, of which waited for: 11 -> 14; matrix products, arithmetic and copies ran while one was open for 42% -> 42% of each run, Pallas kernels for 0% -> 0%
where the time goes in v5:
time: 559 us; the launch traced here: 549 us
  waiting for transfers between devices  206 us (37%)
  matrix products  119 us (21%)
  local copies, waits for them, and re-layouts  75.8 us (14%)
  blocking collectives  58.1 us (10%)
  other arithmetic  47.6 us (9%)
  starting transfers between devices  26.9 us (5%)
  between operations  15.5 us (3%)
    psum x1, waiting for transfers between devices, on_device(): lax.psum(jnp.concatenate([weight_rows, kernel_padded.reshape(-1, row_widt...  81.7 us
    all_gather x1, waiting for transfers between devices, on_device(): pair_rows = lax.all_gather(pair_part, 'dp', axis=0, tiled=True)  59.5 us
    ppermute x6, waiting for transfers between devices, from_behind(): lax.ppermute(value, axis, [(source, source + steps) for source in range(f...  50 us
    dot_general x8, matrix products, on_device(): lax.dot_general(table_whole[codebook], picks, (((0,), (0,)), ((), ())), p...  25.8 us
    all_gather x1, blocking collectives, on_device(): ids_whole = lax.all_gather(ids, 'ctx', axis=1, tiled=True)  24 us
    sub x1, matrix products, on_device(): grad_probs - row_sum  22.4 us
    all_to_all x1, blocking collectives, on_device(): lax.all_to_all(transposed, 'ctx', split_axis=1, concat_axis=0, tiled=True)  18.9 us
    slice x4, local copies, waits for them, and re-layouts, on_device(): grad_key_far[:, position]  17.4 us
  transfers between devices with their start and end apart: 19, of which 14 were waited for; matrix products, arithmetic and copies ran while one was open for 42% of the time, Pallas kernels for 0%

profile of v5, /device:TPU:0, one launch (start us, length us, event | category | flops | bytes accessed | tf_op | source)
XLA Modules:
  0.0 548.8 jit_solution(1213998814136609216)
XLA Ops:
  8.7 24.0 %all_gather.33 = s32[1,4096,8]{1,2,0:T(8,128)S(1)} all-gather(s32[1,256,8]{1,2,0:T(8,128)} %param.10), channel_id=1, replica_groups=mesh['dp'=8,'ctx'=16] {'ctx'}, dimensions={1}, use_global_device_ids=true | all-gather | bytes 139264 | tf_op jit(solution)/shard_map/all_gather | solution.py:74
  32.8 2.9 all-gather.12.cloned.1.call-done
  35.8 4.0 fusion.3
  39.8 3.1 fusion.35
  42.9 3.1 fusion.34
  46.0 3.1 fusion.33
  49.0 3.3 fusion.32
  52.3 3.1 fusion.31
  55.4 3.1 fusion.30
  58.5 3.1 fusion.36
  61.7 18.9 %all_to_all.4 = bf16[64,16,256]{2,0,1:T(8,128)(2,1)S(1)} all-to-all(bf16[64,16,256]{2,0,1:T(8,128)(2,1)S(1)} %bitcast.273), channel_id=1, replica_groups=mesh['dp'=8,'ctx'=16] {'ctx'}, dimensions={1} | all-to-all | bytes 1048576 | tf_op jit(solution)/shard_map/all_to_all | solution.py:87
  82.9 4.8 fusion.39
  90.0 3.7 collective-permute-start.1
  93.7 3.5 collective-permute-start
  104.1 12.6 %collective-permute-done.1 = bf16[1,256,2048]{2,1,0:T(8,128)(2,1)} collective-permute-done((bf16[1,256,2048]{2,1,0:T(8,128)(2,1)}, bf16[1,256,2048]{2,1,0:T(8,128)(2,1)}, u32[]{:S(2)}, u32[]{:S(2)}) %collective-permute-start.1) | collective-permute-done | bytes 1048608 | tf_op jit(solution)/shard_map/ppermute | solution.py:16
  116.6 21.3 %collective-permute-done = bf16[1,256,2048]{2,1,0:T(8,128)(2,1)} collective-permute-done((bf16[1,256,2048]{2,1,0:T(8,128)(2,1)}, bf16[1,256,2048]{2,1,0:T(8,128)(2,1)}, u32[]{:S(2)}, u32[]{:S(2)}) %collective-permute-start) | collective-permute-done | bytes 1048608 | tf_op jit(solution)/shard_map/ppermute | solution.py:16
  140.3 2.5 fusion.154
  142.8 3.0 copy.87
  145.8 2.8 reshape.373
  148.6 3.0 copy.85
  151.6 2.8 reshape.370
  154.4 10.3 %fusion.162 = (f32[16,256]{1,0:T(8,128)S(1)}, f32[16,256,1024]{2,1,0:T(8,128)}) fusion(pred[1024]{0:T(1024)(128)(4,1)S(1)} %reshape.371, bf16[256,16,64]{0,2,1:T(8,128)(2,1)} %bitcast.253, bf16[1024,16,64]{0,2,1:T(8,128)(2,1)} %reshape.373), kind=kOutput, calls=%fused_computation.280 | convolution fusion | flops 553649152 | bytes 19416064 | tf_op jit(solution)/shard_map/sub | solution.py:133
  164.7 9.4 %fusion.58 = bf16[16,64,256]{2,1,0:T(8,128)(2,1)} fusion(bf16[1024,16,64]{0,2,1:T(8,128)(2,1)S(1)} %copy-done.6, f32[16,256,1024]{2,1,0:T(8,128)} %get-tuple-element.110, f32[16,256]{1,0:T(8,128)S(1)} %get-tuple-element.109), kind=kOutput, calls=%fused_computation.116 | convolution fusion | flops 545521664 | bytes 19415040 | tf_op jit(solution)/shard_map/rhqk,rkhd->rqhd/dot_general | solution.py:136
  174.3 2.6 fusion.72
  177.1 4.3 collective-permute-start.3
  183.0 4.2 collective-permute-done.4
  187.4 6.2 %fusion.69 = (bf16[1,256,1024]{2,1,0:T(8,128)(2,1)S(1)}, f32[1,256,1024]{2,1,0:T(8,128)}) fusion(bf16[1,256,1024]{2,1,0:T(8,128)(2,1)} %param.19, f32[1,286,1024]{2,1,0:T(8,128)S(1)} %maximum_convert_fusion, f32[1024]{0:T(1024)S(1)} %bitcast.335, f32[1024]{0:T(1024)S(1)} %bitcast.337, f32[1024]{0:T(1024)S(1)} %bitcast.279, f32[1024]{0:T(1024)S(1)} %bitcast.281, ...), kind=kLoop, calls=%fused_computation.125 | loop fusion | flops 18612224 | bytes 34729984 | tf_op jit(solution)/shard_map/convert_element_type | solution.py:160
  193.6 3.2 collective-permute-start.5
  198.4 4.2 collective-permute-done.6
  202.8 5.6 %fusion.74 = (f32[256]{0:T(256)S(1)}, f32[256,1024]{1,0:T(8,128)S(1)}) fusion(bf16[256,1024]{1,0:T(8,128)(2,1)S(1)} %get-tuple-element.112, f32[1024]{0:T(1024)S(1)} %copy-done.10, f32[1,286,1024]{2,1,0:T(8,128)S(1)} %maximum_convert_fusion.1, f32[1024]{0:T(1024)S(1)} %bitcast.336, f32[1024]{0:T(1024)S(1)} %bitcast.338, f32[1024]{0:T(1024)S(1)} %bitcast.280, ...), kind=kLoop, calls=%fused_computation.130 | loop fusion | flops 17039104 | bytes 34210816 | tf_op jit(solution)/shard_map/reduce_sum | solution.py:37
  212.7 2.5 fusion.105
  215.4 15.1 %all-gather.2 = f32[8,31,1024]{2,1,0:T(8,128)S(1)} all-gather(f32[1,31,1024]{2,1,0:T(8,128)S(1)} %bitcast.274), channel_id=2, replica_groups=mesh['dp'=8,'ctx'=16] {'dp'}, dimensions={0}, use_global_device_ids=true | all-gather | bytes 1142784 | tf_op jit(solution)/shard_map/all_gather | solution.py:174
  230.6 2.5 convolution_convert_fusion.1
  233.4 22.4 %multiply_convert_fusion = bf16[16,256,1024]{2,1,0:T(8,128)(2,1)} fusion(bf16[256,16,64]{0,2,1:T(8,128)(2,1)S(1)} %bitcast.256, bf16[1024,16,64]{0,2,1:T(8,128)(2,1)} %reshape.370, f32[16,256,1024]{2,1,0:T(8,128)} %get-tuple-element.110, f32[16,256]{1,0:T(8,128)S(1)} %get-tuple-element.109), kind=kOutput, calls=%fused_computation.2 | convolution fusion | flops 1103107072 | bytes 27803648 | tf_op jit(solution)/shard_map/sub | solution.py:197
  255.7 7.5 %convolution_bitcast_fusion = bf16[1,256,16,64]{1,3,2,0:T(8,128)(2,1)} fusion(bf16[1024,16,64]{0,2,1:T(8,128)(2,1)} %reshape.373, bf16[16,256,1024]{2,1,0:T(8,128)(2,1)} %multiply_convert_fusion), kind=kOutput, calls=%fused_computation.110 | convolution fusion | flops 536870912 | bytes 11010048 | tf_op jit(solution)/shard_map/rhqk,rkhd->rqhd/dot_general | solution.py:198
  263.5 9.5 %convert_bitcast_fusion = bf16[1,16,256,1024]{3,2,1,0:T(8,128)(2,1)} fusion(f32[16,256,1024]{2,1,0:T(8,128)} %get-tuple-element.110, f32[16,256]{1,0:T(8,128)S(1)} %get-tuple-element.109), kind=kLoop, calls=%fused_computation.82 | loop fusion | flops 8388608 | bytes 25182208 | tf_op jit(solution)/shard_map/convert_element_type | solution.py:135
  273.1 5.6 %fusion.56 = bf16[1,768,16,64]{1,3,2,0:T(8,128)(2,1)} fusion(bf16[256,16,64]{0,2,1:T(8,128)(2,1)S(1)} %bitcast.254, bf16[1,16,256,1024]{3,2,1,0:T(8,128)(2,1)} %bitcast.251), kind=kOutput, calls=%fused_computation.109 | convolution fusion | flops 403439616 | bytes 8388608 | tf_op jit(solution)/shard_map/rhqk,rqhd->rkhd/dot_general | solution.py:209
  278.7 5.3 reshape.385
  283.9 5.4 fusion.55
  289.3 5.3 reshape.387
  294.6 7.0 %fusion.156 = (bf16[1,1,256,1024]{2,1,3,0:T(2,128)(2,1)}, bf16[1,1,256,1024]{2,1,3,0:T(2,128)(2,1)}, bf16[1,1,256,1024]{2,1,3,0:T(2,128)(2,1)}) fusion(bf16[1,3,256,1024]{2,1,3,0:T(4,128)(2,1)} %reshape.387), kind=kLoop, calls=%fused_computation.274 | loop fusion | bytes 3145728 | tf_op jit(solution)/shard_map/slice | solution.py:235
  301.6 2.3 copy.98
  303.9 3.5 copy.99
  307.5 3.5 copy.100
  311.0 6.9 %fusion.155 = (bf16[1,1,256,1024]{2,1,3,0:T(2,128)(2,1)}, bf16[1,1,256,1024]{2,1,3,0:T(2,128)(2,1)}, bf16[1,1,256,1024]{2,1,3,0:T(2,128)(2,1)}) fusion(bf16[1,3,256,1024]{2,1,3,0:T(4,128)(2,1)} %reshape.385), kind=kLoop, calls=%fused_computation.273 | loop fusion | bytes 3145728 | tf_op jit(solution)/shard_map/slice | solution.py:235
  317.9 3.5 copy.91
  321.4 3.5 copy.95
  324.9 3.5 copy.93
  328.4 2.3 pad_maximum_fusion.3
  334.3 4.8 collective-permute-start.9
  341.5 3.0 fusion.43
  344.5 2.6 copy.89
  347.1 3.0 fusion.42
  351.7 9.3 %collective-permute-done.8 = bf16[1,256,2048]{2,1,0:T(8,128)(2,1)} collective-permute-done((bf16[1,256,2048]{2,1,0:T(8,128)(2,1)}, bf16[1,256,2048]{2,1,0:T(8,128)(2,1)}, u32[]{:S(2)}, u32[]{:S(2)}) %collective-permute-start.8) | collective-permute-done | bytes 1048608 | tf_op jit(solution)/shard_map/ppermute | solution.py:16
  361.4 6.2 %collective-permute-done.7 = bf16[1,256,2048]{2,1,0:T(8,128)(2,1)} collective-permute-done((bf16[1,256,2048]{2,1,0:T(8,128)(2,1)}, bf16[1,256,2048]{2,1,0:T(8,128)(2,1)}, u32[]{:S(2)}, u32[]{:S(2)}) %collective-permute-start.7) | collective-permute-done | bytes 1048608 | tf_op jit(solution)/shard_map/ppermute | solution.py:16
  367.6 3.8 fusion.46
  371.9 3.1 fusion.142
  375.0 3.9 fusion.145
  378.9 59.5 %all-gather.26.cloned.1.call-done = bf16[1,2048,2048]{2,1,0:T(8,128)(2,1)} async-done(((bf16[1,256,2048]{2,1,0:T(8,128)(2,1)}), bf16[1,2048,2048]{2,1,0:T(8,128)(2,1)}) %all-gather.26.cloned.1.call-update) | async-done | bytes 8388624 | tf_op jit(solution)/shard_map/all_gather | solution.py:252
  438.4 4.9 fusion.14
  444.9 2.4 fusion.71
  447.5 5.1 fusion.139
  453.8 81.7 %all-reduce.3.cloned.1.call-done = f32[136,4096]{1,0:T(8,128)} async-done(((f32[136,4096]{1,0:T(8,128)}), f32[136,4096]{1,0:T(8,128)}) %all-reduce.3.cloned.1.call-update) | async-done | bytes 2228240 | tf_op jit(solution)/shard_map/psum | solution.py:267
  539.0 2.7 slice.682
  (109 shorter events, 38.3 us)
Async XLA Ops:
  7.2 91.4 %copy-start = (s32[16,1]{0,1:T(1,128)S(1)}, s32[16,1]{0,1:T(1,128)}, u32[]{:S(2)}) copy-start(s32[16,1]{0,1:T(1,128)} %param.18) | copy-start | bytes 196
  7.2 28.6 %all-gather.12.cloned.1.call-start = ((), (), s32[]{:S(2)}) async-start(), calls=%async_computation.1 | async-start | bytes 1179648 | tf_op jit(solution)/shard_map/all_gather | solution.py:75
  7.9 74.9 %all-gather.16.cloned.1.call-start = ((), (), s32[]{:S(2)}) async-start(), calls=%async_computation.3 | async-start | bytes 7077888 | tf_op jit(solution)/shard_map/all_gather | solution.py:90
  8.7 165.5 %all-gather.14.cloned.1.call-start = ((), (), s32[]{:S(2)}) async-start(), calls=%async_computation.2 | async-start | bytes 4718592 | tf_op jit(solution)/shard_map/all_gather | solution.py:141
  35.8 4.0 copy-start.16
  61.6 20.2 %copy-start.11 = (f32[1024]{0:T(1024)S(1)}, f32[1024]{0:T(1024)}, u32[]{:S(2)}) copy-start(f32[1024]{0:T(1024)} %param.14) | copy-start | bytes 12292
  81.2 0.6 copy-start.13
  82.8 17.0 %copy-start.15 = (s32[16,2]{0,1:T(2,128)S(1)}, s32[16,2]{0,1:T(2,128)}, u32[]{:S(2)}) copy-start(s32[16,2]{0,1:T(2,128)} %param.17) | copy-start | bytes 388
  82.8 91.5 %all-gather.18.cloned.1.call-start = ((), (), s32[]{:S(2)}) async-start(), calls=%async_computation.4 | async-start | bytes 2359296 | tf_op jit(solution)/shard_map/all_gather | solution.py:91
  87.6 1.1 copy-start.8
  90.0 26.6 %collective-permute-start.1 = (bf16[1,256,2048]{2,1,0:T(8,128)(2,1)}, bf16[1,256,2048]{2,1,0:T(8,128)(2,1)}, u32[]{:S(2)}, u32[]{:S(2)}) collective-permute-start(bf16[1,256,2048]{2,1,0:T(8,128)(2,1)} %get-tuple-element.65), channel_id=1, source_target_pairs={{0,2},{1,3},{2,4},{3,5},{4,6},{5,7},{6,8},{7,9},{8,10},{9,11},{10,... | collective-permute-start | bytes 3145736 | tf_op jit(solution)/shard_map/ppermute | solution.py:16
  93.7 44.2 %collective-permute-start = (bf16[1,256,2048]{2,1,0:T(8,128)(2,1)}, bf16[1,256,2048]{2,1,0:T(8,128)(2,1)}, u32[]{:S(2)}, u32[]{:S(2)}) collective-permute-start(bf16[1,256,2048]{2,1,0:T(8,128)(2,1)} %get-tuple-element.65), channel_id=1, source_target_pairs={{0,1},{1,2},{2,3},{3,4},{4,5},{5,6},{6,7},{7,8},{8,9},{9,10},{10,1... | collective-permute-start | bytes 3145736 | tf_op jit(solution)/shard_map/ppermute | solution.py:16
  97.2 40.9 %collective-permute-start.2 = (bf16[1,256,2048]{2,1,0:T(8,128)(2,1)}, bf16[1,256,2048]{2,1,0:T(8,128)(2,1)}, u32[]{:S(2)}, u32[]{:S(2)}) collective-permute-start(bf16[1,256,2048]{2,1,0:T(8,128)(2,1)} %get-tuple-element.65), channel_id=1, source_target_pairs={{1,0},{2,1},{3,2},{4,3},{5,4},{6,5},{7,6},{8,7},{9,8},{10,9},{11,1... | collective-permute-start | bytes 3145736 | tf_op jit(solution)/shard_map/ppermute | solution.py:16
  98.5 112.3 %all-gather.20.cloned.1.call-start = ((), (), s32[]{:S(2)}) async-start(), calls=%async_computation.5 | async-start | bytes 4718592 | tf_op jit(solution)/shard_map/all_gather | solution.py:180
  154.4 10.3 %copy-start.6 = (bf16[1024,16,64]{0,2,1:T(8,128)(2,1)S(1)}, bf16[1024,16,64]{0,2,1:T(8,128)(2,1)}, u32[]{:S(2)}) copy-start(bf16[1024,16,64]{0,2,1:T(8,128)(2,1)} %reshape.370) | copy-start | bytes 6291460
  164.7 9.5 %copy-start.9 = (f32[31,1024]{1,0:T(8,128)S(1)}, f32[31,1024]{1,0:T(8,128)}, u32[]{:S(2)}) copy-start(f32[31,1024]{1,0:T(8,128)} %param.16) | copy-start | bytes 380932
  174.1 2.8 copy-start.10
  174.1 89.1 %all-gather.22.cloned.1.call-start = ((), (), s32[]{:S(2)}) async-start(), calls=%async_computation.6 | async-start | bytes 4718592 | tf_op jit(solution)/shard_map/all_gather | solution.py:190
  177.1 5.8 %collective-permute-start.3 = (bf16[1,15,1024]{2,1,0:T(8,128)(2,1)S(1)}, bf16[1,15,1024]{2,1,0:T(8,128)(2,1)S(1)}, u32[]{:S(2)}, u32[]{:S(2)}) collective-permute-start(bf16[1,15,1024]{2,1,0:T(8,128)(2,1)S(1)} %get-tuple-element.68), channel_id=1, source_target_pairs={{0,1},{1,2},{2,3},{3,4},{4,5},{5,6},{6,7},{7,8},{8,9},{9,10},{10,1... | collective-permute-start | bytes 92168 | tf_op jit(solution)/shard_map/ppermute | solution.py:24
  181.4 5.8 %collective-permute-start.4 = (bf16[1,15,1024]{2,1,0:T(8,128)(2,1)S(1)}, bf16[1,15,1024]{2,1,0:T(8,128)(2,1)S(1)}, u32[]{:S(2)}, u32[]{:S(2)}) collective-permute-start(bf16[1,15,1024]{2,1,0:T(8,128)(2,1)S(1)} %get-tuple-element.69), channel_id=1, source_target_pairs={{1,0},{2,1},{3,2},{4,3},{5,4},{6,5},{7,6},{8,7},{9,8},{10,9},{11,1... | collective-permute-start | bytes 92168 | tf_op jit(solution)/shard_map/ppermute | solution.py:27
  193.6 4.8 collective-permute-start.5
  196.9 5.8 %collective-permute-start.6 = (bf16[1,15,1024]{2,1,0:T(8,128)(2,1)S(1)}, bf16[1,15,1024]{2,1,0:T(8,128)(2,1)S(1)}, u32[]{:S(2)}, u32[]{:S(2)}) collective-permute-start(bf16[1,15,1024]{2,1,0:T(8,128)(2,1)S(1)} %get-tuple-element.67), channel_id=1, source_target_pairs={{1,0},{2,1},{3,2},{4,3},{5,4},{6,5},{7,6},{8,7},{9,8},{10,9},{11,1... | collective-permute-start | bytes 92168 | tf_op jit(solution)/shard_map/ppermute | solution.py:27
  202.8 5.7 %copy-start.5 = (bf16[1,256,1024]{2,1,0:T(8,128)(2,1)S(1)}, bf16[1,256,1024]{2,1,0:T(8,128)(2,1)}, u32[]{:S(2)}) copy-start(bf16[1,256,1024]{2,1,0:T(8,128)(2,1)} %param.19) | copy-start | bytes 1572868
  210.8 164.2 %all-gather.24.cloned.1.call-start = ((), (), s32[]{:S(2)}) async-start(), calls=%async_computation.7 | async-start | bytes 4718592 | tf_op jit(solution)/shard_map/all_gather | solution.py:247
  263.2 9.8 %copy-start.2 = (bf16[1,256,1024]{1,2,0:T(8,128)(2,1)S(1)}, bf16[1,256,1024]{1,2,0:T(8,128)(2,1)}, u32[]{:S(2)}) copy-start(bf16[1,256,1024]{1,2,0:T(8,128)(2,1)} %copy.86) | copy-start | bytes 1572868
  263.3 175.2 %all-gather.26.cloned.1.call-start = ((), (), s32[]{:S(2)}) async-start(), calls=%async_computation.9 | async-start | bytes 9437184 | tf_op jit(solution)/shard_map/all_gather | solution.py:252
  328.4 10.7 %copy-start.7 = (bf16[1,1,256,1024]{3,2,1,0:T(8,128)(2,1)S(1)}, bf16[1,1,256,1024]{3,2,1,0:T(8,128)(2,1)}, u32[]{:S(2)}) copy-start(bf16[1,1,256,1024]{3,2,1,0:T(8,128)(2,1)} %copy.91) | copy-start | bytes 1572868
  330.8 30.2 %collective-permute-start.8 = (bf16[1,256,2048]{2,1,0:T(8,128)(2,1)}, bf16[1,256,2048]{2,1,0:T(8,128)(2,1)}, u32[]{:S(2)}, u32[]{:S(2)}) collective-permute-start(bf16[1,256,2048]{2,1,0:T(8,128)(2,1)} %pad_maximum_fusion.3), channel_id=1, source_target_pairs={{2,0},{3,1},{4,2},{5,3},{6,4},{7,5},{8,6},{9,7},{10,8},{11,9},{12,... | collective-permute-start | bytes 3145736 | tf_op jit(solution)/shard_map/ppermute | solution.py:16
  334.3 27.0 %collective-permute-start.9 = (bf16[1,256,2048]{2,1,0:T(8,128)(2,1)}, bf16[1,256,2048]{2,1,0:T(8,128)(2,1)}, u32[]{:S(2)}, u32[]{:S(2)}) collective-permute-start(bf16[1,256,2048]{2,1,0:T(8,128)(2,1)} %pad_maximum_fusion.4), channel_id=1, source_target_pairs={{0,1},{1,2},{2,3},{3,4},{4,5},{5,6},{6,7},{7,8},{8,9},{9,10},{10,1... | collective-permute-start | bytes 3145736 | tf_op jit(solution)/shard_map/ppermute | solution.py:16
  340.2 27.4 %collective-permute-start.7 = (bf16[1,256,2048]{2,1,0:T(8,128)(2,1)}, bf16[1,256,2048]{2,1,0:T(8,128)(2,1)}, u32[]{:S(2)}, u32[]{:S(2)}) collective-permute-start(bf16[1,256,2048]{2,1,0:T(8,128)(2,1)} %pad_maximum_fusion.2), channel_id=1, source_target_pairs={{1,0},{2,1},{3,2},{4,3},{5,4},{6,5},{7,6},{8,7},{9,8},{10,9},{11,1... | collective-permute-start | bytes 3145736 | tf_op jit(solution)/shard_map/ppermute | solution.py:16
  371.4 164.1 %all-reduce.3.cloned.1.call-start = ((), (), s32[]{:S(2)}) async-start(), calls=%async_computation.8 | async-start | bytes 4456448 | tf_op jit(solution)/shard_map/psum | solution.py:267
  443.3 3.9 copy-start.4
  443.3 4.1 copy-start.12
  447.5 5.1 copy-start.3
  447.5 5.1 copy-start.14
  447.5 94.2 %copy-start.1 = (s32[16,1]{0,1:T(1,128)S(1)}, s32[16,1]{0,1:T(1,128)}, u32[]{:S(2)}) copy-start(s32[16,1]{0,1:T(1,128)} %param.18) | copy-start | bytes 196
Sparse Core Ops, SparseCore 0:
  9.7 26.0 all-gather.11
  37.5 41.9 all-gather.15
  82.9 31.1 all-gather.13
  115.6 25.1 all-gather.17
  174.3 36.4 all-gather.19
  212.9 33.8 all-gather.21
  263.4 37.8 all-gather.23
  371.6 66.8 all-gather.25
  445.0 90.5 all-reduce.2

commit v6 on v5

--- a/solution.py
+++ b/solution.py
@@ -264,8 +264,9 @@
     kernel_padded = jnp.pad(
         kernel_dp, ((0, (-tap_count * model_width) % row_width // model_width), (0, 0))
     )
-    summed = lax.psum(
-        jnp.concatenate([weight_rows, kernel_padded.reshape(-1, row_width)], axis=0), "ctx"
+    packed = jnp.concatenate([weight_rows, kernel_padded.reshape(-1, row_width)], axis=0)
+    summed = lax.all_gather(
+        lax.psum_scatter(packed, "ctx", scatter_dimension=1, tiled=True), "ctx", axis=1, tiled=True
     )
     shard_rows = weight_rows.shape[0]
     qkv_width = grad_wq.shape[1] + grad_wkv.shape[1]

time: 559 us -> 593 us (1.061)
  waiting for transfers between devices: 206 us -> 239 us
    psum x1 -> x0, waiting for transfers between devices: 81.7 us -> none  [on_device(): lax.psum(jnp.concatenate([weight_rows, kernel_padded.reshape(-1, row_widt...]
    reduce_scatter x0 -> x1, waiting for transfers between devices: none -> 74.9 us  [on_device(): lax.psum_scatter(packed, 'ctx', scatter_dimension=1, tiled=True)]
    all_gather x0 -> x1, waiting for transfers between devices: none -> 40.5 us  [on_device(): lax.all_gather(lax.psum_scatter(packed, 'ctx', scatter_dimension=1, tiled...]
  transfers between devices with their start and end apart: 19 -> 20, of which waited for: 14 -> 15; matrix products, arithmetic and copies ran while one was open for 42% -> 39% of each run, Pallas kernels for 0% -> 0%
where the time goes in v6:
time: 593 us; the launch traced here: 583 us
  waiting for transfers between devices  239 us (40%)
  matrix products  119 us (20%)
  local copies, waits for them, and re-layouts  75.8 us (13%)
  blocking collectives  58.1 us (10%)
  other arithmetic  47.6 us (8%)
  starting transfers between devices  27 us (5%)
  between operations  15.8 us (3%)
    reduce_scatter x1, waiting for transfers between devices, on_device(): lax.psum_scatter(packed, 'ctx', scatter_dimension=1, tiled=True)  74.9 us
    all_gather x1, waiting for transfers between devices, on_device(): pair_rows = lax.all_gather(pair_part, 'dp', axis=0, tiled=True)  59.5 us
    ppermute x6, waiting for transfers between devices, from_behind(): lax.ppermute(value, axis, [(source, source + steps) for source in range(f...  50 us
    all_gather x1, waiting for transfers between devices, on_device(): lax.all_gather(lax.psum_scatter(packed, 'ctx', scatter_dimension=1, tiled...  40.5 us
    dot_general x8, matrix products, on_device(): lax.dot_general(table_whole[codebook], picks, (((0,), (0,)), ((), ())), p...  25.8 us
    all_gather x1, blocking collectives, on_device(): ids_whole = lax.all_gather(ids, 'ctx', axis=1, tiled=True)  24 us
    sub x1, matrix products, on_device(): grad_probs - row_sum  22.4 us
    all_to_all x1, blocking collectives, on_device(): lax.all_to_all(transposed, 'ctx', split_axis=1, concat_axis=0, tiled=True)  18.9 us
  transfers between devices with their start and end apart: 20, of which 15 were waited for; matrix products, arithmetic and copies ran while one was open for 39% of the time, Pallas kernels for 0%

profile of v6, /device:TPU:0, one launch (start us, length us, event | category | flops | bytes accessed | tf_op | source)
XLA Modules:
  0.0 582.8 jit_solution(1800088134292963125)
XLA Ops:
  8.7 24.0 %all_gather.36 = s32[1,4096,8]{1,2,0:T(8,128)S(1)} all-gather(s32[1,256,8]{1,2,0:T(8,128)} %param.10), channel_id=1, replica_groups=mesh['dp'=8,'ctx'=16] {'ctx'}, dimensions={1}, use_global_device_ids=true | all-gather | bytes 139264 | tf_op jit(solution)/shard_map/all_gather | solution.py:74
  32.8 2.9 all-gather.13.cloned.1.call-done
  35.8 4.0 fusion.3
  39.8 3.1 fusion.35
  42.9 3.1 fusion.34
  46.0 3.1 fusion.33
  49.0 3.3 fusion.32
  52.3 3.1 fusion.31
  55.4 3.1 fusion.30
  58.5 3.1 fusion.36
  61.7 18.9 %all_to_all.4 = bf16[64,16,256]{2,0,1:T(8,128)(2,1)S(1)} all-to-all(bf16[64,16,256]{2,0,1:T(8,128)(2,1)S(1)} %bitcast.273), channel_id=1, replica_groups=mesh['dp'=8,'ctx'=16] {'ctx'}, dimensions={1} | all-to-all | bytes 1048576 | tf_op jit(solution)/shard_map/all_to_all | solution.py:87
  82.9 4.8 fusion.39
  90.0 3.7 collective-permute-start.1
  93.7 3.5 collective-permute-start
  104.1 12.6 %collective-permute-done.1 = bf16[1,256,2048]{2,1,0:T(8,128)(2,1)} collective-permute-done((bf16[1,256,2048]{2,1,0:T(8,128)(2,1)}, bf16[1,256,2048]{2,1,0:T(8,128)(2,1)}, u32[]{:S(2)}, u32[]{:S(2)}) %collective-permute-start.1) | collective-permute-done | bytes 1048608 | tf_op jit(solution)/shard_map/ppermute | solution.py:16
  116.6 21.3 %collective-permute-done = bf16[1,256,2048]{2,1,0:T(8,128)(2,1)} collective-permute-done((bf16[1,256,2048]{2,1,0:T(8,128)(2,1)}, bf16[1,256,2048]{2,1,0:T(8,128)(2,1)}, u32[]{:S(2)}, u32[]{:S(2)}) %collective-permute-start) | collective-permute-done | bytes 1048608 | tf_op jit(solution)/shard_map/ppermute | solution.py:16
  140.3 2.5 fusion.154
  142.8 3.0 copy.87
  145.8 2.8 reshape.373
  148.6 3.0 copy.85
  151.6 2.8 reshape.370
  154.4 10.3 %fusion.162 = (f32[16,256]{1,0:T(8,128)S(1)}, f32[16,256,1024]{2,1,0:T(8,128)}) fusion(pred[1024]{0:T(1024)(128)(4,1)S(1)} %reshape.371, bf16[256,16,64]{0,2,1:T(8,128)(2,1)} %bitcast.253, bf16[1024,16,64]{0,2,1:T(8,128)(2,1)} %reshape.373), kind=kOutput, calls=%fused_computation.280 | convolution fusion | flops 553649152 | bytes 19416064 | tf_op jit(solution)/shard_map/sub | solution.py:133
  164.7 9.4 %fusion.58 = bf16[16,64,256]{2,1,0:T(8,128)(2,1)} fusion(bf16[1024,16,64]{0,2,1:T(8,128)(2,1)S(1)} %copy-done.6, f32[16,256,1024]{2,1,0:T(8,128)} %get-tuple-element.110, f32[16,256]{1,0:T(8,128)S(1)} %get-tuple-element.109), kind=kOutput, calls=%fused_computation.116 | convolution fusion | flops 545521664 | bytes 19415040 | tf_op jit(solution)/shard_map/rhqk,rkhd->rqhd/dot_general | solution.py:136
  174.3 2.6 fusion.72
  177.1 4.3 collective-permute-start.3
  183.0 4.2 collective-permute-done.4
  187.4 6.2 %fusion.69 = (bf16[1,256,1024]{2,1,0:T(8,128)(2,1)S(1)}, f32[1,256,1024]{2,1,0:T(8,128)}) fusion(bf16[1,256,1024]{2,1,0:T(8,128)(2,1)} %param.19, f32[1,286,1024]{2,1,0:T(8,128)S(1)} %maximum_convert_fusion, f32[1024]{0:T(1024)S(1)} %bitcast.335, f32[1024]{0:T(1024)S(1)} %bitcast.337, f32[1024]{0:T(1024)S(1)} %bitcast.279, f32[1024]{0:T(1024)S(1)} %bitcast.281, ...), kind=kLoop, calls=%fused_computation.125 | loop fusion | flops 18612224 | bytes 34729984 | tf_op jit(solution)/shard_map/convert_element_type | solution.py:160
  193.6 3.2 collective-permute-start.5
  198.4 4.2 collective-permute-done.6
  202.8 5.6 fusion.74
  212.7 2.5 fusion.105
  215.4 15.1 %all-gather.2 = f32[8,31,1024]{2,1,0:T(8,128)S(1)} all-gather(f32[1,31,1024]{2,1,0:T(8,128)S(1)} %bitcast.274), channel_id=2, replica_groups=mesh['dp'=8,'ctx'=16] {'dp'}, dimensions={0}, use_global_device_ids=true | all-gather | bytes 1142784 | tf_op jit(solution)/shard_map/all_gather | solution.py:174
  230.6 2.5 convolution_convert_fusion.1
  233.4 22.4 %multiply_convert_fusion = bf16[16,256,1024]{2,1,0:T(8,128)(2,1)} fusion(bf16[256,16,64]{0,2,1:T(8,128)(2,1)S(1)} %bitcast.256, bf16[1024,16,64]{0,2,1:T(8,128)(2,1)} %reshape.370, f32[16,256,1024]{2,1,0:T(8,128)} %get-tuple-element.110, f32[16,256]{1,0:T(8,128)S(1)} %get-tuple-element.109), kind=kOutput, calls=%fused_computation.2 | convolution fusion | flops 1103107072 | bytes 27803648 | tf_op jit(solution)/shard_map/sub | solution.py:197
  255.7 7.5 %convolution_bitcast_fusion = bf16[1,256,16,64]{1,3,2,0:T(8,128)(2,1)} fusion(bf16[1024,16,64]{0,2,1:T(8,128)(2,1)} %reshape.373, bf16[16,256,1024]{2,1,0:T(8,128)(2,1)} %multiply_convert_fusion), kind=kOutput, calls=%fused_computation.110 | convolution fusion | flops 536870912 | bytes 11010048 | tf_op jit(solution)/shard_map/rhqk,rkhd->rqhd/dot_general | solution.py:198
  263.5 9.5 %convert_bitcast_fusion = bf16[1,16,256,1024]{3,2,1,0:T(8,128)(2,1)} fusion(f32[16,256,1024]{2,1,0:T(8,128)} %get-tuple-element.110, f32[16,256]{1,0:T(8,128)S(1)} %get-tuple-element.109), kind=kLoop, calls=%fused_computation.82 | loop fusion | flops 8388608 | bytes 25182208 | tf_op jit(solution)/shard_map/convert_element_type | solution.py:135
  273.1 5.6 fusion.56
  278.7 5.3 reshape.385
  283.9 5.4 fusion.55
  289.3 5.3 reshape.387
  294.6 7.0 %fusion.156 = (bf16[1,1,256,1024]{2,1,3,0:T(2,128)(2,1)}, bf16[1,1,256,1024]{2,1,3,0:T(2,128)(2,1)}, bf16[1,1,256,1024]{2,1,3,0:T(2,128)(2,1)}) fusion(bf16[1,3,256,1024]{2,1,3,0:T(4,128)(2,1)} %reshape.387), kind=kLoop, calls=%fused_computation.274 | loop fusion | bytes 3145728 | tf_op jit(solution)/shard_map/slice | solution.py:235
  301.6 2.3 copy.98
  303.9 3.5 copy.99
  307.5 3.5 copy.100
  311.0 6.9 %fusion.155 = (bf16[1,1,256,1024]{2,1,3,0:T(2,128)(2,1)}, bf16[1,1,256,1024]{2,1,3,0:T(2,128)(2,1)}, bf16[1,1,256,1024]{2,1,3,0:T(2,128)(2,1)}) fusion(bf16[1,3,256,1024]{2,1,3,0:T(4,128)(2,1)} %reshape.385), kind=kLoop, calls=%fused_computation.273 | loop fusion | bytes 3145728 | tf_op jit(solution)/shard_map/slice | solution.py:235
  317.9 3.5 copy.91
  321.4 3.5 copy.95
  324.9 3.5 copy.93
  334.3 4.8 collective-permute-start.9
  341.5 3.0 fusion.43
  344.5 2.6 copy.89
  347.1 3.0 fusion.42
  351.7 9.3 %collective-permute-done.8 = bf16[1,256,2048]{2,1,0:T(8,128)(2,1)} collective-permute-done((bf16[1,256,2048]{2,1,0:T(8,128)(2,1)}, bf16[1,256,2048]{2,1,0:T(8,128)(2,1)}, u32[]{:S(2)}, u32[]{:S(2)}) %collective-permute-start.8) | collective-permute-done | bytes 1048608 | tf_op jit(solution)/shard_map/ppermute | solution.py:16
  361.4 6.2 %collective-permute-done.7 = bf16[1,256,2048]{2,1,0:T(8,128)(2,1)} collective-permute-done((bf16[1,256,2048]{2,1,0:T(8,128)(2,1)}, bf16[1,256,2048]{2,1,0:T(8,128)(2,1)}, u32[]{:S(2)}, u32[]{:S(2)}) %collective-permute-start.7) | collective-permute-done | bytes 1048608 | tf_op jit(solution)/shard_map/ppermute | solution.py:16
  367.6 3.8 fusion.46
  371.9 3.1 fusion.142
  375.0 3.9 fusion.145
  378.9 59.5 %all-gather.29.cloned.1.call-done = bf16[1,2048,2048]{2,1,0:T(8,128)(2,1)} async-done(((bf16[1,256,2048]{2,1,0:T(8,128)(2,1)}), bf16[1,2048,2048]{2,1,0:T(8,128)(2,1)}) %all-gather.29.cloned.1.call-update) | async-done | bytes 8388624 | tf_op jit(solution)/shard_map/all_gather | solution.py:252
  438.4 4.9 fusion.14
  444.9 74.9 %reduce-scatter.2.cloned.1.call-done = f32[136,256]{1,0:T(8,128)} async-done(((f32[136,4096]{1,0:T(8,128)}), f32[136,256]{1,0:T(8,128)}) %reduce-scatter.2.cloned.1.call-update) | async-done | bytes 139280 | tf_op jit(solution)/shard_map/reduce_scatter | solution.py:269
  519.9 2.4 fusion.71
  522.5 5.1 fusion.139
  528.8 40.5 %all-gather.27.cloned.1.call-done = f32[136,4096]{1,0:T(8,128)} async-done(((f32[136,256]{1,0:T(8,128)}), f32[136,4096]{1,0:T(8,128)}) %all-gather.27.cloned.1.call-update) | async-done | bytes 2228240 | tf_op jit(solution)/shard_map/all_gather | solution.py:268
  572.8 2.7 slice.682
  (112 shorter events, 40.7 us)
Async XLA Ops:
  7.2 91.4 %copy-start = (s32[16,1]{0,1:T(1,128)S(1)}, s32[16,1]{0,1:T(1,128)}, u32[]{:S(2)}) copy-start(s32[16,1]{0,1:T(1,128)} %param.18) | copy-start | bytes 196
  7.2 28.6 %all-gather.13.cloned.1.call-start = ((), (), s32[]{:S(2)}) async-start(), calls=%async_computation.2 | async-start | bytes 1179648 | tf_op jit(solution)/shard_map/all_gather | solution.py:75
  7.9 74.9 %all-gather.17.cloned.1.call-start = ((), (), s32[]{:S(2)}) async-start(), calls=%async_computation.4 | async-start | bytes 7077888 | tf_op jit(solution)/shard_map/all_gather | solution.py:90
  8.7 165.5 %all-gather.15.cloned.1.call-start = ((), (), s32[]{:S(2)}) async-start(), calls=%async_computation.3 | async-start | bytes 4718592 | tf_op jit(solution)/shard_map/all_gather | solution.py:141
  35.8 4.0 copy-start.16
  61.6 20.2 %copy-start.11 = (f32[1024]{0:T(1024)S(1)}, f32[1024]{0:T(1024)}, u32[]{:S(2)}) copy-start(f32[1024]{0:T(1024)} %param.14) | copy-start | bytes 12292
  81.2 0.6 copy-start.13
  82.8 17.0 %copy-start.15 = (s32[16,2]{0,1:T(2,128)S(1)}, s32[16,2]{0,1:T(2,128)}, u32[]{:S(2)}) copy-start(s32[16,2]{0,1:T(2,128)} %param.17) | copy-start | bytes 388
  82.8 91.5 %all-gather.19.cloned.1.call-start = ((), (), s32[]{:S(2)}) async-start(), calls=%async_computation.5 | async-start | bytes 2359296 | tf_op jit(solution)/shard_map/all_gather | solution.py:91
  87.6 1.1 copy-start.8
  90.0 26.6 %collective-permute-start.1 = (bf16[1,256,2048]{2,1,0:T(8,128)(2,1)}, bf16[1,256,2048]{2,1,0:T(8,128)(2,1)}, u32[]{:S(2)}, u32[]{:S(2)}) collective-permute-start(bf16[1,256,2048]{2,1,0:T(8,128)(2,1)} %get-tuple-element.65), channel_id=1, source_target_pairs={{0,2},{1,3},{2,4},{3,5},{4,6},{5,7},{6,8},{7,9},{8,10},{9,11},{10,... | collective-permute-start | bytes 3145736 | tf_op jit(solution)/shard_map/ppermute | solution.py:16
  93.7 44.2 %collective-permute-start = (bf16[1,256,2048]{2,1,0:T(8,128)(2,1)}, bf16[1,256,2048]{2,1,0:T(8,128)(2,1)}, u32[]{:S(2)}, u32[]{:S(2)}) collective-permute-start(bf16[1,256,2048]{2,1,0:T(8,128)(2,1)} %get-tuple-element.65), channel_id=1, source_target_pairs={{0,1},{1,2},{2,3},{3,4},{4,5},{5,6},{6,7},{7,8},{8,9},{9,10},{10,1... | collective-permute-start | bytes 3145736 | tf_op jit(solution)/shard_map/ppermute | solution.py:16
  97.2 40.9 %collective-permute-start.2 = (bf16[1,256,2048]{2,1,0:T(8,128)(2,1)}, bf16[1,256,2048]{2,1,0:T(8,128)(2,1)}, u32[]{:S(2)}, u32[]{:S(2)}) collective-permute-start(bf16[1,256,2048]{2,1,0:T(8,128)(2,1)} %get-tuple-element.65), channel_id=1, source_target_pairs={{1,0},{2,1},{3,2},{4,3},{5,4},{6,5},{7,6},{8,7},{9,8},{10,9},{11,1... | collective-permute-start | bytes 3145736 | tf_op jit(solution)/shard_map/ppermute | solution.py:16
  98.5 112.3 %all-gather.21.cloned.1.call-start = ((), (), s32[]{:S(2)}) async-start(), calls=%async_computation.6 | async-start | bytes 4718592 | tf_op jit(solution)/shard_map/all_gather | solution.py:180
  154.4 10.3 %copy-start.6 = (bf16[1024,16,64]{0,2,1:T(8,128)(2,1)S(1)}, bf16[1024,16,64]{0,2,1:T(8,128)(2,1)}, u32[]{:S(2)}) copy-start(bf16[1024,16,64]{0,2,1:T(8,128)(2,1)} %reshape.370) | copy-start | bytes 6291460
  164.7 9.5 %copy-start.9 = (f32[31,1024]{1,0:T(8,128)S(1)}, f32[31,1024]{1,0:T(8,128)}, u32[]{:S(2)}) copy-start(f32[31,1024]{1,0:T(8,128)} %param.16) | copy-start | bytes 380932
  174.1 2.8 copy-start.10
  174.1 89.1 %all-gather.23.cloned.1.call-start = ((), (), s32[]{:S(2)}) async-start(), calls=%async_computation.7 | async-start | bytes 4718592 | tf_op jit(solution)/shard_map/all_gather | solution.py:190
  177.1 5.8 %collective-permute-start.3 = (bf16[1,15,1024]{2,1,0:T(8,128)(2,1)S(1)}, bf16[1,15,1024]{2,1,0:T(8,128)(2,1)S(1)}, u32[]{:S(2)}, u32[]{:S(2)}) collective-permute-start(bf16[1,15,1024]{2,1,0:T(8,128)(2,1)S(1)} %get-tuple-element.68), channel_id=1, source_target_pairs={{0,1},{1,2},{2,3},{3,4},{4,5},{5,6},{6,7},{7,8},{8,9},{9,10},{10,1... | collective-permute-start | bytes 92168 | tf_op jit(solution)/shard_map/ppermute | solution.py:24
  181.4 5.8 collective-permute-start.4
  193.6 4.8 collective-permute-start.5
  196.9 5.8 collective-permute-start.6
  202.8 5.7 copy-start.5
  210.8 164.2 %all-gather.25.cloned.1.call-start = ((), (), s32[]{:S(2)}) async-start(), calls=%async_computation.8 | async-start | bytes 4718592 | tf_op jit(solution)/shard_map/all_gather | solution.py:247
  263.2 9.8 %copy-start.2 = (bf16[1,256,1024]{1,2,0:T(8,128)(2,1)S(1)}, bf16[1,256,1024]{1,2,0:T(8,128)(2,1)}, u32[]{:S(2)}) copy-start(bf16[1,256,1024]{1,2,0:T(8,128)(2,1)} %copy.86) | copy-start | bytes 1572868
  263.3 175.2 %all-gather.29.cloned.1.call-start = ((), (), s32[]{:S(2)}) async-start(), calls=%async_computation.11 | async-start | bytes 9437184 | tf_op jit(solution)/shard_map/all_gather | solution.py:252
  328.4 10.7 %copy-start.7 = (bf16[1,1,256,1024]{3,2,1,0:T(8,128)(2,1)S(1)}, bf16[1,1,256,1024]{3,2,1,0:T(8,128)(2,1)}, u32[]{:S(2)}) copy-start(bf16[1,1,256,1024]{3,2,1,0:T(8,128)(2,1)} %copy.91) | copy-start | bytes 1572868
  330.8 30.2 %collective-permute-start.8 = (bf16[1,256,2048]{2,1,0:T(8,128)(2,1)}, bf16[1,256,2048]{2,1,0:T(8,128)(2,1)}, u32[]{:S(2)}, u32[]{:S(2)}) collective-permute-start(bf16[1,256,2048]{2,1,0:T(8,128)(2,1)} %pad_maximum_fusion.3), channel_id=1, source_target_pairs={{2,0},{3,1},{4,2},{5,3},{6,4},{7,5},{8,6},{9,7},{10,8},{11,9},{12,... | collective-permute-start | bytes 3145736 | tf_op jit(solution)/shard_map/ppermute | solution.py:16
  334.3 27.0 %collective-permute-start.9 = (bf16[1,256,2048]{2,1,0:T(8,128)(2,1)}, bf16[1,256,2048]{2,1,0:T(8,128)(2,1)}, u32[]{:S(2)}, u32[]{:S(2)}) collective-permute-start(bf16[1,256,2048]{2,1,0:T(8,128)(2,1)} %pad_maximum_fusion.4), channel_id=1, source_target_pairs={{0,1},{1,2},{2,3},{3,4},{4,5},{5,6},{6,7},{7,8},{8,9},{9,10},{10,1... | collective-permute-start | bytes 3145736 | tf_op jit(solution)/shard_map/ppermute | solution.py:16
  340.2 27.4 %collective-permute-start.7 = (bf16[1,256,2048]{2,1,0:T(8,128)(2,1)}, bf16[1,256,2048]{2,1,0:T(8,128)(2,1)}, u32[]{:S(2)}, u32[]{:S(2)}) collective-permute-start(bf16[1,256,2048]{2,1,0:T(8,128)(2,1)} %pad_maximum_fusion.2), channel_id=1, source_target_pairs={{1,0},{2,1},{3,2},{4,3},{5,4},{6,5},{7,6},{8,7},{9,8},{10,9},{11,1... | collective-permute-start | bytes 3145736 | tf_op jit(solution)/shard_map/ppermute | solution.py:16
  371.4 148.4 %reduce-scatter.2.cloned.1.call-start = ((), (), s32[]{:S(2)}) async-start(), calls=%async_computation.9 | async-start | bytes 2367488 | tf_op jit(solution)/shard_map/reduce_scatter | solution.py:269
  443.3 78.9 %copy-start.4 = (bf16[1,256,16,64]{1,3,2,0:T(8,128)(2,1)S(1)}, bf16[1,256,16,64]{1,3,2,0:T(8,128)(2,1)}, u32[]{:S(2)}) copy-start(bf16[1,256,16,64]{1,3,2,0:T(8,128)(2,1)} %convolution_bitcast_fusion) | copy-start | bytes 1572868
  443.3 79.1 %copy-start.12 = (f32[1024]{0:T(1024)S(1)}, f32[1024]{0:T(1024)}, u32[]{:S(2)}) copy-start(f32[1024]{0:T(1024)} %param.14) | copy-start | bytes 12292
  444.9 124.4 %all-gather.27.cloned.1.call-start = ((), (), s32[]{:S(2)}) async-start(), calls=%async_computation.10 | async-start | bytes 2367488 | tf_op jit(solution)/shard_map/all_gather | solution.py:268
  522.4 5.1 copy-start.3
  522.5 5.1 copy-start.14
  522.5 53.0 %copy-start.1 = (s32[16,1]{0,1:T(1,128)S(1)}, s32[16,1]{0,1:T(1,128)}, u32[]{:S(2)}) copy-start(s32[16,1]{0,1:T(1,128)} %param.18) | copy-start | bytes 196
Sparse Core Ops, SparseCore 0:
  9.7 26.0 all-gather.12
  37.5 41.9 all-gather.16
  82.9 31.1 all-gather.14
  115.6 25.1 all-gather.18
  174.3 36.4 all-gather.20
  212.9 33.8 all-gather.22
  263.4 37.8 all-gather.24
  371.6 66.8 all-gather.28
  445.0 74.7 reduce-scatter.1
  521.8 47.4 all-gather.26

commit v7 on v5

--- a/solution.py
+++ b/solution.py
@@ -198,64 +198,49 @@
     grad_query = jnp.einsum(
         "rhqk,rkhd->rqhd", grad_scores, key_flat, preferred_element_type=jnp.float32
     )
-    grad_key_own = jnp.einsum(
-        "rhqk,rqhd->rkhd", grad_scores[..., :frames_dev], query_all,
-        preferred_element_type=jnp.float32,
-    )
-    grad_value_own = jnp.einsum(
-        "rhqk,rqhd->rkhd", probs_low[..., :frames_dev], grad_heads,
-        preferred_element_type=jnp.float32,
-    )
-    grad_key_far = jnp.einsum(
-        "rhqk,rqhd->rkhd", grad_scores[..., frames_dev:], query_all,
-        preferred_element_type=jnp.float32,
-    ).astype(jnp.bfloat16)
-    grad_value_far = jnp.einsum(
-        "rhqk,rqhd->rkhd", probs_low[..., frames_dev:], grad_heads,
-        preferred_element_type=jnp.float32,
-    ).astype(jnp.bfloat16)
+    transposed_dims = (((1,), (2,)), ((0, 2), (0, 1)))
+    key_grads = lax.dot_general(
+        query_all, grad_scores, transposed_dims, preferred_element_type=jnp.float32
+    ).reshape(recordings, model_width, -1)
+    value_grads = lax.dot_general(
+        grad_heads, probs_low, transposed_dims, preferred_element_type=jnp.float32
+    ).reshape(recordings, model_width, -1)
     kernel_dp, middle_rows, grad_query = lax.optimization_barrier(
         (kernel_dp, middle_rows, grad_query)
     )
     grad_wout = lax.dot_general(
         mixed_columns, middle_rows, contract_rows, preferred_element_type=jnp.float32
     )
-    grad_query = grad_query.reshape(recordings * frames_dev, model_width)
-    grad_key_far = grad_key_far.reshape(recordings, seen_count - 1, frames_dev, model_width)
-    grad_value_far = grad_value_far.reshape(recordings, seen_count - 1, frames_dev, model_width)
+    grad_query = grad_query.reshape(recordings * frames_dev, model_width).astype(jnp.bfloat16)
     pair_total = jnp.concatenate(
-        [
-            grad_key_own.reshape(recordings, frames_dev, model_width),
-            grad_value_own.reshape(recordings, frames_dev, model_width),
-        ],
-        axis=2,
+        [key_grads[:, :, :frames_dev], value_grads[:, :, :frames_dev]], axis=1
     )
     for position, offset in enumerate(offsets):
+        window = slice((position + 1) * frames_dev, (position + 2) * frames_dev)
         outgoing = jnp.concatenate(
-            [grad_key_far[:, position], grad_value_far[:, position]], axis=2
-        )
+            [key_grads[:, :, window], value_grads[:, :, window]], axis=1
+        ).astype(jnp.bfloat16)
         arrived = from_behind(outgoing, "ctx", offset)
         pair_total = pair_total + arrived.astype(jnp.float32)
-    grad_projected = jnp.concatenate(
-        [
-            grad_query.astype(jnp.bfloat16),
-            pair_total.reshape(recordings * frames_dev, 2 * model_width).astype(jnp.bfloat16),
-        ],
-        axis=1,
-    )
+    pair_low = pair_total.astype(jnp.bfloat16)
     normed_columns = lax.dynamic_slice_in_dim(normed_all, dp_index * shard_width, shard_width, 1)
-    query_rows = lax.all_gather(grad_projected[:, :model_width], "dp", axis=0, tiled=True)
+    query_rows = lax.all_gather(grad_query, "dp", axis=0, tiled=True)
     grad_wq = lax.dot_general(
         normed_columns, query_rows, contract_rows, preferred_element_type=jnp.float32
     )
-    pair_part = grad_projected[:, model_width:]
-    pair_rows = lax.all_gather(pair_part, "dp", axis=0, tiled=True)
-    grad_wkv = lax.dot_general(
-        normed_columns, pair_rows, contract_rows, preferred_element_type=jnp.float32
+    pair_rows = lax.all_gather(pair_low, "dp", axis=0, tiled=True)
+    grad_wkv = jnp.einsum(
+        "nfc,nkf->ck",
+        normed_columns.reshape(pair_rows.shape[0], frames_dev, shard_width),
+        pair_rows,
+        preferred_element_type=jnp.float32,
     )
     grad_normed = lax.dot_general(
-        grad_projected, weight_qkv, contract_columns, preferred_element_type=jnp.float32
-    )
+        grad_query, weight_qkv[:, :model_width], contract_columns,
+        preferred_element_type=jnp.float32,
+    ) + jnp.einsum(
+        "rkf,ik->rfi", pair_low, weight_qkv[:, model_width:], preferred_element_type=jnp.float32
+    ).reshape(recordings * frames_dev, model_width)
     grad_embedded = (
         grad_middle.astype(jnp.float32) + norm_back(features, attn_inverse, attn_gain, grad_normed)
     ).astype(jnp.bfloat16)

time: 559 us -> 543 us (0.971)
  local copies, waits for them, and re-layouts: 75.8 us -> 31.6 us
  matrix products: 119 us -> 155 us
  other arithmetic: 47.6 us -> 29.7 us
  waiting for transfers between devices: 206 us -> 219 us
    dot_general x6, matrix products: 27 us -> 61 us  [the longest x1 31.6 us: on_device(): lax.dot_general(query_all, grad_scores, transposed_dims, preferred_elemen...]
    slice x5 -> x3, local copies, waits for them, and re-layouts: 24.4 us -> 0.43 us  [the longest x1 0.21 us: on_device(): key_grads[:, :, window]]
    dot_general x1, matrix products: 7.47 us -> 30.2 us  [on_device(): jnp.einsum('rhqk,rkhd->rqhd', grad_scores, key_flat, preferred_element_ty...]
    sub x1 -> x0, matrix products: 22.4 us -> none  [on_device(): grad_probs - row_sum]
    reshape x4 -> x0, local copies, waits for them, and re-layouts: 14.7 us -> none  [the longest x1 5.29 us: on_device(): grad_value_far.reshape(recordings, seen_count - 1, frames_dev, model_width)]
    convert_element_type x2 -> x1, other arithmetic: 13.3 us -> 1.54 us  [on_device(): pair_low = pair_total.astype(jnp.bfloat16)]
    ppermute x6, waiting for transfers between devices: 50 us -> 60.8 us  [from_behind(): lax.ppermute(value, axis, [(source, source + steps) for source in range(f...]
    unnamed x37 -> x40, local copies, waits for them, and re-layouts: 11.2 us -> 3.08 us
  transfers between devices with their start and end apart: 19 -> 19, of which waited for: 14 -> 13; matrix products, arithmetic and copies ran while one was open for 42% -> 37% of each run, Pallas kernels for 0% -> 0%
where the time goes in v7:
time: 543 us; the launch traced here: 534 us
  waiting for transfers between devices  219 us (40%)
  matrix products  155 us (29%)
  blocking collectives  57.7 us (11%)
  local copies, waits for them, and re-layouts  31.6 us (6%)
  other arithmetic  29.7 us (5%)
  starting transfers between devices  25.4 us (5%)
  between operations  15.5 us (3%)
    psum x1, waiting for transfers between devices, on_device(): lax.psum(jnp.concatenate([weight_rows, kernel_padded.reshape(-1, row_widt...  82.1 us
    all_gather x1, waiting for transfers between devices, on_device(): pair_rows = lax.all_gather(pair_low, 'dp', axis=0, tiled=True)  61 us
    ppermute x6, waiting for transfers between devices, from_behind(): lax.ppermute(value, axis, [(source, source + steps) for source in range(f...  60.8 us
    dot_general x1, matrix products, on_device(): lax.dot_general(query_all, grad_scores, transposed_dims, preferred_elemen...  31.6 us
    dot_general x1, matrix products, on_device(): jnp.einsum('rhqk,rkhd->rqhd', grad_scores, key_flat, preferred_element_ty...  30.2 us
    dot_general x8, matrix products, on_device(): lax.dot_general(table_whole[codebook], picks, (((0,), (0,)), ((), ())), p...  25.8 us
    all_gather x1, blocking collectives, on_device(): ids_whole = lax.all_gather(ids, 'ctx', axis=1, tiled=True)  24 us
    all_to_all x1, blocking collectives, on_device(): lax.all_to_all(transposed, 'ctx', split_axis=1, concat_axis=0, tiled=True)  18.5 us
  transfers between devices with their start and end apart: 19, of which 13 were waited for; matrix products, arithmetic and copies ran while one was open for 37% of the time, Pallas kernels for 0%

profile of v7, /device:TPU:0, one launch (start us, length us, event | category | flops | bytes accessed | tf_op | source)
XLA Modules:
  0.0 533.5 jit_solution(5023312380979488275)
XLA Ops:
  8.7 24.0 %all_gather.33 = s32[1,4096,8]{1,2,0:T(8,128)S(1)} all-gather(s32[1,256,8]{1,2,0:T(8,128)} %param.10), channel_id=1, replica_groups=mesh['dp'=8,'ctx'=16] {'ctx'}, dimensions={1}, use_global_device_ids=true | all-gather | bytes 139264 | tf_op jit(solution)/shard_map/all_gather | solution.py:74
  32.8 2.9 all-gather.11.cloned.1.call-done
  35.8 4.0 fusion.3
  39.8 3.1 fusion.37
  42.9 3.1 fusion.36
  46.0 3.1 fusion.35
  49.0 3.3 fusion.34
  52.3 3.1 fusion.33
  55.4 3.1 fusion.32
  58.5 3.1 fusion.38
  61.7 18.5 %all_to_all.4 = bf16[64,16,256]{2,0,1:T(8,128)(2,1)S(1)} all-to-all(bf16[64,16,256]{2,0,1:T(8,128)(2,1)S(1)} %bitcast.214), channel_id=1, replica_groups=mesh['dp'=8,'ctx'=16] {'ctx'}, dimensions={1} | all-to-all | bytes 1048576 | tf_op jit(solution)/shard_map/all_to_all | solution.py:87
  82.3 4.8 fusion.45
  88.2 1.2 slice_bitcast_fusion.16
  89.5 3.7 collective-permute-start.1
  93.2 3.5 collective-permute-start
  96.6 1.3 collective-permute-start.2
  100.0 1.4 pad_add_fusion
  103.5 12.6 %collective-permute-done.1 = bf16[1,256,2048]{2,1,0:T(8,128)(2,1)} collective-permute-done((bf16[1,256,2048]{2,1,0:T(8,128)(2,1)}, bf16[1,256,2048]{2,1,0:T(8,128)(2,1)}, u32[]{:S(2)}, u32[]{:S(2)}) %collective-permute-start.1) | collective-permute-done | bytes 1048608 | tf_op jit(solution)/shard_map/ppermute | solution.py:16
  116.1 21.3 %collective-permute-done = bf16[1,256,2048]{2,1,0:T(8,128)(2,1)} collective-permute-done((bf16[1,256,2048]{2,1,0:T(8,128)(2,1)}, bf16[1,256,2048]{2,1,0:T(8,128)(2,1)}, u32[]{:S(2)}, u32[]{:S(2)}) %collective-permute-start) | collective-permute-done | bytes 1048608 | tf_op jit(solution)/shard_map/ppermute | solution.py:16
  138.1 2.2 pad_maximum_fusion
  140.3 2.4 fusion.155
  142.7 3.0 copy.35
  145.8 2.7 reshape.444
  148.5 4.3 copy.33
  152.8 3.2 reshape.441
  156.0 10.9 %fusion.163 = (f32[16,256]{1,0:T(8,128)S(1)}, f32[16,256,1024]{2,1,0:T(8,128)}) fusion(pred[1024]{0:T(1024)(128)(4,1)S(1)} %reshape.442, bf16[256,16,64]{0,2,1:T(8,128)(2,1)} %bitcast.216, bf16[1024,16,64]{0,2,1:T(8,128)(2,1)} %reshape.444), kind=kOutput, calls=%fused_computation.272 | convolution fusion | flops 553649152 | bytes 19416064 | tf_op jit(solution)/shard_map/sub | solution.py:133
  167.0 9.4 %fusion.60 = bf16[16,64,256]{2,1,0:T(8,128)(2,1)} fusion(bf16[1024,16,64]{0,2,1:T(8,128)(2,1)S(1)} %reshape.441, f32[16,256,1024]{2,1,0:T(8,128)} %get-tuple-element.110, f32[16,256]{1,0:T(8,128)S(1)} %get-tuple-element.109), kind=kOutput, calls=%fused_computation.106 | convolution fusion | flops 545521664 | bytes 19415040 | tf_op jit(solution)/shard_map/rhqk,rkhd->rqhd/dot_general | solution.py:136
  176.5 2.6 fusion.74
  179.4 4.3 collective-permute-start.3
  183.6 1.5 collective-permute-start.4
  185.2 4.2 collective-permute-done.4
  189.6 6.2 %fusion.71 = (bf16[1,256,1024]{2,1,0:T(8,128)(2,1)S(1)}, f32[1,256,1024]{2,1,0:T(8,128)}) fusion(bf16[1,256,1024]{2,1,0:T(8,128)(2,1)} %param.19, f32[1,286,1024]{2,1,0:T(8,128)S(1)} %maximum_convert_fusion, f32[1024]{0:T(1024)S(1)} %bitcast.280, f32[1024]{0:T(1024)S(1)} %bitcast.282, f32[1024]{0:T(1024)S(1)} %bitcast.224, f32[1024]{0:T(1024)S(1)} %bitcast.226, ...), kind=kLoop, calls=%fused_computation.115 | loop fusion | flops 18612224 | bytes 34729984 | tf_op jit(solution)/shard_map/convert_element_type | solution.py:160
  195.8 2.7 collective-permute-start.5
  198.5 1.3 collective-permute-start.6
  200.1 4.2 collective-permute-done.6
  204.5 5.6 %fusion.76 = (f32[256]{0:T(256)S(1)}, f32[256,1024]{1,0:T(8,128)S(1)}) fusion(bf16[256,1024]{1,0:T(8,128)(2,1)S(1)} %get-tuple-element.112, f32[1024]{0:T(1024)S(1)} %copy-done.13, f32[1,286,1024]{2,1,0:T(8,128)S(1)} %maximum_convert_fusion.1, f32[1024]{0:T(1024)S(1)} %bitcast.281, f32[1024]{0:T(1024)S(1)} %bitcast.283, f32[1024]{0:T(1024)S(1)} %bitcast.225, ...), kind=kLoop, calls=%fused_computation.120 | loop fusion | flops 17039104 | bytes 34210816 | tf_op jit(solution)/shard_map/reduce_sum | solution.py:37
  210.1 1.2 fusion.70
  211.4 1.7 all-gather.19.cloned.1.call-done
  213.1 1.8 fusion.106
  214.9 2.5 fusion.107
  217.7 15.1 %all-gather.1 = f32[8,31,1024]{2,1,0:T(8,128)S(1)} all-gather(f32[1,31,1024]{2,1,0:T(8,128)S(1)} %bitcast.215), channel_id=2, replica_groups=mesh['dp'=8,'ctx'=16] {'dp'}, dimensions={0}, use_global_device_ids=true | all-gather | bytes 1142784 | tf_op jit(solution)/shard_map/all_gather | solution.py:174
  232.9 2.5 convolution_convert_fusion.1
  235.6 9.8 %fusion.164 = f32[16,256,1024]{2,1,0:T(8,128)} fusion(bf16[256,16,64]{0,2,1:T(8,128)(2,1)S(1)} %bitcast.212, bf16[1024,16,64]{0,2,1:T(8,128)(2,1)} %copy-done.2), kind=kOutput, calls=%fused_computation.273 | convolution fusion | flops 536870912 | bytes 19398656 | tf_op jit(solution)/shard_map/rqhd,rkhd->rhqk/dot_general | solution.py:193
  245.4 30.2 %fusion.53 = bf16[1,256,16,64]{1,3,2,0:T(8,128)(2,1)} fusion(bf16[1024,16,64]{0,2,1:T(8,128)(2,1)} %reshape.444, f32[16,256,1024]{2,1,0:T(8,128)} %fusion.164, f32[16,256,1024]{2,1,0:T(8,128)} %get-tuple-element.110, f32[16,256]{1,0:T(8,128)S(1)} %get-tuple-element.109), kind=kOutput, calls=%fused_computation.99 | convolution fusion | flops 566236160 | bytes 36192256 | tf_op jit(solution)/shard_map/rhqk,rkhd->rqhd/dot_general | solution.py:198
  275.7 31.6 %fusion.26 = f32[16,64,1024]{2,1,0:T(8,128)} fusion(bf16[256,16,64]{0,2,1:T(8,128)(2,1)S(1)} %bitcast.217, f32[16,256,1024]{2,1,0:T(8,128)} %fusion.164, f32[16,256,1024]{2,1,0:T(8,128)} %get-tuple-element.110, f32[16,256]{1,0:T(8,128)S(1)} %get-tuple-element.109), kind=kOutput, calls=%fused_computation.67 | convolution fusion | flops 566236160 | bytes 38289408 | tf_op jit(solution)/shard_map/dot_general | solution.py:202
  307.3 7.1 %fusion.41 = f32[16,64,1024]{2,1,0:T(8,128)S(1)} fusion(bf16[256,16,64]{0,2,1:T(8,128)(2,1)S(1)} %bitcast.213, f32[16,256,1024]{2,1,0:T(8,128)} %get-tuple-element.110, f32[16,256]{1,0:T(8,128)S(1)} %get-tuple-element.109), kind=kOutput, calls=%fused_computation.80 | convolution fusion | flops 545259520 | bytes 21512192 | tf_op jit(solution)/shard_map/dot_general | solution.py:205
  314.8 1.9 copy-done.3
  317.2 1.3 collective-permute-start.8
  318.6 3.6 collective-permute-start.9
  322.3 1.3 collective-permute-start.7
  323.9 22.9 %collective-permute-done.8 = bf16[1,2048,256]{2,1,0:T(8,128)(2,1)S(1)} collective-permute-done((bf16[1,2048,256]{2,1,0:T(8,128)(2,1)S(1)}, bf16[1,2048,256]{2,1,0:T(8,128)(2,1)S(1)}, u32[]{:S(2)}, u32[]{:S(2)}) %collective-permute-start.8) | collective-permute-done | bytes 1048608 | tf_op jit(solution)/shard_map/ppermute | solution.py:16
  346.7 3.4 collective-permute-done.7
  350.1 1.5 fusion.50
  353.1 3.9 fusion.145
  357.0 3.7 fusion.165
  360.8 61.0 %all-gather.25.cloned.1.call-done = bf16[8,2048,256]{2,1,0:T(8,128)(2,1)} async-done(((bf16[1,2048,256]{2,1,0:T(8,128)(2,1)}), bf16[8,2048,256]{2,1,0:T(8,128)(2,1)}) %all-gather.25.cloned.1.call-update) | async-done | bytes 8388624 | tf_op jit(solution)/shard_map/all_gather | solution.py:231
  421.7 6.3 %convolution_bitcast_fusion = f32[128,2048]{1,0:T(8,128)S(1)} fusion(bf16[8,256,128]{2,1,0:T(8,128)(2,1)S(1)} %bitcast.208, bf16[8,2048,256]{2,1,0:T(8,128)(2,1)} %all-gather.25.cloned.1.call-done), kind=kOutput, calls=%fused_computation.86 | convolution fusion | flops 1073741824 | bytes 9961472 | tf_op jit(solution)/shard_map/nfc,nkf->ck/dot_general | solution.py:232
  428.1 1.6 pad_maximum_fusion.1
  430.9 2.3 fusion.46
  433.3 3.8 fusion.142
  437.1 1.2 fusion.143
  438.3 82.1 %all-reduce.3.cloned.1.call-done = f32[136,4096]{1,0:T(8,128)} async-done(((f32[136,4096]{1,0:T(8,128)}), f32[136,4096]{1,0:T(8,128)}) %all-reduce.3.cloned.1.call-update) | async-done | bytes 2228240 | tf_op jit(solution)/shard_map/psum | solution.py:252
  522.0 1.9 slice.689
  523.8 2.7 slice.688
  (106 shorter events, 16.3 us)
Async XLA Ops:
  7.2 90.8 %copy-start = (s32[16,1]{0,1:T(1,128)S(1)}, s32[16,1]{0,1:T(1,128)}, u32[]{:S(2)}) copy-start(s32[16,1]{0,1:T(1,128)} %param.18) | copy-start | bytes 196
  7.2 28.6 %all-gather.11.cloned.1.call-start = ((), (), s32[]{:S(2)}) async-start(), calls=%async_computation.1 | async-start | bytes 1179648 | tf_op jit(solution)/shard_map/all_gather | solution.py:75
  7.9 74.4 %all-gather.15.cloned.1.call-start = ((), (), s32[]{:S(2)}) async-start(), calls=%async_computation.3 | async-start | bytes 7077888 | tf_op jit(solution)/shard_map/all_gather | solution.py:90
  8.7 167.7 %all-gather.13.cloned.1.call-start = ((), (), s32[]{:S(2)}) async-start(), calls=%async_computation.2 | async-start | bytes 4718592 | tf_op jit(solution)/shard_map/all_gather | solution.py:141
  35.8 4.0 copy-start.19
  61.6 19.2 %copy-start.14 = (f32[1024]{0:T(1024)S(1)}, f32[1024]{0:T(1024)}, u32[]{:S(2)}) copy-start(f32[1024]{0:T(1024)} %param.14) | copy-start | bytes 12292
  80.8 1.5 copy-start.16
  81.8 17.4 %copy-start.18 = (s32[16,2]{0,1:T(2,128)S(1)}, s32[16,2]{0,1:T(2,128)}, u32[]{:S(2)}) copy-start(s32[16,2]{0,1:T(2,128)} %param.17) | copy-start | bytes 388
  81.8 94.7 %all-gather.17.cloned.1.call-start = ((), (), s32[]{:S(2)}) async-start(), calls=%async_computation.4 | async-start | bytes 2359296 | tf_op jit(solution)/shard_map/all_gather | solution.py:91
  87.1 1.1 copy-start.9
  89.5 26.6 %collective-permute-start.1 = (bf16[1,256,2048]{2,1,0:T(8,128)(2,1)}, bf16[1,256,2048]{2,1,0:T(8,128)(2,1)}, u32[]{:S(2)}, u32[]{:S(2)}) collective-permute-start(bf16[1,256,2048]{2,1,0:T(8,128)(2,1)} %get-tuple-element.65), channel_id=1, source_target_pairs={{0,2},{1,3},{2,4},{3,5},{4,6},{5,7},{6,8},{7,9},{8,10},{9,11},{10,... | collective-permute-start | bytes 3145736 | tf_op jit(solution)/shard_map/ppermute | solution.py:16
  93.2 44.2 %collective-permute-start = (bf16[1,256,2048]{2,1,0:T(8,128)(2,1)}, bf16[1,256,2048]{2,1,0:T(8,128)(2,1)}, u32[]{:S(2)}, u32[]{:S(2)}) collective-permute-start(bf16[1,256,2048]{2,1,0:T(8,128)(2,1)} %get-tuple-element.65), channel_id=1, source_target_pairs={{0,1},{1,2},{2,3},{3,4},{4,5},{5,6},{6,7},{7,8},{8,9},{9,10},{10,1... | collective-permute-start | bytes 3145736 | tf_op jit(solution)/shard_map/ppermute | solution.py:16
  96.6 41.5 %collective-permute-start.2 = (bf16[1,256,2048]{2,1,0:T(8,128)(2,1)}, bf16[1,256,2048]{2,1,0:T(8,128)(2,1)}, u32[]{:S(2)}, u32[]{:S(2)}) collective-permute-start(bf16[1,256,2048]{2,1,0:T(8,128)(2,1)} %get-tuple-element.65), channel_id=1, source_target_pairs={{1,0},{2,1},{3,2},{4,3},{5,4},{6,5},{7,6},{8,7},{9,8},{10,9},{11,1... | collective-permute-start | bytes 3145736 | tf_op jit(solution)/shard_map/ppermute | solution.py:16
  98.0 115.1 %all-gather.19.cloned.1.call-start = ((), (), s32[]{:S(2)}) async-start(), calls=%async_computation.5 | async-start | bytes 4718592 | tf_op jit(solution)/shard_map/all_gather | solution.py:180
  156.0 11.0 %copy-start.2 = (bf16[1024,16,64]{0,2,1:T(8,128)(2,1)}, bf16[1024,16,64]{0,2,1:T(8,128)(2,1)S(1)}, u32[]{:S(2)}) copy-start(bf16[1024,16,64]{0,2,1:T(8,128)(2,1)S(1)} %reshape.441) | copy-start | bytes 6291460
  166.9 9.5 %copy-start.12 = (f32[31,1024]{1,0:T(8,128)S(1)}, f32[31,1024]{1,0:T(8,128)}, u32[]{:S(2)}) copy-start(f32[31,1024]{1,0:T(8,128)} %param.16) | copy-start | bytes 380932
  176.4 2.8 copy-start.13
  176.4 99.2 %all-gather.21.cloned.1.call-start = ((), (), s32[]{:S(2)}) async-start(), calls=%async_computation.6 | async-start | bytes 4718592 | tf_op jit(solution)/shard_map/all_gather | solution.py:190
  179.4 5.8 %collective-permute-start.3 = (bf16[1,15,1024]{2,1,0:T(8,128)(2,1)S(1)}, bf16[1,15,1024]{2,1,0:T(8,128)(2,1)S(1)}, u32[]{:S(2)}, u32[]{:S(2)}) collective-permute-start(bf16[1,15,1024]{2,1,0:T(8,128)(2,1)S(1)} %get-tuple-element.68), channel_id=1, source_target_pairs={{0,1},{1,2},{2,3},{3,4},{4,5},{5,6},{6,7},{7,8},{8,9},{9,10},{10,1... | collective-permute-start | bytes 92168 | tf_op jit(solution)/shard_map/ppermute | solution.py:24
  183.6 5.8 %collective-permute-start.4 = (bf16[1,15,1024]{2,1,0:T(8,128)(2,1)S(1)}, bf16[1,15,1024]{2,1,0:T(8,128)(2,1)S(1)}, u32[]{:S(2)}, u32[]{:S(2)}) collective-permute-start(bf16[1,15,1024]{2,1,0:T(8,128)(2,1)S(1)} %get-tuple-element.69), channel_id=1, source_target_pairs={{1,0},{2,1},{3,2},{4,3},{5,4},{6,5},{7,6},{8,7},{9,8},{10,9},{11,1... | collective-permute-start | bytes 92168 | tf_op jit(solution)/shard_map/ppermute | solution.py:27
  195.8 4.3 collective-permute-start.5
  198.5 5.8 %collective-permute-start.6 = (bf16[1,15,1024]{2,1,0:T(8,128)(2,1)S(1)}, bf16[1,15,1024]{2,1,0:T(8,128)(2,1)S(1)}, u32[]{:S(2)}, u32[]{:S(2)}) collective-permute-start(bf16[1,15,1024]{2,1,0:T(8,128)(2,1)S(1)} %get-tuple-element.67), channel_id=1, source_target_pairs={{1,0},{2,1},{3,2},{4,3},{5,4},{6,5},{7,6},{8,7},{9,8},{10,9},{11,1... | collective-permute-start | bytes 92168 | tf_op jit(solution)/shard_map/ppermute | solution.py:27
  204.5 5.7 %copy-start.7 = (bf16[1,256,1024]{2,1,0:T(8,128)(2,1)S(1)}, bf16[1,256,1024]{2,1,0:T(8,128)(2,1)}, u32[]{:S(2)}) copy-start(bf16[1,256,1024]{2,1,0:T(8,128)(2,1)} %param.19) | copy-start | bytes 1572868
  213.1 144.0 %all-gather.23.cloned.1.call-start = ((), (), s32[]{:S(2)}) async-start(), calls=%async_computation.7 | async-start | bytes 4718592 | tf_op jit(solution)/shard_map/all_gather | solution.py:227
  245.4 30.2 %copy-start.10 = (bf16[1,256,1024]{1,2,0:T(8,128)(2,1)S(1)}, bf16[1,256,1024]{1,2,0:T(8,128)(2,1)}, u32[]{:S(2)}) copy-start(bf16[1,256,1024]{1,2,0:T(8,128)(2,1)} %copy.34) | copy-start | bytes 1572868
  275.6 146.1 %all-gather.25.cloned.1.call-start = ((), (), s32[]{:S(2)}) async-start(), calls=%async_computation.8 | async-start | bytes 9437184 | tf_op jit(solution)/shard_map/all_gather | solution.py:231
  314.4 2.2 copy-start.3
  317.2 29.5 %collective-permute-start.8 = (bf16[1,2048,256]{2,1,0:T(8,128)(2,1)S(1)}, bf16[1,2048,256]{2,1,0:T(8,128)(2,1)S(1)}, u32[]{:S(2)}, u32[]{:S(2)}) collective-permute-start(bf16[1,2048,256]{2,1,0:T(8,128)(2,1)S(1)} %pad_maximum_fusion.3), channel_id=1, source_target_pairs={{2,0},{3,1},{4,2},{5,3},{6,4},{7,5},{8,6},{9,7},{10,8},{11,9},{12,... | collective-permute-start | bytes 3145736 | tf_op jit(solution)/shard_map/ppermute | solution.py:16
  318.6 28.1 %collective-permute-start.9 = (bf16[1,2048,256]{2,1,0:T(8,128)(2,1)S(1)}, bf16[1,2048,256]{2,1,0:T(8,128)(2,1)S(1)}, u32[]{:S(2)}, u32[]{:S(2)}) collective-permute-start(bf16[1,2048,256]{2,1,0:T(8,128)(2,1)S(1)} %pad_maximum_fusion.4), channel_id=1, source_target_pairs={{0,1},{1,2},{2,3},{3,4},{4,5},{5,6},{6,7},{7,8},{8,9},{9,10},{10,1... | collective-permute-start | bytes 3145736 | tf_op jit(solution)/shard_map/ppermute | solution.py:16
  322.3 27.8 %collective-permute-start.7 = (bf16[1,2048,256]{2,1,0:T(8,128)(2,1)S(1)}, bf16[1,2048,256]{2,1,0:T(8,128)(2,1)S(1)}, u32[]{:S(2)}, u32[]{:S(2)}) collective-permute-start(bf16[1,2048,256]{2,1,0:T(8,128)(2,1)S(1)} %pad_maximum_fusion.2), channel_id=1, source_target_pairs={{1,0},{2,1},{3,2},{4,3},{5,4},{6,5},{7,6},{8,7},{9,8},{10,9},{11,1... | collective-permute-start | bytes 3145736 | tf_op jit(solution)/shard_map/ppermute | solution.py:16
  351.7 168.7 %all-reduce.3.cloned.1.call-start = ((), (), s32[]{:S(2)}) async-start(), calls=%async_computation.9 | async-start | bytes 4456448 | tf_op jit(solution)/shard_map/psum | solution.py:252
  421.7 6.3 %copy-start.8 = (f32[128,1024]{1,0:T(8,128)S(1)}, f32[128,1024]{1,0:T(8,128)}, u32[]{:S(2)}) copy-start(f32[128,1024]{1,0:T(8,128)} %fusion.145) | copy-start | bytes 1572868
  428.1 1.6 copy-start.5
  429.7 1.2 copy-start.11
  429.7 3.6 copy-start.15
  429.7 3.5 copy-start.6
  433.2 3.8 copy-start.4
  433.2 3.8 copy-start.17
  433.3 93.3 %copy-start.1 = (s32[16,1]{0,1:T(1,128)S(1)}, s32[16,1]{0,1:T(1,128)}, u32[]{:S(2)}) copy-start(s32[16,1]{0,1:T(1,128)} %param.18) | copy-start | bytes 196
Sparse Core Ops, SparseCore 0:
  9.7 26.0 all-gather.10
  37.5 41.9 all-gather.14
  81.9 32.0 all-gather.12
  115.6 25.1 all-gather.16
  176.5 36.4 all-gather.18
  215.2 33.8 all-gather.20
  275.8 37.1 all-gather.22
  351.8 69.8 all-gather.24
  429.8 90.4 all-reduce.2

commit v8 on v7

--- a/solution.py
+++ b/solution.py
@@ -194,9 +194,8 @@
         "rqhd,rkhd->rhqk", grad_heads, value_flat, preferred_element_type=jnp.float32
     )
     row_sum = jnp.sum(probs * grad_probs, axis=3, keepdims=True)
-    grad_scores = (probs * (grad_probs - row_sum) * score_scale).astype(jnp.bfloat16)
-    grad_query = jnp.einsum(
-        "rhqk,rkhd->rqhd", grad_scores, key_flat, preferred_element_type=jnp.float32
+    grad_scores = lax.optimization_barrier(
+        (probs * (grad_probs - row_sum) * score_scale).astype(jnp.bfloat16)
     )
     transposed_dims = (((1,), (2,)), ((0, 2), (0, 1)))
     key_grads = lax.dot_general(
@@ -205,6 +204,20 @@
     value_grads = lax.dot_general(
         grad_heads, probs_low, transposed_dims, preferred_element_type=jnp.float32
     ).reshape(recordings, model_width, -1)
+    outgoing = [
+        jnp.concatenate(
+            [key_grads[:, :, window], value_grads[:, :, window]], axis=1
+        ).astype(jnp.bfloat16)
+        for window in [
+            slice((position + 1) * frames_dev, (position + 2) * frames_dev)
+            for position in range(len(offsets))
+        ]
+    ]
+    outgoing, scores_for_query = lax.optimization_barrier((outgoing, grad_scores))
+    arrivals = [from_behind(sent, "ctx", offset) for sent, offset in zip(outgoing, offsets)]
+    grad_query = jnp.einsum(
+        "rhqk,rkhd->rqhd", scores_for_query, key_flat, preferred_element_type=jnp.float32
+    )
     kernel_dp, middle_rows, grad_query = lax.optimization_barrier(
         (kernel_dp, middle_rows, grad_query)
     )
@@ -215,12 +228,7 @@
     pair_total = jnp.concatenate(
         [key_grads[:, :, :frames_dev], value_grads[:, :, :frames_dev]], axis=1
     )
-    for position, offset in enumerate(offsets):
-        window = slice((position + 1) * frames_dev, (position + 2) * frames_dev)
-        outgoing = jnp.concatenate(
-            [key_grads[:, :, window], value_grads[:, :, window]], axis=1
-        ).astype(jnp.bfloat16)
-        arrived = from_behind(outgoing, "ctx", offset)
+    for arrived in arrivals:
         pair_total = pair_total + arrived.astype(jnp.float32)
     pair_low = pair_total.astype(jnp.bfloat16)
     normed_columns = lax.dynamic_slice_in_dim(normed_all, dp_index * shard_width, shard_width, 1)

time: 543 us -> 514 us (0.947)
  matrix products: 155 us -> 112 us
  local copies, waits for them, and re-layouts: 31.6 us -> 45.7 us
  waiting for transfers between devices: 219 us -> 213 us
    dot_general x2 -> x1, matrix products: 40 us -> 3.46 us  [on_device(): jnp.einsum('rhqk,rkhd->rqhd', scores_for_query, key_flat, preferred_eleme...]
    dot_general x1, matrix products: 31.6 us -> 1.57 us  [on_device(): lax.dot_general(query_all, grad_scores, transposed_dims, preferred_elemen...]
    sub x0 -> x1, matrix products: none -> 22.5 us  [on_device(): grad_probs - row_sum]
  transfers between devices with their start and end apart: 19 -> 19, of which waited for: 13 -> 10; matrix products, arithmetic and copies ran while one was open for 37% -> 34% of each run, Pallas kernels for 0% -> 0%
where the time goes in v8:
time: 514 us; the launch traced here: 504 us
  waiting for transfers between devices  213 us (41%)
  matrix products  112 us (22%)
  blocking collectives  57.3 us (11%)
  local copies, waits for them, and re-layouts  45.7 us (9%)
  other arithmetic  33.6 us (7%)
  starting transfers between devices  27.2 us (5%)
  between operations  15.6 us (3%)
    psum x1, waiting for transfers between devices, on_device(): lax.psum(jnp.concatenate([weight_rows, kernel_padded.reshape(-1, row_widt...  82.1 us
    all_gather x1, waiting for transfers between devices, on_device(): pair_rows = lax.all_gather(pair_low, 'dp', axis=0, tiled=True)  62.8 us
    ppermute x6, waiting for transfers between devices, from_behind(): lax.ppermute(value, axis, [(source, source + steps) for source in range(f...  59 us
    dot_general x8, matrix products, on_device(): lax.dot_general(table_whole[codebook], picks, (((0,), (0,)), ((), ())), p...  25.8 us
    all_gather x1, blocking collectives, on_device(): ids_whole = lax.all_gather(ids, 'ctx', axis=1, tiled=True)  24 us
    sub x1, matrix products, on_device(): grad_probs - row_sum  22.5 us
    all_to_all x1, blocking collectives, on_device(): lax.all_to_all(transposed, 'ctx', split_axis=1, concat_axis=0, tiled=True)  18.5 us
    ppermute x6, starting transfers between devices, from_behind(): lax.ppermute(value, axis, [(source, source + steps) for source in range(f...  16.2 us
  transfers between devices with their start and end apart: 19, of which 10 were waited for; matrix products, arithmetic and copies ran while one was open for 34% of the time, Pallas kernels for 0%

profile of v8, /device:TPU:0, one launch (start us, length us, event | category | flops | bytes accessed | tf_op | source)
XLA Modules:
  0.0 504.3 jit_solution(16240192141750936419)
XLA Ops:
  8.7 24.0 %all_gather.33 = s32[1,4096,8]{1,2,0:T(8,128)S(1)} all-gather(s32[1,256,8]{1,2,0:T(8,128)} %param.10), channel_id=1, replica_groups=mesh['dp'=8,'ctx'=16] {'ctx'}, dimensions={1}, use_global_device_ids=true | all-gather | bytes 139264 | tf_op jit(solution)/shard_map/all_gather | solution.py:74
  32.8 2.9 all-gather.11.cloned.1.call-done
  35.8 4.0 fusion.3
  39.8 3.1 fusion.38
  42.9 3.1 fusion.37
  46.0 3.1 fusion.36
  49.0 3.3 fusion.35
  52.3 3.1 fusion.34
  55.4 3.1 fusion.33
  58.5 3.1 fusion.39
  61.7 18.5 %all_to_all.4 = bf16[64,16,256]{2,0,1:T(8,128)(2,1)S(1)} all-to-all(bf16[64,16,256]{2,0,1:T(8,128)(2,1)S(1)} %bitcast.226), channel_id=1, replica_groups=mesh['dp'=8,'ctx'=16] {'ctx'}, dimensions={1} | all-to-all | bytes 1048576 | tf_op jit(solution)/shard_map/all_to_all | solution.py:87
  82.3 4.8 fusion.46
  89.5 3.7 collective-permute-start.1
  93.2 3.5 collective-permute-start
  100.0 1.4 pad_add_fusion
  102.7 13.4 %collective-permute-done.1 = bf16[1,256,2048]{2,1,0:T(8,128)(2,1)} collective-permute-done((bf16[1,256,2048]{2,1,0:T(8,128)(2,1)}, bf16[1,256,2048]{2,1,0:T(8,128)(2,1)}, u32[]{:S(2)}, u32[]{:S(2)}) %collective-permute-start.1) | collective-permute-done | bytes 1048608 | tf_op jit(solution)/shard_map/ppermute | solution.py:16
  116.1 21.3 %collective-permute-done = bf16[1,256,2048]{2,1,0:T(8,128)(2,1)} collective-permute-done((bf16[1,256,2048]{2,1,0:T(8,128)(2,1)}, bf16[1,256,2048]{2,1,0:T(8,128)(2,1)}, u32[]{:S(2)}, u32[]{:S(2)}) %collective-permute-start) | collective-permute-done | bytes 1048608 | tf_op jit(solution)/shard_map/ppermute | solution.py:16
  138.1 2.2 pad_maximum_fusion
  140.3 2.5 fusion.154
  142.8 4.3 copy.35
  147.0 4.4 reshape.446
  151.4 4.3 copy.33
  155.7 4.5 reshape.443
  160.2 10.1 %fusion.162 = (f32[16,256]{1,0:T(8,128)S(1)}, f32[16,256,1024]{2,1,0:T(8,128)}) fusion(pred[1024]{0:T(1024)(128)(4,1)S(1)} %reshape.444, bf16[256,16,64]{0,2,1:T(8,128)(2,1)S(1)} %bitcast.222, bf16[1024,16,64]{0,2,1:T(8,128)(2,1)} %reshape.446), kind=kOutput, calls=%fused_computation.272 | convolution fusion | flops 553649152 | bytes 19416064 | tf_op jit(solution)/shard_map/sub | solution.py:133
  170.3 10.0 %fusion.63 = bf16[16,64,256]{2,1,0:T(8,128)(2,1)} fusion(bf16[1024,16,64]{0,2,1:T(8,128)(2,1)} %reshape.443, f32[16,256,1024]{2,1,0:T(8,128)} %get-tuple-element.118, f32[16,256]{1,0:T(8,128)S(1)} %get-tuple-element.117), kind=kOutput, calls=%fused_computation.110 | convolution fusion | flops 545521664 | bytes 19415040 | tf_op jit(solution)/shard_map/rhqk,rkhd->rqhd/dot_general | solution.py:136
  180.4 2.6 fusion.77
  183.6 4.3 collective-permute-start.3
  187.9 1.5 collective-permute-start.4
  189.5 4.2 collective-permute-done.4
  193.8 5.4 %fusion.74 = (bf16[1,256,1024]{2,1,0:T(8,128)(2,1)S(1)}, f32[1,256,1024]{2,1,0:T(8,128)S(1)}) fusion(bf16[1,256,1024]{2,1,0:T(8,128)(2,1)} %param.19, f32[1,286,1024]{2,1,0:T(8,128)S(1)} %maximum_convert_fusion, f32[1024]{0:T(1024)S(1)} %bitcast.292, f32[1024]{0:T(1024)S(1)} %bitcast.294, f32[1024]{0:T(1024)S(1)} %bitcast.236, f32[1024]{0:T(1024)S(1)} %bitcast.238, ...), kind=kLoop, calls=%fused_computation.119 | loop fusion | flops 18612224 | bytes 34729984 | tf_op jit(solution)/shard_map/convert_element_type | solution.py:160
  199.2 2.7 collective-permute-start.5
  202.0 1.3 collective-permute-start.6
  203.3 2.4 fusion.109
  205.7 3.2 fusion.110
  208.8 3.1 stack.160
  211.9 14.8 %all-gather.1 = f32[8,31,1024]{2,1,0:T(8,128)} all-gather(f32[1,31,1024]{2,1,0:T(8,128)S(1)} %bitcast.229), channel_id=2, replica_groups=mesh['dp'=8,'ctx'=16] {'dp'}, dimensions={0}, use_global_device_ids=true | all-gather | bytes 1142784 | tf_op jit(solution)/shard_map/all_gather | solution.py:174
  226.7 1.3 reduce_sum.377
  228.2 5.6 %fusion.79 = (f32[256]{0:T(256)S(1)}, f32[256,1024]{1,0:T(8,128)S(1)}) fusion(bf16[256,1024]{1,0:T(8,128)(2,1)S(1)} %get-tuple-element.120, f32[1024]{0:T(1024)S(1)} %copy-done.16, f32[1,286,1024]{2,1,0:T(8,128)S(1)} %maximum_convert_fusion.1, f32[1024]{0:T(1024)S(1)} %bitcast.293, f32[1024]{0:T(1024)S(1)} %bitcast.295, f32[1024]{0:T(1024)S(1)} %bitcast.237, ...), kind=kLoop, calls=%fused_computation.124 | loop fusion | flops 17039104 | bytes 34210816 | tf_op jit(solution)/shard_map/reduce_sum | solution.py:37
  235.4 3.3 convolution_convert_fusion.1
  239.9 22.5 %fusion.29 = bf16[1,16,256,1024]{3,2,1,0:T(8,128)(2,1)} fusion(bf16[256,16,64]{0,2,1:T(8,128)(2,1)S(1)} %bitcast.230, bf16[1024,16,64]{0,2,1:T(8,128)(2,1)} %reshape.443, f32[16,256,1024]{2,1,0:T(8,128)} %get-tuple-element.118, f32[16,256]{1,0:T(8,128)S(1)} %copy-done.26), kind=kOutput, calls=%fused_computation.71 | convolution fusion | flops 1103107072 | bytes 27803648 | tf_op jit(solution)/shard_map/sub | solution.py:198
  262.5 7.2 %fusion.42 = f32[16,64,1024]{2,1,0:T(8,128)S(1)} fusion(bf16[256,16,64]{0,2,1:T(8,128)(2,1)S(1)} %bitcast.231, f32[16,256,1024]{2,1,0:T(8,128)} %get-tuple-element.118, f32[16,256]{1,0:T(8,128)S(1)} %copy-done.26), kind=kOutput, calls=%fused_computation.83 | convolution fusion | flops 545259520 | bytes 21512192 | tf_op jit(solution)/shard_map/dot_general | solution.py:204
  270.1 1.7 copy-done.5
  271.8 2.8 copy-done.2
  274.6 1.6 fusion.16
  276.7 1.5 copy-done.3
  279.2 1.5 pad_maximum_fusion.2
  280.7 3.5 fusion.56
  284.2 1.3 collective-permute-start.7
  286.8 5.2 %collective-permute-start.9 = (bf16[1,2048,256]{2,1,0:T(8,128)(2,1)}, bf16[1,2048,256]{2,1,0:T(8,128)(2,1)S(1)}, u32[]{:S(2)}, u32[]{:S(2)}) collective-permute-start(bf16[1,2048,256]{2,1,0:T(8,128)(2,1)} %pad_maximum_fusion.4), channel_id=1, source_target_pairs={{0,1},{1,2},{2,3},{3,4},{4,5},{5,6},{6,7},{7,8},{8,9},{9,10},{10,1... | collective-permute-start | bytes 3145736 | tf_op jit(solution)/shard_map/ppermute | solution.py:16
  292.0 1.3 slice.686
  293.3 1.3 slice.685
  294.6 17.9 %collective-permute-done.7 = bf16[1,2048,256]{2,1,0:T(8,128)(2,1)S(1)} collective-permute-done((bf16[1,2048,256]{2,1,0:T(8,128)(2,1)}, bf16[1,2048,256]{2,1,0:T(8,128)(2,1)S(1)}, u32[]{:S(2)}, u32[]{:S(2)}) %collective-permute-start.7) | collective-permute-done | bytes 1048608 | tf_op jit(solution)/shard_map/ppermute | solution.py:16
  312.5 5.7 %collective-permute-done.8 = bf16[1,2048,256]{2,1,0:T(8,128)(2,1)S(1)} collective-permute-done((bf16[1,2048,256]{2,1,0:T(8,128)(2,1)}, bf16[1,2048,256]{2,1,0:T(8,128)(2,1)S(1)}, u32[]{:S(2)}, u32[]{:S(2)}) %collective-permute-start.8) | collective-permute-done | bytes 1048608 | tf_op jit(solution)/shard_map/ppermute | solution.py:16
  318.2 1.4 fusion.51
  321.2 4.0 fusion.148
  325.2 4.6 fusion.163
  329.7 62.8 %all-gather.25.cloned.1.call-done = bf16[8,2048,256]{2,1,0:T(8,128)(2,1)} async-done(((bf16[1,2048,256]{2,1,0:T(8,128)(2,1)}), bf16[8,2048,256]{2,1,0:T(8,128)(2,1)}) %all-gather.25.cloned.1.call-update) | async-done | bytes 8388624 | tf_op jit(solution)/shard_map/all_gather | solution.py:239
  392.5 6.4 %convolution_bitcast_fusion = f32[128,2048]{1,0:T(8,128)S(1)} fusion(bf16[8,256,128]{2,1,0:T(8,128)(2,1)S(1)} %bitcast.220, bf16[8,2048,256]{2,1,0:T(8,128)(2,1)} %all-gather.25.cloned.1.call-done), kind=kOutput, calls=%fused_computation.89 | convolution fusion | flops 1073741824 | bytes 9961472 | tf_op jit(solution)/shard_map/nfc,nkf->ck/dot_general | solution.py:240
  398.9 1.6 pad_maximum_fusion.1
  401.7 2.3 fusion.47
  404.1 3.8 fusion.145
  409.1 82.1 %all-reduce.3.cloned.1.call-done = f32[136,4096]{1,0:T(8,128)} async-done(((f32[136,4096]{1,0:T(8,128)}), f32[136,4096]{1,0:T(8,128)}) %all-reduce.3.cloned.1.call-update) | async-done | bytes 2228240 | tf_op jit(solution)/shard_map/psum | solution.py:260
  492.8 1.9 slice.689
  494.6 2.7 slice.688
  (120 shorter events, 23.5 us)
Async XLA Ops:
  7.2 90.8 %copy-start = (s32[16,1]{0,1:T(1,128)S(1)}, s32[16,1]{0,1:T(1,128)}, u32[]{:S(2)}) copy-start(s32[16,1]{0,1:T(1,128)} %param.18) | copy-start | bytes 196
  7.2 28.6 %all-gather.11.cloned.1.call-start = ((), (), s32[]{:S(2)}) async-start(), calls=%async_computation.1 | async-start | bytes 1179648 | tf_op jit(solution)/shard_map/all_gather | solution.py:75
  7.9 74.4 %all-gather.15.cloned.1.call-start = ((), (), s32[]{:S(2)}) async-start(), calls=%async_computation.3 | async-start | bytes 7077888 | tf_op jit(solution)/shard_map/all_gather | solution.py:90
  8.7 171.6 %all-gather.13.cloned.1.call-start = ((), (), s32[]{:S(2)}) async-start(), calls=%async_computation.2 | async-start | bytes 4718592 | tf_op jit(solution)/shard_map/all_gather | solution.py:141
  35.8 4.0 copy-start.24
  61.6 19.2 %copy-start.17 = (f32[1024]{0:T(1024)S(1)}, f32[1024]{0:T(1024)}, u32[]{:S(2)}) copy-start(f32[1024]{0:T(1024)} %param.14) | copy-start | bytes 12292
  80.8 6.2 %copy-start.21 = (f32[256]{0:T(256)}, f32[256]{0:T(256)S(1)}, u32[]{:S(2)}) copy-start(f32[256]{0:T(256)S(1)} %add_rsqrt_fusion.1) | copy-start | bytes 3076
  81.8 17.4 %copy-start.23 = (s32[16,2]{0,1:T(2,128)S(1)}, s32[16,2]{0,1:T(2,128)}, u32[]{:S(2)}) copy-start(s32[16,2]{0,1:T(2,128)} %param.17) | copy-start | bytes 388
  81.8 98.6 %all-gather.17.cloned.1.call-start = ((), (), s32[]{:S(2)}) async-start(), calls=%async_computation.4 | async-start | bytes 2359296 | tf_op jit(solution)/shard_map/all_gather | solution.py:91
  87.1 1.1 copy-start.14
  89.5 26.6 %collective-permute-start.1 = (bf16[1,256,2048]{2,1,0:T(8,128)(2,1)}, bf16[1,256,2048]{2,1,0:T(8,128)(2,1)}, u32[]{:S(2)}, u32[]{:S(2)}) collective-permute-start(bf16[1,256,2048]{2,1,0:T(8,128)(2,1)} %get-tuple-element.73), channel_id=1, source_target_pairs={{0,2},{1,3},{2,4},{3,5},{4,6},{5,7},{6,8},{7,9},{8,10},{9,11},{10,... | collective-permute-start | bytes 3145736 | tf_op jit(solution)/shard_map/ppermute | solution.py:16
  93.2 44.2 %collective-permute-start = (bf16[1,256,2048]{2,1,0:T(8,128)(2,1)}, bf16[1,256,2048]{2,1,0:T(8,128)(2,1)}, u32[]{:S(2)}, u32[]{:S(2)}) collective-permute-start(bf16[1,256,2048]{2,1,0:T(8,128)(2,1)} %get-tuple-element.73), channel_id=1, source_target_pairs={{0,1},{1,2},{2,3},{3,4},{4,5},{5,6},{6,7},{7,8},{8,9},{9,10},{10,1... | collective-permute-start | bytes 3145736 | tf_op jit(solution)/shard_map/ppermute | solution.py:16
  96.6 41.5 %collective-permute-start.2 = (bf16[1,256,2048]{2,1,0:T(8,128)(2,1)}, bf16[1,256,2048]{2,1,0:T(8,128)(2,1)}, u32[]{:S(2)}, u32[]{:S(2)}) collective-permute-start(bf16[1,256,2048]{2,1,0:T(8,128)(2,1)} %get-tuple-element.73), channel_id=1, source_target_pairs={{1,0},{2,1},{3,2},{4,3},{5,4},{6,5},{7,6},{8,7},{9,8},{10,9},{11,1... | collective-permute-start | bytes 3145736 | tf_op jit(solution)/shard_map/ppermute | solution.py:16
  98.0 137.1 %all-gather.19.cloned.1.call-start = ((), (), s32[]{:S(2)}) async-start(), calls=%async_computation.5 | async-start | bytes 4718592 | tf_op jit(solution)/shard_map/all_gather | solution.py:180
  102.7 57.4 %copy-start.8 = (bf16[1,256,1024]{1,2,0:T(8,128)(2,1)}, bf16[1,256,1024]{1,2,0:T(8,128)(2,1)S(1)}, u32[]{:S(2)}) copy-start(bf16[1,256,1024]{1,2,0:T(8,128)(2,1)S(1)} %copy.34) | copy-start | bytes 1572868
  170.3 10.0 %copy-start.25 = (f32[16,256]{1,0:T(8,128)}, f32[16,256]{1,0:T(8,128)S(1)}, u32[]{:S(2)}) copy-start(f32[16,256]{1,0:T(8,128)S(1)} %get-tuple-element.117) | copy-start | bytes 49156
  170.3 10.0 %copy-start.15 = (f32[31,1024]{1,0:T(8,128)S(1)}, f32[31,1024]{1,0:T(8,128)}, u32[]{:S(2)}) copy-start(f32[31,1024]{1,0:T(8,128)} %param.16) | copy-start | bytes 380932
  180.2 2.8 copy-start.16
  180.3 103.9 %all-gather.21.cloned.1.call-start = ((), (), s32[]{:S(2)}) async-start(), calls=%async_computation.6 | async-start | bytes 4718592 | tf_op jit(solution)/shard_map/all_gather | solution.py:190
  183.0 0.6 copy-start.19
  183.6 5.8 %collective-permute-start.3 = (bf16[1,15,1024]{2,1,0:T(8,128)(2,1)S(1)}, bf16[1,15,1024]{2,1,0:T(8,128)(2,1)S(1)}, u32[]{:S(2)}, u32[]{:S(2)}) collective-permute-start(bf16[1,15,1024]{2,1,0:T(8,128)(2,1)S(1)} %get-tuple-element.76), channel_id=1, source_target_pairs={{0,1},{1,2},{2,3},{3,4},{4,5},{5,6},{6,7},{7,8},{8,9},{9,10},{10,1... | collective-permute-start | bytes 92168 | tf_op jit(solution)/shard_map/ppermute | solution.py:24
  187.9 5.8 %collective-permute-start.4 = (bf16[1,15,1024]{2,1,0:T(8,128)(2,1)S(1)}, bf16[1,15,1024]{2,1,0:T(8,128)(2,1)S(1)}, u32[]{:S(2)}, u32[]{:S(2)}) collective-permute-start(bf16[1,15,1024]{2,1,0:T(8,128)(2,1)S(1)} %get-tuple-element.77), channel_id=1, source_target_pairs={{1,0},{2,1},{3,2},{4,3},{5,4},{6,5},{7,6},{8,7},{9,8},{10,9},{11,1... | collective-permute-start | bytes 92168 | tf_op jit(solution)/shard_map/ppermute | solution.py:27
  199.2 28.7 %collective-permute-start.5 = (bf16[1,15,1024]{2,1,0:T(8,128)(2,1)S(1)}, bf16[1,15,1024]{2,1,0:T(8,128)(2,1)S(1)}, u32[]{:S(2)}, u32[]{:S(2)}) collective-permute-start(bf16[1,15,1024]{2,1,0:T(8,128)(2,1)S(1)} %get-tuple-element.74), channel_id=1, source_target_pairs={{0,1},{1,2},{2,3},{3,4},{4,5},{5,6},{6,7},{7,8},{8,9},{9,10},{10,1... | collective-permute-start | bytes 92168 | tf_op jit(solution)/shard_map/ppermute | solution.py:24
  202.0 26.0 %collective-permute-start.6 = (bf16[1,15,1024]{2,1,0:T(8,128)(2,1)S(1)}, bf16[1,15,1024]{2,1,0:T(8,128)(2,1)S(1)}, u32[]{:S(2)}, u32[]{:S(2)}) collective-permute-start(bf16[1,15,1024]{2,1,0:T(8,128)(2,1)S(1)} %get-tuple-element.75), channel_id=1, source_target_pairs={{1,0},{2,1},{3,2},{4,3},{5,4},{6,5},{7,6},{8,7},{9,8},{10,9},{11,1... | collective-permute-start | bytes 92168 | tf_op jit(solution)/shard_map/ppermute | solution.py:27
  228.1 5.7 %copy-start.10 = (bf16[1,256,1024]{2,1,0:T(8,128)(2,1)S(1)}, bf16[1,256,1024]{2,1,0:T(8,128)(2,1)}, u32[]{:S(2)}) copy-start(bf16[1,256,1024]{2,1,0:T(8,128)(2,1)} %param.19) | copy-start | bytes 1572868
  228.2 5.7 %copy-start.20 = (f32[256]{0:T(256)S(1)}, f32[256]{0:T(256)}, u32[]{:S(2)}) copy-start(f32[256]{0:T(256)} %copy-done.19) | copy-start | bytes 3076
  233.8 6.1 %copy-start.26 = (f32[16,256]{1,0:T(8,128)S(1)}, f32[16,256]{1,0:T(8,128)}, u32[]{:S(2)}) copy-start(f32[16,256]{1,0:T(8,128)} %copy-done.25) | copy-start | bytes 49156
  235.1 90.1 %all-gather.23.cloned.1.call-start = ((), (), s32[]{:S(2)}) async-start(), calls=%async_computation.7 | async-start | bytes 4718592 | tf_op jit(solution)/shard_map/all_gather | solution.py:235
  269.7 2.1 copy-start.5
  269.7 4.9 copy-start.2
  269.7 4.9 copy-start.9
  276.2 2.0 copy-start.3
  276.5 4.1 copy-start.4
  284.2 108.3 %all-gather.25.cloned.1.call-start = ((), (), s32[]{:S(2)}) async-start(), calls=%async_computation.8 | async-start | bytes 9437184 | tf_op jit(solution)/shard_map/all_gather | solution.py:239
  284.2 28.3 %collective-permute-start.7 = (bf16[1,2048,256]{2,1,0:T(8,128)(2,1)}, bf16[1,2048,256]{2,1,0:T(8,128)(2,1)S(1)}, u32[]{:S(2)}, u32[]{:S(2)}) collective-permute-start(bf16[1,2048,256]{2,1,0:T(8,128)(2,1)} %get-tuple-element.20), channel_id=1, source_target_pairs={{1,0},{2,1},{3,2},{4,3},{5,4},{6,5},{7,6},{8,7},{9,8},{10,9},{11,1... | collective-permute-start | bytes 3145736 | tf_op jit(solution)/shard_map/ppermute | solution.py:16
  285.5 32.7 %collective-permute-start.8 = (bf16[1,2048,256]{2,1,0:T(8,128)(2,1)}, bf16[1,2048,256]{2,1,0:T(8,128)(2,1)S(1)}, u32[]{:S(2)}, u32[]{:S(2)}) collective-permute-start(bf16[1,2048,256]{2,1,0:T(8,128)(2,1)} %get-tuple-element.21), channel_id=1, source_target_pairs={{2,0},{3,1},{4,2},{5,3},{6,4},{7,5},{8,6},{9,7},{10,8},{11,9},{12,... | collective-permute-start | bytes 3145736 | tf_op jit(solution)/shard_map/ppermute | solution.py:16
  286.8 31.4 %collective-permute-start.9 = (bf16[1,2048,256]{2,1,0:T(8,128)(2,1)}, bf16[1,2048,256]{2,1,0:T(8,128)(2,1)S(1)}, u32[]{:S(2)}, u32[]{:S(2)}) collective-permute-start(bf16[1,2048,256]{2,1,0:T(8,128)(2,1)} %pad_maximum_fusion.4), channel_id=1, source_target_pairs={{0,1},{1,2},{2,3},{3,4},{4,5},{5,6},{6,7},{7,8},{8,9},{9,10},{10,1... | collective-permute-start | bytes 3145736 | tf_op jit(solution)/shard_map/ppermute | solution.py:16
  319.7 171.5 %all-reduce.3.cloned.1.call-start = ((), (), s32[]{:S(2)}) async-start(), calls=%async_computation.9 | async-start | bytes 4456448 | tf_op jit(solution)/shard_map/psum | solution.py:260
  392.5 6.4 %copy-start.11 = (f32[128,1024]{1,0:T(8,128)S(1)}, f32[128,1024]{1,0:T(8,128)}, u32[]{:S(2)}) copy-start(f32[128,1024]{1,0:T(8,128)} %fusion.163) | copy-start | bytes 1572868
  392.5 6.4 %copy-start.12 = (f32[128,1024]{1,0:T(8,128)S(1)}, f32[128,1024]{1,0:T(8,128)}, u32[]{:S(2)}) copy-start(f32[128,1024]{1,0:T(8,128)} %fusion.148) | copy-start | bytes 1572868
  398.9 2.8 copy-start.13
  400.5 3.5 copy-start.18
  400.5 3.5 copy-start.7
  404.0 3.8 copy-start.6
  404.1 3.8 copy-start.22
  404.1 93.3 %copy-start.1 = (s32[16,1]{0,1:T(1,128)S(1)}, s32[16,1]{0,1:T(1,128)}, u32[]{:S(2)}) copy-start(s32[16,1]{0,1:T(1,128)} %param.18) | copy-start | bytes 196
Sparse Core Ops, SparseCore 0:
  9.7 26.0 all-gather.10
  37.5 41.9 all-gather.14
  81.9 32.0 all-gather.12
  115.6 25.1 all-gather.16
  180.4 36.8 all-gather.18
  235.2 35.3 all-gather.20
  284.3 39.0 all-gather.22
  325.7 66.7 all-gather.24
  400.6 90.4 all-reduce.2

commit v9 on v8

--- a/solution.py
+++ b/solution.py
@@ -98,24 +98,27 @@
     normed = (features * attn_inverse * attn_gain).astype(jnp.bfloat16)
     projected = jnp.dot(normed, weight_qkv, preferred_element_type=jnp.float32).astype(jnp.bfloat16)
     projected = projected.reshape(recordings, frames_dev, 3 * model_width)
-    own_pairs = projected[:, :, model_width:]
     ctx_index = lax.axis_index("ctx")
     back_row = lax.dynamic_index_in_dim(back_list, ctx_index, 0, keepdims=False)
     ahead_row = lax.dynamic_index_in_dim(ahead_list, ctx_index, 0, keepdims=False)
     offsets = [-(step + 1) for step in range(back_list.shape[1])] + [1]
     listed_items = [jnp.array(True)]
-    pair_blocks = [own_pairs]
+    own_keys = projected[:, :, model_width : 2 * model_width]
+    own_values = projected[:, :, 2 * model_width :]
+    key_blocks = [own_keys]
+    value_blocks = [own_values]
     for offset in offsets:
         list_row = back_row if offset < 0 else ahead_row
         listed_items.append(jnp.any(list_row == ctx_index + offset))
-        pair_blocks.append(from_behind(own_pairs, "ctx", -offset))
+        key_blocks.append(from_behind(own_keys, "ctx", -offset))
+    for offset in offsets:
+        value_blocks.append(from_behind(own_values, "ctx", -offset))
     listed = jnp.stack(listed_items)
-    seen_count = len(pair_blocks)
-    stacked = jnp.stack(pair_blocks, axis=1)
-    key_all = stacked[..., :model_width].reshape(
+    seen_count = len(key_blocks)
+    key_all = jnp.stack(key_blocks, axis=1).reshape(
         recordings, seen_count, frames_dev, head_count, head_size
     )
-    value_all = stacked[..., model_width:].reshape(
+    value_all = jnp.stack(value_blocks, axis=1).reshape(
         recordings, seen_count, frames_dev, head_count, head_size
     )
     query_all = projected[:, :, :model_width].reshape(recordings, frames_dev, head_count, head_size)
@@ -171,7 +174,10 @@
             :, start_row : start_row + frames_dev
         ]
     kernel_rows = jnp.stack(kernel_list)
-    kernel_dp = jnp.sum(lax.all_gather(kernel_rows, "dp"), axis=0)
+    kernel_high = lax.reduce_precision(kernel_rows, exponent_bits=8, mantissa_bits=7)
+    kernel_parts = jnp.concatenate(
+        [kernel_high.astype(jnp.bfloat16), (kernel_rows - kernel_high).astype(jnp.bfloat16)], axis=0
+    )
     grad_middle = (
         upstream.reshape(-1, model_width)
         + norm_back(middle_wide, conv_inverse, conv_gain, grad_input.reshape(-1, model_width))
@@ -218,9 +224,7 @@
     grad_query = jnp.einsum(
         "rhqk,rkhd->rqhd", scores_for_query, key_flat, preferred_element_type=jnp.float32
     )
-    kernel_dp, middle_rows, grad_query = lax.optimization_barrier(
-        (kernel_dp, middle_rows, grad_query)
-    )
+    middle_rows, grad_query = lax.optimization_barrier((middle_rows, grad_query))
     grad_wout = lax.dot_general(
         mixed_columns, middle_rows, contract_rows, preferred_element_type=jnp.float32
     )
@@ -232,7 +236,18 @@
         pair_total = pair_total + arrived.astype(jnp.float32)
     pair_low = pair_total.astype(jnp.bfloat16)
     normed_columns = lax.dynamic_slice_in_dim(normed_all, dp_index * shard_width, shard_width, 1)
-    query_rows = lax.all_gather(grad_query, "dp", axis=0, tiled=True)
+    query_width = grad_query.shape[0]
+    query_block = jnp.concatenate([grad_query, kernel_parts], axis=0)
+    query_block = jnp.pad(query_block, ((0, (-query_block.shape[0]) % 16), (0, 0)))
+    query_gathered = lax.all_gather(query_block[None], "dp", axis=0, tiled=True)
+    query_rows = query_gathered[:, :query_width].reshape(-1, model_width)
+    kernel_dp = jnp.sum(
+        query_gathered[:, query_width : query_width + tap_count].astype(jnp.float32)
+        + query_gathered[:, query_width + tap_count : query_width + 2 * tap_count].astype(
+            jnp.float32
+        ),
+        axis=0,
+    )
     grad_wq = lax.dot_general(
         normed_columns, query_rows, contract_rows, preferred_element_type=jnp.float32
     )

time: 514 us -> 508 us (0.988)
  blocking collectives: 57.3 us -> 42.6 us
  local copies, waits for them, and re-layouts: 45.7 us -> 34.5 us
  waiting for transfers between devices: 213 us -> 223 us
  starting transfers between devices: 27.2 us -> 35.8 us
    all_gather x1, waiting for transfers between devices: 0.01 us -> 32.2 us  [on_device(): query_gathered = lax.all_gather(query_block[None], 'dp', axis=0, tiled=True)]
    ppermute x6 -> x9, waiting for transfers between devices: 59 us -> 41.1 us  [from_behind(): lax.ppermute(value, axis, [(source, source + steps) for source in range(f...]
    all_gather x1 -> x0, blocking collectives: 14.8 us -> none  [on_device(): kernel_dp = jnp.sum(lax.all_gather(kernel_rows, 'dp'), axis=0)]
    ppermute x6 -> x9, starting transfers between devices: 16.2 us -> 24.8 us  [from_behind(): lax.ppermute(value, axis, [(source, source + steps) for source in range(f...]
    slice x3 -> x1, local copies, waits for them, and re-layouts: 11 us -> 2.63 us  [on_device(): query_rows = query_gathered[:, :query_width].reshape(-1, model_width)]
    all_gather x1, waiting for transfers between devices: 62.8 us -> 54.8 us  [on_device(): pair_rows = lax.all_gather(pair_low, 'dp', axis=0, tiled=True)]
    another operation x3 -> x5, local copies, waits for them, and re-layouts: 10.1 us -> 15.6 us
  transfers between devices with their start and end apart: 19 -> 22, of which waited for: 10 -> 16; matrix products, arithmetic and copies ran while one was open for 34% -> 33% of each run, Pallas kernels for 0% -> 0%
where the time goes in v9:
time: 508 us; the launch traced here: 498 us
  waiting for transfers between devices  223 us (44%)
  matrix products  110 us (22%)
  blocking collectives  42.6 us (8%)
  other arithmetic  35.9 us (7%)
  starting transfers between devices  35.8 us (7%)
  local copies, waits for them, and re-layouts  34.5 us (7%)
  between operations  15.4 us (3%)
    psum x1, waiting for transfers between devices, on_device(): lax.psum(jnp.concatenate([weight_rows, kernel_padded.reshape(-1, row_widt...  80.7 us
    all_gather x1, waiting for transfers between devices, on_device(): pair_rows = lax.all_gather(pair_low, 'dp', axis=0, tiled=True)  54.8 us
    ppermute x9, waiting for transfers between devices, from_behind(): lax.ppermute(value, axis, [(source, source + steps) for source in range(f...  41.1 us
    all_gather x1, waiting for transfers between devices, on_device(): query_gathered = lax.all_gather(query_block[None], 'dp', axis=0, tiled=True)  32.2 us
    dot_general x8, matrix products, on_device(): lax.dot_general(table_whole[codebook], picks, (((0,), (0,)), ((), ())), p...  25.8 us
    ppermute x9, starting transfers between devices, from_behind(): lax.ppermute(value, axis, [(source, source + steps) for source in range(f...  24.8 us
    all_gather x1, blocking collectives, on_device(): ids_whole = lax.all_gather(ids, 'ctx', axis=1, tiled=True)  24 us
    sub x1, matrix products, on_device(): grad_probs - row_sum  20.8 us
  transfers between devices with their start and end apart: 22, of which 16 were waited for; matrix products, arithmetic and copies ran while one was open for 33% of the time, Pallas kernels for 0%

profile of v9, /device:TPU:0, one launch (start us, length us, event | category | flops | bytes accessed | tf_op | source)
XLA Modules:
  0.0 497.9 jit_solution(14414354917880197956)
XLA Ops:
  8.7 24.0 %all_gather.27 = s32[1,4096,8]{1,2,0:T(8,128)S(1)} all-gather(s32[1,256,8]{1,2,0:T(8,128)} %param.10), channel_id=1, replica_groups=mesh['dp'=8,'ctx'=16] {'ctx'}, dimensions={1}, use_global_device_ids=true | all-gather | bytes 139264 | tf_op jit(solution)/shard_map/all_gather | solution.py:74
  32.8 2.9 all-gather.10.cloned.1.call-done
  35.8 4.0 fusion.3
  39.8 3.1 fusion.38
  42.9 3.1 fusion.37
  46.0 3.1 fusion.36
  49.0 3.3 fusion.35
  52.3 3.1 fusion.34
  55.4 3.1 fusion.33
  58.5 3.1 fusion.39
  61.7 18.5 %all_to_all.4 = bf16[64,16,256]{2,0,1:T(8,128)(2,1)S(1)} all-to-all(bf16[64,16,256]{2,0,1:T(8,128)(2,1)S(1)} %bitcast.235), channel_id=1, replica_groups=mesh['dp'=8,'ctx'=16] {'ctx'}, dimensions={1} | all-to-all | bytes 1048576 | tf_op jit(solution)/shard_map/all_to_all | solution.py:87
  82.8 4.8 fusion.46
  88.9 2.7 collective-permute-start.4
  91.7 2.5 collective-permute-start.3
  95.5 6.2 %collective-permute-start.1 = (bf16[1,256,1024]{2,1,0:T(8,128)(2,1)}, bf16[1,256,1024]{2,1,0:T(8,128)(2,1)}, u32[]{:S(2)}, u32[]{:S(2)}) collective-permute-start(bf16[1,256,1024]{2,1,0:T(8,128)(2,1)} %get-tuple-element.72), channel_id=1, source_target_pairs={{0,2},{1,3},{2,4},{3,5},{4,6},{5,7},{6,8},{7,9},{8,10},{9,11},{10,... | collective-permute-start | bytes 1572872 | tf_op jit(solution)/shard_map/ppermute | solution.py:16
  101.8 3.3 collective-permute-start
  108.5 1.3 pad_add_fusion
  111.0 4.3 collective-permute-done.3
  116.4 1.8 pad_maximum_fusion.2
  118.1 2.7 copy.36
  120.8 4.4 reshape.449
  125.2 1.4 collective-permute-done.1
  126.6 10.1 %collective-permute-done = bf16[1,256,1024]{2,1,0:T(8,128)(2,1)} collective-permute-done((bf16[1,256,1024]{2,1,0:T(8,128)(2,1)}, bf16[1,256,1024]{2,1,0:T(8,128)(2,1)}, u32[]{:S(2)}, u32[]{:S(2)}) %collective-permute-start) | collective-permute-done | bytes 524320 | tf_op jit(solution)/shard_map/ppermute | solution.py:16
  136.8 1.8 pad_maximum_fusion.1
  138.6 2.7 copy.34
  141.3 4.6 reshape.446
  145.9 9.9 %fusion.167 = (f32[16,256]{1,0:T(8,128)S(1)}, f32[16,256,1024]{2,1,0:T(8,128)}) fusion(pred[1024]{0:T(1024)(128)(4,1)S(1)} %reshape.447, bf16[256,16,64]{0,2,1:T(8,128)(2,1)} %bitcast.231, bf16[1024,16,64]{0,2,1:T(8,128)(2,1)S(1)} %copy-done.3), kind=kOutput, calls=%fused_computation.283 | convolution fusion | flops 553649152 | bytes 19416064 | tf_op jit(solution)/shard_map/sub | solution.py:136
  155.8 10.0 %fusion.66 = bf16[16,64,256]{2,1,0:T(8,128)(2,1)} fusion(bf16[1024,16,64]{0,2,1:T(8,128)(2,1)} %reshape.446, f32[16,256,1024]{2,1,0:T(8,128)} %get-tuple-element.119, f32[16,256]{1,0:T(8,128)S(1)} %get-tuple-element.118), kind=kOutput, calls=%fused_computation.115 | convolution fusion | flops 545521664 | bytes 19415040 | tf_op jit(solution)/shard_map/rhqk,rkhd->rqhd/dot_general | solution.py:139
  165.9 2.6 fusion.80
  168.7 4.3 collective-permute-start.6
  173.0 1.5 collective-permute-start.7
  174.6 4.2 collective-permute-done.7
  179.0 6.2 %fusion.77 = (bf16[1,256,1024]{2,1,0:T(8,128)(2,1)S(1)}, f32[1,256,1024]{2,1,0:T(8,128)}) fusion(bf16[1,256,1024]{2,1,0:T(8,128)(2,1)} %param.19, f32[1,286,1024]{2,1,0:T(8,128)S(1)} %maximum_convert_fusion, f32[1024]{0:T(1024)S(1)} %bitcast.302, f32[1024]{0:T(1024)S(1)} %bitcast.304, f32[1024]{0:T(1024)S(1)} %bitcast.246, f32[1024]{0:T(1024)S(1)} %bitcast.248, ...), kind=kLoop, calls=%fused_computation.124 | loop fusion | flops 18612224 | bytes 34729984 | tf_op jit(solution)/shard_map/convert_element_type | solution.py:163
  185.2 3.2 collective-permute-start.8
  190.0 4.2 collective-permute-done.9
  194.4 5.6 %fusion.82 = (f32[256]{0:T(256)S(1)}, f32[256,1024]{1,0:T(8,128)S(1)}) fusion(bf16[256,1024]{1,0:T(8,128)(2,1)S(1)} %get-tuple-element.121, f32[1024]{0:T(1024)S(1)} %copy-done.13, f32[1,286,1024]{2,1,0:T(8,128)S(1)} %maximum_convert_fusion.1, f32[1024]{0:T(1024)S(1)} %bitcast.303, f32[1024]{0:T(1024)S(1)} %bitcast.305, f32[1024]{0:T(1024)S(1)} %bitcast.247, ...), kind=kLoop, calls=%fused_computation.129 | loop fusion | flops 17039104 | bytes 34210816 | tf_op jit(solution)/shard_map/reduce_sum | solution.py:37
  202.5 3.3 convolution_convert_fusion.1
  205.8 2.0 copy.37
  207.9 20.8 %fusion.29 = bf16[1,16,256,1024]{3,2,1,0:T(8,128)(2,1)} fusion(bf16[256,16,64]{0,2,1:T(8,128)(2,1)} %bitcast.238, bf16[1024,16,64]{0,2,1:T(8,128)(2,1)} %reshape.446, f32[16,256,1024]{2,1,0:T(8,128)} %get-tuple-element.119, f32[16,256]{1,0:T(8,128)S(1)} %get-tuple-element.118), kind=kOutput, calls=%fused_computation.71 | convolution fusion | flops 1103107072 | bytes 27803648 | tf_op jit(solution)/shard_map/sub | solution.py:204
  228.7 7.1 %fusion.42 = f32[16,64,1024]{2,1,0:T(8,128)S(1)} fusion(bf16[256,16,64]{0,2,1:T(8,128)(2,1)} %bitcast.239, f32[16,256,1024]{2,1,0:T(8,128)} %get-tuple-element.119, f32[16,256]{1,0:T(8,128)S(1)} %get-tuple-element.118), kind=kOutput, calls=%fused_computation.82 | convolution fusion | flops 545259520 | bytes 21512192 | tf_op jit(solution)/shard_map/dot_general | solution.py:210
  236.2 3.0 copy-done.2
  239.2 1.6 fusion.16
  242.8 1.5 collective-permute-start.11
  244.3 4.6 collective-permute-start.12
  249.2 19.6 %collective-permute-done.10 = bf16[1,2048,256]{2,1,0:T(8,128)(2,1)S(1)} collective-permute-done((bf16[1,2048,256]{2,1,0:T(8,128)(2,1)S(1)}, bf16[1,2048,256]{2,1,0:T(8,128)(2,1)S(1)}, u32[]{:S(2)}, u32[]{:S(2)}) %collective-permute-start.10) | collective-permute-done | bytes 1048608 | tf_op jit(solution)/shard_map/ppermute | solution.py:16
  268.7 4.6 collective-permute-done.11
  273.3 1.4 fusion.51
  274.8 1.8 fusion.112
  276.6 2.5 fusion.113
  279.4 6.7 %fusion.56 = bf16[1,256,16,64]{1,3,2,0:T(8,128)(2,1)S(1)} fusion(bf16[1024,16,64]{0,2,1:T(8,128)(2,1)} %reshape.449, bf16[1,16,256,1024]{3,2,1,0:T(8,128)(2,1)} %fusion.29), kind=kOutput, calls=%fused_computation.104 | convolution fusion | flops 536870912 | bytes 11010048 | tf_op jit(solution)/shard_map/rhqk,rkhd->rqhd/dot_general | solution.py:224
  288.5 3.9 fusion.153
  292.3 54.8 %all-gather.22.cloned.1.call-done = bf16[8,2048,256]{2,1,0:T(8,128)(2,1)} async-done(((bf16[1,2048,256]{2,1,0:T(8,128)(2,1)}), bf16[8,2048,256]{2,1,0:T(8,128)(2,1)}) %all-gather.22.cloned.1.call-update) | async-done | bytes 8388624 | tf_op jit(solution)/shard_map/all_gather | solution.py:254
  347.1 6.3 %convolution_bitcast_fusion = f32[128,2048]{1,0:T(8,128)S(1)} fusion(bf16[8,256,128]{2,1,0:T(8,128)(2,1)S(1)} %bitcast.229, bf16[8,2048,256]{2,1,0:T(8,128)(2,1)} %all-gather.22.cloned.1.call-done), kind=kOutput, calls=%fused_computation.88 | convolution fusion | flops 1073741824 | bytes 9961472 | tf_op jit(solution)/shard_map/nfc,nkf->ck/dot_general | solution.py:255
  353.4 32.2 %all-gather.24.cloned.1.call-done = bf16[2560,1024]{1,0:T(8,128)(2,1)} async-done(((bf16[320,1024]{1,0:T(8,128)(2,1)}), bf16[2560,1024]{1,0:T(8,128)(2,1)}) %all-gather.24.cloned.1.call-update) | async-done | bytes 5242896 | tf_op jit(solution)/shard_map/all_gather | solution.py:242
  385.6 1.5 add_reduce_fusion
  387.1 2.6 slice.695
  389.7 1.6 fusion.168
  391.4 2.8 pad_maximum_fusion
  394.2 2.5 fusion.79
  396.7 2.3 fusion.47
  399.1 3.8 fusion.148
  404.1 80.7 %all-reduce.4.cloned.1.call-done = f32[136,4096]{1,0:T(8,128)} async-done(((f32[136,4096]{1,0:T(8,128)}), f32[136,4096]{1,0:T(8,128)}) %all-reduce.4.cloned.1.call-update) | async-done | bytes 2228240 | tf_op jit(solution)/shard_map/psum | solution.py:275
  486.4 1.9 slice.699
  488.3 2.7 slice.698
  (114 shorter events, 24.9 us)
Async XLA Ops:
  7.2 99.3 %copy-start = (s32[16,1]{0,1:T(1,128)S(1)}, s32[16,1]{0,1:T(1,128)}, u32[]{:S(2)}) copy-start(s32[16,1]{0,1:T(1,128)} %param.18) | copy-start | bytes 196
  7.2 28.6 %all-gather.10.cloned.1.call-start = ((), (), s32[]{:S(2)}) async-start(), calls=%async_computation.1 | async-start | bytes 1179648 | tf_op jit(solution)/shard_map/all_gather | solution.py:75
  7.9 74.9 %all-gather.14.cloned.1.call-start = ((), (), s32[]{:S(2)}) async-start(), calls=%async_computation.3 | async-start | bytes 7077888 | tf_op jit(solution)/shard_map/all_gather | solution.py:90
  8.7 157.1 %all-gather.12.cloned.1.call-start = ((), (), s32[]{:S(2)}) async-start(), calls=%async_computation.2 | async-start | bytes 4718592 | tf_op jit(solution)/shard_map/all_gather | solution.py:144
  35.8 4.0 copy-start.19
  61.6 19.8 %copy-start.14 = (f32[1024]{0:T(1024)S(1)}, f32[1024]{0:T(1024)}, u32[]{:S(2)}) copy-start(f32[1024]{0:T(1024)} %param.14) | copy-start | bytes 12292
  80.8 0.6 copy-start.16
  82.4 83.5 %all-gather.16.cloned.1.call-start = ((), (), s32[]{:S(2)}) async-start(), calls=%async_computation.4 | async-start | bytes 2359296 | tf_op jit(solution)/shard_map/all_gather | solution.py:91
  87.6 20.1 %copy-start.18 = (s32[16,2]{0,1:T(2,128)S(1)}, s32[16,2]{0,1:T(2,128)}, u32[]{:S(2)}) copy-start(s32[16,2]{0,1:T(2,128)} %param.17) | copy-start | bytes 388
  88.9 16.2 %collective-permute-start.4 = (bf16[1,256,1024]{2,1,0:T(8,128)(2,1)S(1)}, bf16[1,256,1024]{2,1,0:T(8,128)(2,1)S(1)}, u32[]{:S(2)}, u32[]{:S(2)}) collective-permute-start(bf16[1,256,1024]{2,1,0:T(8,128)(2,1)S(1)} %get-tuple-element.70), channel_id=1, source_target_pairs={{0,2},{1,3},{2,4},{3,5},{4,6},{5,7},{6,8},{7,9},{8,10},{9,11},{10,... | collective-permute-start | bytes 1572872 | tf_op jit(solution)/shard_map/ppermute | solution.py:16
  91.7 23.6 %collective-permute-start.3 = (bf16[1,256,1024]{2,1,0:T(8,128)(2,1)S(1)}, bf16[1,256,1024]{2,1,0:T(8,128)(2,1)S(1)}, u32[]{:S(2)}, u32[]{:S(2)}) collective-permute-start(bf16[1,256,1024]{2,1,0:T(8,128)(2,1)S(1)} %get-tuple-element.70), channel_id=1, source_target_pairs={{0,1},{1,2},{2,3},{3,4},{4,5},{5,6},{6,7},{7,8},{8,9},{9,10},{10,1... | collective-permute-start | bytes 1572872 | tf_op jit(solution)/shard_map/ppermute | solution.py:16
  94.2 22.2 %collective-permute-start.5 = (bf16[1,256,1024]{2,1,0:T(8,128)(2,1)S(1)}, bf16[1,256,1024]{2,1,0:T(8,128)(2,1)}, u32[]{:S(2)}, u32[]{:S(2)}) collective-permute-start(bf16[1,256,1024]{2,1,0:T(8,128)(2,1)S(1)} %get-tuple-element.70), channel_id=1, source_target_pairs={{1,0},{2,1},{3,2},{4,3},{5,4},{6,5},{7,6},{8,7},{9,8},{10,9},{11,1... | collective-permute-start | bytes 1572872 | tf_op jit(solution)/shard_map/ppermute | solution.py:16
  95.5 106.9 %all-gather.18.cloned.1.call-start = ((), (), s32[]{:S(2)}) async-start(), calls=%async_computation.5 | async-start | bytes 4718592 | tf_op jit(solution)/shard_map/all_gather | solution.py:186
  95.5 31.1 %collective-permute-start.1 = (bf16[1,256,1024]{2,1,0:T(8,128)(2,1)}, bf16[1,256,1024]{2,1,0:T(8,128)(2,1)}, u32[]{:S(2)}, u32[]{:S(2)}) collective-permute-start(bf16[1,256,1024]{2,1,0:T(8,128)(2,1)} %get-tuple-element.72), channel_id=1, source_target_pairs={{0,2},{1,3},{2,4},{3,5},{4,6},{5,7},{6,8},{7,9},{8,10},{9,11},{10,... | collective-permute-start | bytes 1572872 | tf_op jit(solution)/shard_map/ppermute | solution.py:16
  101.8 34.9 %collective-permute-start = (bf16[1,256,1024]{2,1,0:T(8,128)(2,1)}, bf16[1,256,1024]{2,1,0:T(8,128)(2,1)}, u32[]{:S(2)}, u32[]{:S(2)}) collective-permute-start(bf16[1,256,1024]{2,1,0:T(8,128)(2,1)} %get-tuple-element.72), channel_id=1, source_target_pairs={{0,1},{1,2},{2,3},{3,4},{4,5},{5,6},{6,7},{7,8},{8,9},{9,10},{10,1... | collective-permute-start | bytes 1572872 | tf_op jit(solution)/shard_map/ppermute | solution.py:16
  105.1 11.2 %copy-start.10 = (bf16[1,256,1024]{2,1,0:T(8,128)(2,1)}, bf16[1,256,1024]{2,1,0:T(8,128)(2,1)S(1)}, u32[]{:S(2)}) copy-start(bf16[1,256,1024]{2,1,0:T(8,128)(2,1)S(1)} %collective-permute-done.4) | copy-start | bytes 1572868
  105.1 31.7 %collective-permute-start.2 = (bf16[1,256,1024]{2,1,0:T(8,128)(2,1)}, bf16[1,256,1024]{2,1,0:T(8,128)(2,1)}, u32[]{:S(2)}, u32[]{:S(2)}) collective-permute-start(bf16[1,256,1024]{2,1,0:T(8,128)(2,1)} %get-tuple-element.72), channel_id=1, source_target_pairs={{1,0},{2,1},{3,2},{4,3},{5,4},{6,5},{7,6},{8,7},{9,8},{10,9},{11,1... | collective-permute-start | bytes 1572872 | tf_op jit(solution)/shard_map/ppermute | solution.py:16
  115.2 1.1 copy-start.11
  141.3 4.6 copy-start.3
  155.8 10.0 %copy-start.12 = (f32[31,1024]{1,0:T(8,128)S(1)}, f32[31,1024]{1,0:T(8,128)}, u32[]{:S(2)}) copy-start(f32[31,1024]{1,0:T(8,128)} %param.16) | copy-start | bytes 380932
  165.7 2.8 copy-start.13
  165.8 120.4 %all-gather.20.cloned.1.call-start = ((), (), s32[]{:S(2)}) async-start(), calls=%async_computation.6 | async-start | bytes 4718592 | tf_op jit(solution)/shard_map/all_gather | solution.py:196
  168.7 5.9 %collective-permute-start.6 = (bf16[1,15,1024]{2,1,0:T(8,128)(2,1)S(1)}, bf16[1,15,1024]{2,1,0:T(8,128)(2,1)S(1)}, u32[]{:S(2)}, u32[]{:S(2)}) collective-permute-start(bf16[1,15,1024]{2,1,0:T(8,128)(2,1)S(1)} %get-tuple-element.75), channel_id=1, source_target_pairs={{0,1},{1,2},{2,3},{3,4},{4,5},{5,6},{6,7},{7,8},{8,9},{9,10},{10,1... | collective-permute-start | bytes 92168 | tf_op jit(solution)/shard_map/ppermute | solution.py:24
  173.0 5.8 %collective-permute-start.7 = (bf16[1,15,1024]{2,1,0:T(8,128)(2,1)S(1)}, bf16[1,15,1024]{2,1,0:T(8,128)(2,1)S(1)}, u32[]{:S(2)}, u32[]{:S(2)}) collective-permute-start(bf16[1,15,1024]{2,1,0:T(8,128)(2,1)S(1)} %get-tuple-element.76), channel_id=1, source_target_pairs={{1,0},{2,1},{3,2},{4,3},{5,4},{6,5},{7,6},{8,7},{9,8},{10,9},{11,1... | collective-permute-start | bytes 92168 | tf_op jit(solution)/shard_map/ppermute | solution.py:27
  185.2 4.8 collective-permute-start.8
  188.4 5.8 %collective-permute-start.9 = (bf16[1,15,1024]{2,1,0:T(8,128)(2,1)S(1)}, bf16[1,15,1024]{2,1,0:T(8,128)(2,1)S(1)}, u32[]{:S(2)}, u32[]{:S(2)}) collective-permute-start(bf16[1,15,1024]{2,1,0:T(8,128)(2,1)S(1)} %get-tuple-element.74), channel_id=1, source_target_pairs={{1,0},{2,1},{3,2},{4,3},{5,4},{6,5},{7,6},{8,7},{9,8},{10,9},{11,1... | collective-permute-start | bytes 92168 | tf_op jit(solution)/shard_map/ppermute | solution.py:27
  194.4 5.7 %copy-start.7 = (bf16[1,256,1024]{2,1,0:T(8,128)(2,1)S(1)}, bf16[1,256,1024]{2,1,0:T(8,128)(2,1)}, u32[]{:S(2)}) copy-start(bf16[1,256,1024]{2,1,0:T(8,128)(2,1)} %param.19) | copy-start | bytes 1572868
  202.5 144.7 %all-gather.22.cloned.1.call-start = ((), (), s32[]{:S(2)}) async-start(), calls=%async_computation.7 | async-start | bytes 9437184 | tf_op jit(solution)/shard_map/all_gather | solution.py:254
  235.8 3.4 copy-start.2
  235.8 3.5 copy-start.6
  241.5 27.2 %collective-permute-start.10 = (bf16[1,2048,256]{2,1,0:T(8,128)(2,1)S(1)}, bf16[1,2048,256]{2,1,0:T(8,128)(2,1)S(1)}, u32[]{:S(2)}, u32[]{:S(2)}) collective-permute-start(bf16[1,2048,256]{2,1,0:T(8,128)(2,1)S(1)} %get-tuple-element.19), channel_id=1, source_target_pairs={{1,0},{2,1},{3,2},{4,3},{5,4},{6,5},{7,6},{8,7},{9,8},{10,9},{11,1... | collective-permute-start | bytes 3145736 | tf_op jit(solution)/shard_map/ppermute | solution.py:16
  242.8 30.5 %collective-permute-start.11 = (bf16[1,2048,256]{2,1,0:T(8,128)(2,1)S(1)}, bf16[1,2048,256]{2,1,0:T(8,128)(2,1)S(1)}, u32[]{:S(2)}, u32[]{:S(2)}) collective-permute-start(bf16[1,2048,256]{2,1,0:T(8,128)(2,1)S(1)} %get-tuple-element.20), channel_id=1, source_target_pairs={{2,0},{3,1},{4,2},{5,3},{6,4},{7,5},{8,6},{9,7},{10,8},{11,9},{12,... | collective-permute-start | bytes 3145736 | tf_op jit(solution)/shard_map/ppermute | solution.py:16
  244.3 29.0 %collective-permute-start.12 = (bf16[1,2048,256]{2,1,0:T(8,128)(2,1)S(1)}, bf16[1,2048,256]{2,1,0:T(8,128)(2,1)S(1)}, u32[]{:S(2)}, u32[]{:S(2)}) collective-permute-start(bf16[1,2048,256]{2,1,0:T(8,128)(2,1)S(1)} %pad_maximum_fusion.5), channel_id=1, source_target_pairs={{0,1},{1,2},{2,3},{3,4},{4,5},{5,6},{6,7},{7,8},{8,9},{9,10},{10,1... | collective-permute-start | bytes 3145736 | tf_op jit(solution)/shard_map/ppermute | solution.py:16
  274.8 110.8 %all-gather.24.cloned.1.call-start = ((), (), s32[]{:S(2)}) async-start(), calls=%async_computation.9 | async-start | bytes 5898240 | tf_op jit(solution)/shard_map/all_gather | solution.py:242
  286.1 6.2 %copy-start.8 = (bf16[1,256,16,64]{1,3,2,0:T(8,128)(2,1)}, bf16[1,256,16,64]{1,3,2,0:T(8,128)(2,1)S(1)}, u32[]{:S(2)}) copy-start(bf16[1,256,16,64]{1,3,2,0:T(8,128)(2,1)S(1)} %fusion.56) | copy-start | bytes 1572868
  287.3 197.5 %all-reduce.4.cloned.1.call-start = ((), (), s32[]{:S(2)}) async-start(), calls=%async_computation.8 | async-start | bytes 4456448 | tf_op jit(solution)/shard_map/psum | solution.py:275
  394.2 2.5 copy-start.9
  394.2 4.9 copy-start.5
  394.2 4.9 copy-start.15
  399.1 3.8 copy-start.4
  399.1 3.8 copy-start.17
  399.1 91.9 %copy-start.1 = (s32[16,1]{0,1:T(1,128)S(1)}, s32[16,1]{0,1:T(1,128)}, u32[]{:S(2)}) copy-start(s32[16,1]{0,1:T(1,128)} %param.18) | copy-start | bytes 196
Sparse Core Ops, SparseCore 0:
  9.7 26.0 all-gather.9
  37.5 41.9 all-gather.13
  82.5 31.4 all-gather.11
  115.6 25.1 all-gather.15
  165.9 36.4 all-gather.17
  204.6 33.1 all-gather.19
  274.9 72.1 all-gather.21
  348.8 36.7 all-gather.23
  394.4 90.3 all-reduce.3
